TPU v7x, 512 devices: a whole 4x8x8 slice. The times are simulated.
512 devices in a mesh: section: 8 (over x, core), tile: 64 (over z, y).
Axes of the slice: x: 4, y: 8, z: 8, core: 2. Of those that a mesh axis runs over, the one named last changes fastest.
Arguments:
- latents: bfloat16 [8, 2, 512, 384], P(None, None, 'tile'), may hold values from -6 to 6
- col_counts: int32 [64], replicated, may hold values from 1 to 8, 480 in all
- conv_weight: bfloat16 [8, 3, 3, 1152, 384], P('section'), may hold values from -0.0625 to 0.0625
- norm_gain: bfloat16 [8, 384], P('section'), may hold values from 0.099609375 to 1.8984375
Outputs:
- decoded: bfloat16 [8, 2, 512, 384], P('section', None, 'tile')
Inputs may be any that keep to these rules, and one draw needn't show every extreme that they name: Strip t holds col_counts[t] image columns; the counts sum to 480 and some strip holds 8.
All inputs are finite; a program needn't handle non-finite values.
Results may differ from a plain program's by a relative error of at most 0.013.
Values may be sent and summed in bfloat16 or wider, within the bound.
No kernel may reach another device: no remote copies, remote signals or barrier semaphores. Data moves between devices by JAX's collectives and lax.ppermute only.
A program may use at most 64 MiB of HBM per device.

v0:
```python
import jax
import jax.numpy as jnp
from jax import lax
from jax.sharding import PartitionSpec as P

SPAN_T = 4


def padded(block, sides, width):
    for axis, dim in sides:
        count = lax.axis_size(axis)
        forward = [(i, i + 1) for i in range(count - 1)]
        backward = [(target, source) for source, target in forward]
        low = lax.ppermute(
            lax.slice_in_dim(block, block.shape[dim] - width, None, axis=dim), axis, forward
        )
        high = lax.ppermute(lax.slice_in_dim(block, 0, width, axis=dim), axis, backward)
        block = jnp.concatenate([low, block, high], axis=dim)
    return block


def passed_along(block, axis, distance):
    devices = range(lax.axis_size(axis))
    route = [(i - distance, i) for i in devices if i - distance in devices]
    return lax.ppermute(block, axis, route)


def from_root(shard, axis, root):
    mine = lax.axis_index(axis) == root
    return lax.psum(jnp.where(mine, shard, jnp.zeros_like(shard)), axis)


def convolve(sequence, kernel, frame_depth, row_count, col_count):
    joined = jnp.concatenate(
        [
            sequence[:, :, 0:col_count],
            sequence[:, :, 1 : col_count + 1],
            sequence[:, :, 2 : col_count + 2],
        ],
        axis=-1,
    )
    summed = jnp.zeros((frame_depth, row_count, col_count, kernel.shape[-1]), jnp.float32)
    for frame_tap in range(3):
        for row_tap in range(3):
            summed = summed + jnp.dot(
                joined[frame_tap : frame_tap + frame_depth, row_tap : row_tap + row_count],
                kernel[frame_tap, row_tap],
                preferred_element_type=jnp.float32,
            )
    return summed


def local(latents, col_counts, conv_weight, norm_gain):
    segments = lax.axis_size("section")
    segment_index = lax.axis_index("section")
    tile_index = lax.axis_index("tile")
    frames_all, row_count, col_count, channels = latents.shape
    live_cols = col_counts[tile_index]
    kernel = conv_weight[0]
    norm_scale = norm_gain[0].astype(jnp.float32)
    frame_depth = SPAN_T
    pieces = frames_all // frame_depth
    total_steps = pieces + segments - 1
    col_live = jnp.arange(col_count)[None, None, :, None] < live_cols
    col_index = jnp.arange(col_count + 2)[None, None, :, None]
    even_segment = segment_index % 2 == 0
    last_segment = segment_index == segments - 1
    zero_value = jnp.zeros((), jnp.bfloat16)

    def advance(step_index, carried):
        inbound, memory, result = carried
        micro_index = step_index - segment_index
        active = (micro_index >= 0) & (micro_index < pieces)
        frame_start = jnp.clip(micro_index, 0, pieces - 1) * frame_depth
        entering = lax.dynamic_slice_in_dim(latents, frame_start, frame_depth, 0)
        residual = jnp.where(
            col_live, jnp.where(segment_index == 0, entering, inbound[0]), zero_value
        )
        branch = inbound[1]
        source = jnp.where(even_segment, residual, branch).astype(jnp.float32)
        normed = (
            source
            * lax.rsqrt(jnp.mean(source * source, axis=-1, keepdims=True) + 1e-06)
            * norm_scale
        )
        activated = jnp.where(col_live, jax.nn.silu(normed), 0.0).astype(jnp.bfloat16)
        first_col = activated[:, :, 0:1]
        last_col = lax.dynamic_slice_in_dim(activated, live_cols - 1, 1, 2)
        haloed = padded(jnp.concatenate([first_col, last_col], axis=2), (("tile", 2),), 1)
        widened = jnp.concatenate([haloed[:, :, 0:1], activated, jnp.zeros_like(first_col)], axis=2)
        widened = jnp.where(col_index == live_cols + 1, haloed[:, :, 3:4], widened)
        extended = jnp.pad(widened, ((0, 0), (1, 1), (0, 0), (0, 0)))
        sequence = jnp.concatenate([memory, extended], axis=0)
        memory = jnp.where(active, sequence[-2:], memory)
        conv_out = jnp.where(
            col_live, convolve(sequence, kernel, frame_depth, row_count, col_count), 0.0
        )
        resid_next = jnp.where(
            even_segment, residual, (residual.astype(jnp.float32) + conv_out).astype(jnp.bfloat16)
        )
        branch_next = jnp.where(even_segment, conv_out.astype(jnp.bfloat16), branch)
        written = lax.dynamic_update_slice_in_dim(result, resid_next, frame_start, 0)
        result = jnp.where(active & last_segment, written, result)
        inbound = passed_along(jnp.stack([resid_next, branch_next]), "section", 1)
        return (inbound, memory, result)

    inbound = jnp.zeros((2, frame_depth, row_count, col_count, channels), jnp.bfloat16)
    memory = jnp.zeros((2, row_count + 2, col_count + 2, channels), jnp.bfloat16)
    result = jnp.zeros((frames_all, row_count, col_count, channels), jnp.bfloat16)
    inbound, memory, result = lax.fori_loop(0, total_steps, advance, (inbound, memory, result))
    gathered = from_root(result, "section", segments - 1)
    frame_share = frames_all // segments
    return lax.dynamic_slice_in_dim(gathered, segment_index * frame_share, frame_share, 0)


def solution(mesh):
    return jax.shard_map(
        local,
        mesh=mesh,
        in_specs=(
            P(None, None, "tile", None),
            P(),
            P("section", None, None, None, None),
            P("section", None),
        ),
        out_specs=P("section", None, "tile", None),
        check_vma=False,
    )
```

profile of v0, /device:TPU:8, one launch (start us, length us, event | category | flops | bytes accessed | tf_op | source)
XLA Modules:
  0.0 376.8 jit_solution(10968144452210081428)
XLA Ops:
  10.5 269.9 %while.20 = (s32[]{:T(128)}, bf16[2,4,2,8,384]{4,3,2,1,0:T(8,128)(2,1)S(1)}, bf16[2,4,10,384]{3,2,1,0:T(8,128)(2,1)S(1)}, bf16[8,2,8,384]{3,2,1,0:T(8,128)(2,1)S...) while((s32[]{:T(128)}, ...), condition=%wide.region_2.3_spmd.clone, body=%wide.region_0.2_spmd.clone.sunk | while | flops 512637024 | bytes 16789532 | solution.py:110
  12.3 3.5 collective-permute-start
  15.8 5.5 %collective-permute-start.1 = (bf16[4,2,1,384]{3,2,1,0:T(2,128)(2,1)S(1)}, bf16[4,2,1,384]{3,2,1,0:T(2,128)(2,1)S(1)}, u32[]{:S(2)}, u32[]{:S(2)}) collective-permute-start(bf16[4,2,1,384]{3,2,1,0:T(2,128)(2,1)S(1)} %get-tuple-element.519), channel_id=1, source_target_pairs={{1,0},{2,1},{3,2},{4,3},{5,4},{6,5},{7,6},{8,7},{9,8},{10,9},{11,1... | collective-permute-start | bytes 18440 | tf_op jit(solution)/shard_map/while/body/eval_jaxpr/ppermute | solution.py:17
  40.1 2.9 collective-permute-start
  43.0 2.9 collective-permute-start.1
  46.0 3.8 collective-permute-done.1
  63.2 3.7 collective-permute-start.2
  69.6 3.6 collective-permute-start
  75.5 3.3 collective-permute-done.1
  92.1 5.0 %collective-permute-start.2 = (bf16[2,4,2,8,384]{4,3,2,1,0:T(8,128)(2,1)S(1)}, bf16[2,4,2,8,384]{4,3,2,1,0:T(8,128)(2,1)S(1)}, u32[]{:S(2)}, u32[]{:S(2)}) collective-permute-start(bf16[2,4,2,8,384]{4,3,2,1,0:T(8,128)(2,1)S(1)} %pad_maximum_fusion.3), channel_id=1, source_target_pairs={{0,64},{64,128},{128,192},{192,256},{256,320},{320,384},{384,448},... | collective-permute-start | bytes 294920 | tf_op jit(solution)/shard_map/while/body/eval_jaxpr/ppermute | solution.py:25
  99.9 3.1 collective-permute-start
  103.0 2.7 collective-permute-start.1
  105.8 2.8 collective-permute-done.1
  121.9 5.0 %collective-permute-start.2 = (bf16[2,4,2,8,384]{4,3,2,1,0:T(8,128)(2,1)S(1)}, bf16[2,4,2,8,384]{4,3,2,1,0:T(8,128)(2,1)S(1)}, u32[]{:S(2)}, u32[]{:S(2)}) collective-permute-start(bf16[2,4,2,8,384]{4,3,2,1,0:T(8,128)(2,1)S(1)} %pad_maximum_fusion.3), channel_id=1, source_target_pairs={{0,64},{64,128},{128,192},{192,256},{256,320},{320,384},{384,448},... | collective-permute-start | bytes 294920 | tf_op jit(solution)/shard_map/while/body/eval_jaxpr/ppermute | solution.py:25
  129.7 3.1 collective-permute-start
  132.8 2.7 collective-permute-start.1
  135.6 2.8 collective-permute-done.1
  151.8 5.0 %collective-permute-start.2 = (bf16[2,4,2,8,384]{4,3,2,1,0:T(8,128)(2,1)S(1)}, bf16[2,4,2,8,384]{4,3,2,1,0:T(8,128)(2,1)S(1)}, u32[]{:S(2)}, u32[]{:S(2)}) collective-permute-start(bf16[2,4,2,8,384]{4,3,2,1,0:T(8,128)(2,1)S(1)} %pad_maximum_fusion.3), channel_id=1, source_target_pairs={{0,64},{64,128},{128,192},{192,256},{256,320},{320,384},{384,448},... | collective-permute-start | bytes 294920 | tf_op jit(solution)/shard_map/while/body/eval_jaxpr/ppermute | solution.py:25
  159.5 3.2 collective-permute-start
  162.7 2.7 collective-permute-start.1
  165.4 2.9 collective-permute-done.1
  181.7 5.3 %collective-permute-start.2 = (bf16[2,4,2,8,384]{4,3,2,1,0:T(8,128)(2,1)S(1)}, bf16[2,4,2,8,384]{4,3,2,1,0:T(8,128)(2,1)S(1)}, u32[]{:S(2)}, u32[]{:S(2)}) collective-permute-start(bf16[2,4,2,8,384]{4,3,2,1,0:T(8,128)(2,1)S(1)} %pad_maximum_fusion.3), channel_id=1, source_target_pairs={{0,64},{64,128},{128,192},{192,256},{256,320},{320,384},{384,448},... | collective-permute-start | bytes 294920 | tf_op jit(solution)/shard_map/while/body/eval_jaxpr/ppermute | solution.py:25
  189.7 3.6 collective-permute-start
  195.7 3.4 collective-permute-done.1
  212.4 5.3 %collective-permute-start.2 = (bf16[2,4,2,8,384]{4,3,2,1,0:T(8,128)(2,1)S(1)}, bf16[2,4,2,8,384]{4,3,2,1,0:T(8,128)(2,1)S(1)}, u32[]{:S(2)}, u32[]{:S(2)}) collective-permute-start(bf16[2,4,2,8,384]{4,3,2,1,0:T(8,128)(2,1)S(1)} %pad_maximum_fusion.3), channel_id=1, source_target_pairs={{0,64},{64,128},{128,192},{192,256},{256,320},{320,384},{384,448},... | collective-permute-start | bytes 294920 | tf_op jit(solution)/shard_map/while/body/eval_jaxpr/ppermute | solution.py:25
  220.4 3.6 collective-permute-start
  226.4 3.7 collective-permute-done.1
  243.5 5.3 %collective-permute-start.2 = (bf16[2,4,2,8,384]{4,3,2,1,0:T(8,128)(2,1)S(1)}, bf16[2,4,2,8,384]{4,3,2,1,0:T(8,128)(2,1)S(1)}, u32[]{:S(2)}, u32[]{:S(2)}) collective-permute-start(bf16[2,4,2,8,384]{4,3,2,1,0:T(8,128)(2,1)S(1)} %pad_maximum_fusion.3), channel_id=1, source_target_pairs={{0,64},{64,128},{128,192},{192,256},{256,320},{320,384},{384,448},... | collective-permute-start | bytes 294920 | tf_op jit(solution)/shard_map/while/body/eval_jaxpr/ppermute | solution.py:25
  251.5 3.6 collective-permute-start
  257.4 3.4 collective-permute-done.1
  274.2 5.3 %collective-permute-start.2 = (bf16[2,4,2,8,384]{4,3,2,1,0:T(8,128)(2,1)S(1)}, bf16[2,4,2,8,384]{4,3,2,1,0:T(8,128)(2,1)S(1)}, u32[]{:S(2)}, u32[]{:S(2)}) collective-permute-start(bf16[2,4,2,8,384]{4,3,2,1,0:T(8,128)(2,1)S(1)} %pad_maximum_fusion.3), channel_id=1, source_target_pairs={{0,64},{64,128},{128,192},{192,256},{256,320},{320,384},{384,448},... | collective-permute-start | bytes 294920 | tf_op jit(solution)/shard_map/while/body/eval_jaxpr/ppermute | solution.py:25
  281.1 87.6 %all-reduce.3.cloned.1.call-done = bf16[8,2,8,384]{3,2,1,0:T(8,128)(2,1)} async-done(((bf16[8,2,8,384]{3,2,1,0:T(8,128)(2,1)}), bf16[8,2,8,384]{3,2,1,0:T(8,128)(2,1)}) %all-reduce.3.cloned.1.call-update) | async-done | bytes 98320 | tf_op jit(solution)/shard_map/psum | solution.py:30
  (240 shorter events, 159.3 us)
Async XLA Ops:
  6.5 362.1 %all-reduce.3.cloned.1.call-start = ((), (), s32[]{:S(2)}) async-start(), calls=%async_computation | async-start | bytes 196608 | tf_op jit(solution)/shard_map/psum | solution.py:30
  12.3 10.4 %collective-permute-start = (bf16[4,2,1,384]{3,2,1,0:T(2,128)(2,1)S(1)}, bf16[4,2,1,384]{3,2,1,0:T(2,128)(2,1)S(1)}, u32[]{:S(2)}, u32[]{:S(2)}) collective-permute-start(bf16[4,2,1,384]{3,2,1,0:T(2,128)(2,1)S(1)} %get-tuple-element.518), channel_id=1, source_target_pairs={{0,1},{1,2},{2,3},{3,4},{4,5},{5,6},{6,7},{7,8},{8,9},{9,10},{10,1... | collective-permute-start | bytes 18440 | tf_op jit(solution)/shard_map/while/body/eval_jaxpr/ppermute | solution.py:14
  15.8 6.9 %collective-permute-start.1 = (bf16[4,2,1,384]{3,2,1,0:T(2,128)(2,1)S(1)}, bf16[4,2,1,384]{3,2,1,0:T(2,128)(2,1)S(1)}, u32[]{:S(2)}, u32[]{:S(2)}) collective-permute-start(bf16[4,2,1,384]{3,2,1,0:T(2,128)(2,1)S(1)} %get-tuple-element.519), channel_id=1, source_target_pairs={{1,0},{2,1},{3,2},{4,3},{5,4},{6,5},{7,6},{8,7},{9,8},{10,9},{11,1... | collective-permute-start | bytes 18440 | tf_op jit(solution)/shard_map/while/body/eval_jaxpr/ppermute | solution.py:17
  36.1 2.2 collective-permute-start.2
  40.1 9.7 %collective-permute-start = (bf16[4,2,1,384]{3,2,1,0:T(2,128)(2,1)S(1)}, bf16[4,2,1,384]{3,2,1,0:T(2,128)(2,1)S(1)}, u32[]{:S(2)}, u32[]{:S(2)}) collective-permute-start(bf16[4,2,1,384]{3,2,1,0:T(2,128)(2,1)S(1)} %get-tuple-element.518), channel_id=1, source_target_pairs={{0,1},{1,2},{2,3},{3,4},{4,5},{5,6},{6,7},{7,8},{8,9},{9,10},{10,1... | collective-permute-start | bytes 18440 | tf_op jit(solution)/shard_map/while/body/eval_jaxpr/ppermute | solution.py:14
  43.0 6.8 %collective-permute-start.1 = (bf16[4,2,1,384]{3,2,1,0:T(2,128)(2,1)S(1)}, bf16[4,2,1,384]{3,2,1,0:T(2,128)(2,1)S(1)}, u32[]{:S(2)}, u32[]{:S(2)}) collective-permute-start(bf16[4,2,1,384]{3,2,1,0:T(2,128)(2,1)S(1)} %get-tuple-element.519), channel_id=1, source_target_pairs={{1,0},{2,1},{3,2},{4,3},{5,4},{6,5},{7,6},{8,7},{9,8},{10,9},{11,1... | collective-permute-start | bytes 18440 | tf_op jit(solution)/shard_map/while/body/eval_jaxpr/ppermute | solution.py:17
  63.2 4.6 %collective-permute-start.2 = (bf16[2,4,2,8,384]{4,3,2,1,0:T(8,128)(2,1)S(1)}, bf16[2,4,2,8,384]{4,3,2,1,0:T(8,128)(2,1)S(1)}, u32[]{:S(2)}, u32[]{:S(2)}) collective-permute-start(bf16[2,4,2,8,384]{4,3,2,1,0:T(8,128)(2,1)S(1)} %pad_maximum_fusion.3), channel_id=1, source_target_pairs={{0,64},{64,128},{128,192},{192,256},{256,320},{320,384},{384,448},... | collective-permute-start | bytes 294920 | tf_op jit(solution)/shard_map/while/body/eval_jaxpr/ppermute | solution.py:25
  69.6 9.3 %collective-permute-start = (bf16[4,2,1,384]{3,2,1,0:T(2,128)(2,1)S(1)}, bf16[4,2,1,384]{3,2,1,0:T(2,128)(2,1)S(1)}, u32[]{:S(2)}, u32[]{:S(2)}) collective-permute-start(bf16[4,2,1,384]{3,2,1,0:T(2,128)(2,1)S(1)} %get-tuple-element.518), channel_id=1, source_target_pairs={{0,1},{1,2},{2,3},{3,4},{4,5},{5,6},{6,7},{7,8},{8,9},{9,10},{10,1... | collective-permute-start | bytes 18440 | tf_op jit(solution)/shard_map/while/body/eval_jaxpr/ppermute | solution.py:14
  73.2 5.6 %collective-permute-start.1 = (bf16[4,2,1,384]{3,2,1,0:T(2,128)(2,1)S(1)}, bf16[4,2,1,384]{3,2,1,0:T(2,128)(2,1)S(1)}, u32[]{:S(2)}, u32[]{:S(2)}) collective-permute-start(bf16[4,2,1,384]{3,2,1,0:T(2,128)(2,1)S(1)} %get-tuple-element.519), channel_id=1, source_target_pairs={{1,0},{2,1},{3,2},{4,3},{5,4},{6,5},{7,6},{8,7},{9,8},{10,9},{11,1... | collective-permute-start | bytes 18440 | tf_op jit(solution)/shard_map/while/body/eval_jaxpr/ppermute | solution.py:17
  92.1 5.9 %collective-permute-start.2 = (bf16[2,4,2,8,384]{4,3,2,1,0:T(8,128)(2,1)S(1)}, bf16[2,4,2,8,384]{4,3,2,1,0:T(8,128)(2,1)S(1)}, u32[]{:S(2)}, u32[]{:S(2)}) collective-permute-start(bf16[2,4,2,8,384]{4,3,2,1,0:T(8,128)(2,1)S(1)} %pad_maximum_fusion.3), channel_id=1, source_target_pairs={{0,64},{64,128},{128,192},{192,256},{256,320},{320,384},{384,448},... | collective-permute-start | bytes 294920 | tf_op jit(solution)/shard_map/while/body/eval_jaxpr/ppermute | solution.py:25
  99.9 8.7 %collective-permute-start = (bf16[4,2,1,384]{3,2,1,0:T(2,128)(2,1)S(1)}, bf16[4,2,1,384]{3,2,1,0:T(2,128)(2,1)S(1)}, u32[]{:S(2)}, u32[]{:S(2)}) collective-permute-start(bf16[4,2,1,384]{3,2,1,0:T(2,128)(2,1)S(1)} %get-tuple-element.518), channel_id=1, source_target_pairs={{0,1},{1,2},{2,3},{3,4},{4,5},{5,6},{6,7},{7,8},{8,9},{9,10},{10,1... | collective-permute-start | bytes 18440 | tf_op jit(solution)/shard_map/while/body/eval_jaxpr/ppermute | solution.py:14
  103.0 5.6 %collective-permute-start.1 = (bf16[4,2,1,384]{3,2,1,0:T(2,128)(2,1)S(1)}, bf16[4,2,1,384]{3,2,1,0:T(2,128)(2,1)S(1)}, u32[]{:S(2)}, u32[]{:S(2)}) collective-permute-start(bf16[4,2,1,384]{3,2,1,0:T(2,128)(2,1)S(1)} %get-tuple-element.519), channel_id=1, source_target_pairs={{1,0},{2,1},{3,2},{4,3},{5,4},{6,5},{7,6},{8,7},{9,8},{10,9},{11,1... | collective-permute-start | bytes 18440 | tf_op jit(solution)/shard_map/while/body/eval_jaxpr/ppermute | solution.py:17
  121.9 5.9 %collective-permute-start.2 = (bf16[2,4,2,8,384]{4,3,2,1,0:T(8,128)(2,1)S(1)}, bf16[2,4,2,8,384]{4,3,2,1,0:T(8,128)(2,1)S(1)}, u32[]{:S(2)}, u32[]{:S(2)}) collective-permute-start(bf16[2,4,2,8,384]{4,3,2,1,0:T(8,128)(2,1)S(1)} %pad_maximum_fusion.3), channel_id=1, source_target_pairs={{0,64},{64,128},{128,192},{192,256},{256,320},{320,384},{384,448},... | collective-permute-start | bytes 294920 | tf_op jit(solution)/shard_map/while/body/eval_jaxpr/ppermute | solution.py:25
  129.7 8.7 %collective-permute-start = (bf16[4,2,1,384]{3,2,1,0:T(2,128)(2,1)S(1)}, bf16[4,2,1,384]{3,2,1,0:T(2,128)(2,1)S(1)}, u32[]{:S(2)}, u32[]{:S(2)}) collective-permute-start(bf16[4,2,1,384]{3,2,1,0:T(2,128)(2,1)S(1)} %get-tuple-element.518), channel_id=1, source_target_pairs={{0,1},{1,2},{2,3},{3,4},{4,5},{5,6},{6,7},{7,8},{8,9},{9,10},{10,1... | collective-permute-start | bytes 18440 | tf_op jit(solution)/shard_map/while/body/eval_jaxpr/ppermute | solution.py:14
  132.8 5.6 %collective-permute-start.1 = (bf16[4,2,1,384]{3,2,1,0:T(2,128)(2,1)S(1)}, bf16[4,2,1,384]{3,2,1,0:T(2,128)(2,1)S(1)}, u32[]{:S(2)}, u32[]{:S(2)}) collective-permute-start(bf16[4,2,1,384]{3,2,1,0:T(2,128)(2,1)S(1)} %get-tuple-element.519), channel_id=1, source_target_pairs={{1,0},{2,1},{3,2},{4,3},{5,4},{6,5},{7,6},{8,7},{9,8},{10,9},{11,1... | collective-permute-start | bytes 18440 | tf_op jit(solution)/shard_map/while/body/eval_jaxpr/ppermute | solution.py:17
  151.8 5.9 %collective-permute-start.2 = (bf16[2,4,2,8,384]{4,3,2,1,0:T(8,128)(2,1)S(1)}, bf16[2,4,2,8,384]{4,3,2,1,0:T(8,128)(2,1)S(1)}, u32[]{:S(2)}, u32[]{:S(2)}) collective-permute-start(bf16[2,4,2,8,384]{4,3,2,1,0:T(8,128)(2,1)S(1)} %pad_maximum_fusion.3), channel_id=1, source_target_pairs={{0,64},{64,128},{128,192},{192,256},{256,320},{320,384},{384,448},... | collective-permute-start | bytes 294920 | tf_op jit(solution)/shard_map/while/body/eval_jaxpr/ppermute | solution.py:25
  159.5 8.9 %collective-permute-start = (bf16[4,2,1,384]{3,2,1,0:T(2,128)(2,1)S(1)}, bf16[4,2,1,384]{3,2,1,0:T(2,128)(2,1)S(1)}, u32[]{:S(2)}, u32[]{:S(2)}) collective-permute-start(bf16[4,2,1,384]{3,2,1,0:T(2,128)(2,1)S(1)} %get-tuple-element.518), channel_id=1, source_target_pairs={{0,1},{1,2},{2,3},{3,4},{4,5},{5,6},{6,7},{7,8},{8,9},{9,10},{10,1... | collective-permute-start | bytes 18440 | tf_op jit(solution)/shard_map/while/body/eval_jaxpr/ppermute | solution.py:14
  162.7 5.7 %collective-permute-start.1 = (bf16[4,2,1,384]{3,2,1,0:T(2,128)(2,1)S(1)}, bf16[4,2,1,384]{3,2,1,0:T(2,128)(2,1)S(1)}, u32[]{:S(2)}, u32[]{:S(2)}) collective-permute-start(bf16[4,2,1,384]{3,2,1,0:T(2,128)(2,1)S(1)} %get-tuple-element.519), channel_id=1, source_target_pairs={{1,0},{2,1},{3,2},{4,3},{5,4},{6,5},{7,6},{8,7},{9,8},{10,9},{11,1... | collective-permute-start | bytes 18440 | tf_op jit(solution)/shard_map/while/body/eval_jaxpr/ppermute | solution.py:17
  181.7 6.2 %collective-permute-start.2 = (bf16[2,4,2,8,384]{4,3,2,1,0:T(8,128)(2,1)S(1)}, bf16[2,4,2,8,384]{4,3,2,1,0:T(8,128)(2,1)S(1)}, u32[]{:S(2)}, u32[]{:S(2)}) collective-permute-start(bf16[2,4,2,8,384]{4,3,2,1,0:T(8,128)(2,1)S(1)} %pad_maximum_fusion.3), channel_id=1, source_target_pairs={{0,64},{64,128},{128,192},{192,256},{256,320},{320,384},{384,448},... | collective-permute-start | bytes 294920 | tf_op jit(solution)/shard_map/while/body/eval_jaxpr/ppermute | solution.py:25
  189.7 9.4 %collective-permute-start = (bf16[4,2,1,384]{3,2,1,0:T(2,128)(2,1)S(1)}, bf16[4,2,1,384]{3,2,1,0:T(2,128)(2,1)S(1)}, u32[]{:S(2)}, u32[]{:S(2)}) collective-permute-start(bf16[4,2,1,384]{3,2,1,0:T(2,128)(2,1)S(1)} %get-tuple-element.518), channel_id=1, source_target_pairs={{0,1},{1,2},{2,3},{3,4},{4,5},{5,6},{6,7},{7,8},{8,9},{9,10},{10,1... | collective-permute-start | bytes 18440 | tf_op jit(solution)/shard_map/while/body/eval_jaxpr/ppermute | solution.py:14
  193.4 5.7 %collective-permute-start.1 = (bf16[4,2,1,384]{3,2,1,0:T(2,128)(2,1)S(1)}, bf16[4,2,1,384]{3,2,1,0:T(2,128)(2,1)S(1)}, u32[]{:S(2)}, u32[]{:S(2)}) collective-permute-start(bf16[4,2,1,384]{3,2,1,0:T(2,128)(2,1)S(1)} %get-tuple-element.519), channel_id=1, source_target_pairs={{1,0},{2,1},{3,2},{4,3},{5,4},{6,5},{7,6},{8,7},{9,8},{10,9},{11,1... | collective-permute-start | bytes 18440 | tf_op jit(solution)/shard_map/while/body/eval_jaxpr/ppermute | solution.py:17
  212.4 6.2 %collective-permute-start.2 = (bf16[2,4,2,8,384]{4,3,2,1,0:T(8,128)(2,1)S(1)}, bf16[2,4,2,8,384]{4,3,2,1,0:T(8,128)(2,1)S(1)}, u32[]{:S(2)}, u32[]{:S(2)}) collective-permute-start(bf16[2,4,2,8,384]{4,3,2,1,0:T(8,128)(2,1)S(1)} %pad_maximum_fusion.3), channel_id=1, source_target_pairs={{0,64},{64,128},{128,192},{192,256},{256,320},{320,384},{384,448},... | collective-permute-start | bytes 294920 | tf_op jit(solution)/shard_map/while/body/eval_jaxpr/ppermute | solution.py:25
  220.4 9.7 %collective-permute-start = (bf16[4,2,1,384]{3,2,1,0:T(2,128)(2,1)S(1)}, bf16[4,2,1,384]{3,2,1,0:T(2,128)(2,1)S(1)}, u32[]{:S(2)}, u32[]{:S(2)}) collective-permute-start(bf16[4,2,1,384]{3,2,1,0:T(2,128)(2,1)S(1)} %get-tuple-element.518), channel_id=1, source_target_pairs={{0,1},{1,2},{2,3},{3,4},{4,5},{5,6},{6,7},{7,8},{8,9},{9,10},{10,1... | collective-permute-start | bytes 18440 | tf_op jit(solution)/shard_map/while/body/eval_jaxpr/ppermute | solution.py:14
  224.1 6.0 %collective-permute-start.1 = (bf16[4,2,1,384]{3,2,1,0:T(2,128)(2,1)S(1)}, bf16[4,2,1,384]{3,2,1,0:T(2,128)(2,1)S(1)}, u32[]{:S(2)}, u32[]{:S(2)}) collective-permute-start(bf16[4,2,1,384]{3,2,1,0:T(2,128)(2,1)S(1)} %get-tuple-element.519), channel_id=1, source_target_pairs={{1,0},{2,1},{3,2},{4,3},{5,4},{6,5},{7,6},{8,7},{9,8},{10,9},{11,1... | collective-permute-start | bytes 18440 | tf_op jit(solution)/shard_map/while/body/eval_jaxpr/ppermute | solution.py:17
  243.5 6.2 %collective-permute-start.2 = (bf16[2,4,2,8,384]{4,3,2,1,0:T(8,128)(2,1)S(1)}, bf16[2,4,2,8,384]{4,3,2,1,0:T(8,128)(2,1)S(1)}, u32[]{:S(2)}, u32[]{:S(2)}) collective-permute-start(bf16[2,4,2,8,384]{4,3,2,1,0:T(8,128)(2,1)S(1)} %pad_maximum_fusion.3), channel_id=1, source_target_pairs={{0,64},{64,128},{128,192},{192,256},{256,320},{320,384},{384,448},... | collective-permute-start | bytes 294920 | tf_op jit(solution)/shard_map/while/body/eval_jaxpr/ppermute | solution.py:25
  251.5 9.4 %collective-permute-start = (bf16[4,2,1,384]{3,2,1,0:T(2,128)(2,1)S(1)}, bf16[4,2,1,384]{3,2,1,0:T(2,128)(2,1)S(1)}, u32[]{:S(2)}, u32[]{:S(2)}) collective-permute-start(bf16[4,2,1,384]{3,2,1,0:T(2,128)(2,1)S(1)} %get-tuple-element.518), channel_id=1, source_target_pairs={{0,1},{1,2},{2,3},{3,4},{4,5},{5,6},{6,7},{7,8},{8,9},{9,10},{10,1... | collective-permute-start | bytes 18440 | tf_op jit(solution)/shard_map/while/body/eval_jaxpr/ppermute | solution.py:14
  255.1 5.7 %collective-permute-start.1 = (bf16[4,2,1,384]{3,2,1,0:T(2,128)(2,1)S(1)}, bf16[4,2,1,384]{3,2,1,0:T(2,128)(2,1)S(1)}, u32[]{:S(2)}, u32[]{:S(2)}) collective-permute-start(bf16[4,2,1,384]{3,2,1,0:T(2,128)(2,1)S(1)} %get-tuple-element.519), channel_id=1, source_target_pairs={{1,0},{2,1},{3,2},{4,3},{5,4},{6,5},{7,6},{8,7},{9,8},{10,9},{11,1... | collective-permute-start | bytes 18440 | tf_op jit(solution)/shard_map/while/body/eval_jaxpr/ppermute | solution.py:17
  274.2 6.2 %collective-permute-start.2 = (bf16[2,4,2,8,384]{4,3,2,1,0:T(8,128)(2,1)S(1)}, bf16[2,4,2,8,384]{4,3,2,1,0:T(8,128)(2,1)S(1)}, u32[]{:S(2)}, u32[]{:S(2)}) collective-permute-start(bf16[2,4,2,8,384]{4,3,2,1,0:T(8,128)(2,1)S(1)} %pad_maximum_fusion.3), channel_id=1, source_target_pairs={{0,64},{64,128},{128,192},{192,256},{256,320},{320,384},{384,448},... | collective-permute-start | bytes 294920 | tf_op jit(solution)/shard_map/while/body/eval_jaxpr/ppermute | solution.py:25
Sparse Core Ops, SparseCore 0:
  281.2 87.4 all-reduce.2
where the time goes:
time: 382 us; the launch traced here: 377 us
  waiting for transfers between devices  123 us (32%)
  matrix products  116 us (30%)
  starting transfers between devices  96.9 us (25%)
  other arithmetic  20.4 us (5%)
  between operations  15.3 us (4%)
    dot_general x81, matrix products, convolve(): jnp.dot(joined[frame_tap:frame_tap + frame_depth, row_tap:row_tap + row_c...  116 us
    psum x1, waiting for transfers between devices, from_root(): return lax.psum(jnp.where(mine, shard, jnp.zeros_like(shard)), axis)  87.6 us
    ppermute x9, starting transfers between devices, passed_along(): return lax.ppermute(block, axis, route)  41.1 us
    ppermute x9, starting transfers between devices, padded(): lax.ppermute(lax.slice_in_dim(block, block.shape[dim] - width, None, axis...  30.4 us
    ppermute x9, waiting for transfers between devices, padded(): lax.ppermute(lax.slice_in_dim(block, 0, width, axis=dim), axis, backward)  27.2 us
    ppermute x9, starting transfers between devices, padded(): lax.ppermute(lax.slice_in_dim(block, 0, width, axis=dim), axis, backward)  25.3 us
    reduce_sum x9, other arithmetic, advance(): jnp.mean(source * source, axis=-1, keepdims=True) + 1e-06  8.76 us
    ppermute x9, waiting for transfers between devices, passed_along(): return lax.ppermute(block, axis, route)  8.26 us
  transfers between devices with their start and end apart: 28, of which 19 were waited for; matrix products, arithmetic and copies ran while one was open for 0% of the time, Pallas kernels for 0%

commit v1 on v0

v1 whole, which is shorter than its diff:
```python
import jax
import jax.numpy as jnp
from jax import lax
from jax.sharding import PartitionSpec as P


def hop(block, pairs, axes):
    return lax.ppermute(block, axes, pairs)


def activate(values, gain):
    widened = values.astype(jnp.float32)
    scaled = widened * lax.rsqrt(jnp.mean(widened * widened, axis=-1, keepdims=True) + 1e-06) * gain
    return jax.nn.silu(scaled).astype(jnp.bfloat16)


def convolve(activated, kernel):
    frames, rows, cols_ext, channels = activated.shape
    cols = cols_ext - 2
    padded = jnp.pad(activated, ((2, 0), (1, 1), (0, 0), (0, 0)))
    taps = []
    for frame_tap in range(3):
        for row_tap in range(3):
            for col_tap in range(3):
                taps.append(
                    padded[frame_tap : frame_tap + frames, row_tap : row_tap + rows, col_tap : col_tap + cols]
                )
    joined = jnp.concatenate(taps, axis=-1).reshape(frames * rows * cols, 27 * channels)
    flat = kernel.reshape(27 * channels, kernel.shape[-1])
    out = jnp.dot(joined, flat, preferred_element_type=jnp.float32)
    return out.reshape(frames, rows, cols, kernel.shape[-1])


def local(latents, col_counts, conv_weight, norm_gain):
    segments = lax.axis_size("section")
    tiles = lax.axis_size("tile")
    segment_index = lax.axis_index("section")
    tile_index = lax.axis_index("tile")
    frames_all, row_count, col_count, channels = latents.shape
    live_cols = col_counts[tile_index]
    kernel = conv_weight[0]
    gain = norm_gain[0].astype(jnp.float32)
    col_live = jnp.arange(col_count)[None, None, :, None] < live_cols
    ext_index = jnp.arange(col_count + 2)[None, None, :, None]
    zero = jnp.zeros((), jnp.bfloat16)
    both = ("section", "tile")

    def edges(block):
        first = block[:, :, 0:1]
        last = lax.dynamic_slice_in_dim(block, live_cols - 1, 1, 2)
        return first, last

    def extend(block, left, right):
        wide = jnp.concatenate([left, block, jnp.zeros_like(left)], axis=2)
        return jnp.where(ext_index == live_cols + 1, right, wide)

    def diagonal(first, last, stage):
        src, dst = stage * tiles, (stage + 1) * tiles
        left = hop(last, [(src + t - 1, dst + t) for t in range(1, tiles)], both)
        right = hop(first, [(src + t + 1, dst + t) for t in range(tiles - 1)], both)
        return left, right

    stream = jnp.where(col_live, latents, zero)
    first, last = edges(stream)
    left = hop(last, [(t - 1, t) for t in range(1, tiles)], "tile")
    right = hop(first, [(t + 1, t) for t in range(tiles - 1)], "tile")
    current = stream
    residual = stream
    for stage in range(segments):
        activated = activate(extend(current, left, right), gain)
        conv_out = convolve(activated, kernel)
        if stage % 2 == 0:
            produced = jnp.where(col_live, conv_out, 0.0).astype(jnp.bfloat16)
        else:
            produced = jnp.where(
                col_live, (residual.astype(jnp.float32) + conv_out).astype(jnp.bfloat16), zero
            )
        if stage == segments - 1:
            break
        first, last = edges(produced)
        left, right = diagonal(first, last, stage)
        nxt = hop(produced, [(stage, stage + 1)], "section")
        if stage % 2 == 1 and stage + 2 < segments:
            residual = hop(produced, [(stage, stage + 2)], "section")
        current = nxt
    final = produced
    result = final[segments - 1 : segments]
    for target in range(segments - 1):
        piece = hop(final[target : target + 1], [(segments - 1, target)], "section")
        result = jnp.where(segment_index == target, piece, result)
    return result


def solution(mesh):
    return jax.shard_map(
        local,
        mesh=mesh,
        in_specs=(
            P(None, None, "tile", None),
            P(),
            P("section", None, None, None, None),
            P("section", None),
        ),
        out_specs=P("section", None, "tile", None),
        check_vma=False,
    )
```

time: 382 us -> 112 us (0.29)
  the two profiles are of different devices: /device:TPU:8 before, /device:TPU:256 now
where the time goes in v1:
time: 112 us; the launch traced here: 111 us
  waiting for transfers between devices  47.8 us (43%)
  starting transfers between devices  29.9 us (27%)
  matrix products  12.2 us (11%)
  local copies, waits for them, and re-layouts  10.6 us (9%)
  other arithmetic  6.84 us (6%)
  between operations  3.64 us (3%)
    ppermute x33, waiting for transfers between devices, hop(): return lax.ppermute(block, axes, pairs)  47.8 us
    ppermute x33, starting transfers between devices, hop(): return lax.ppermute(block, axes, pairs)  29.9 us
    dot_general x8, matrix products, convolve(): out = jnp.dot(joined, flat, preferred_element_type=jnp.float32)  12.2 us
    unnamed x212, local copies, waits for them, and re-layouts  8.52 us
  transfers between devices with their start and end apart: 33, of which 4 were waited for; matrix products, arithmetic and copies ran while one was open for 5% of the time, Pallas kernels for 0%

profile of v1, /device:TPU:256, one launch (start us, length us, event | category | flops | bytes accessed | tf_op | source)
XLA Modules:
  0.0 111.0 jit_solution(4407479309796803565)
XLA Ops:
  0.0 1.2 %dynamic_slice.27 = s32[1]{0:T(128)} dynamic-slice(s32[64]{0:T(128)} %param.5, s32[]{:T(128)S(6)} %select_n.112), dynamic_slice_sizes={1} | dynamic-slice | bytes 12 | tf_op jit(solution)/shard_map/dynamic_slice | solution.py:40
  3.2 1.0 broadcast_select_fusion
  4.2 4.5 %collective-permute-start = (bf16[8,2,1,384]{3,2,1,0:T(2,128)(2,1)S(1)}, bf16[8,2,1,384]{3,2,1,0:T(2,128)(2,1)S(1)}, u32[]{:S(2)}, u32[]{:S(2)}) collective-permute-start(bf16[8,2,1,384]{3,2,1,0:T(2,128)(2,1)S(1)} %get-tuple-element.26), channel_id=1, source_target_pairs={{1,0},{2,1},{3,2},{4,3},{5,4},{6,5},{7,6},{8,7},{9,8},{10,9},{11,1... | collective-permute-start | bytes 36872 | tf_op jit(solution)/shard_map/ppermute | solution.py:8
  8.7 1.9 %collective-permute-start.1 = (bf16[8,2,1,384]{3,2,1,0:T(2,128)(2,1)S(1)}, bf16[8,2,1,384]{3,2,1,0:T(2,128)(2,1)S(1)}, u32[]{:S(2)}, u32[]{:S(2)}) collective-permute-start(bf16[8,2,1,384]{3,2,1,0:T(2,128)(2,1)S(1)} %get-tuple-element.27), channel_id=1, source_target_pairs={{0,1},{1,2},{2,3},{3,4},{4,5},{5,6},{6,7},{7,8},{8,9},{9,10},{10,1... | collective-permute-start | bytes 36872 | tf_op jit(solution)/shard_map/ppermute | solution.py:8
  11.3 0.7 convert_reduce_fusion
  12.1 5.6 %collective-permute-done.1 = bf16[8,2,1,384]{3,2,1,0:T(2,128)(2,1)S(1)} collective-permute-done((bf16[8,2,1,384]{3,2,1,0:T(2,128)(2,1)S(1)}, bf16[8,2,1,384]{3,2,1,0:T(2,128)(2,1)S(1)}, u32[]{:S(2)}, u32[]{:S(2)}) %collective-permute-start.1) | collective-permute-done | bytes 12320 | tf_op jit(solution)/shard_map/ppermute | solution.py:8
  19.2 2.1 %copy-done = bf16[1,3,3,1152,384]{4,3,2,1,0:T(8,128)(2,1)S(1)} copy-done((bf16[1,3,3,1152,384]{4,3,2,1,0:T(8,128)(2,1)S(1)}, bf16[1,3,3,1152,384]{4,3,2,1,0:T(8,128)(2,1)}, u32[]{:S(2)}) %copy-start) | copy-done | bytes 7962648
  21.3 1.5 %fusion = bf16[8,2,8,384]{3,2,1,0:T(8,128)(2,1)S(1)} fusion(bf16[8,2,8,10368]{3,2,1,0:T(8,128)(2,1)S(1)} %constant_dynamic-update-slice_fusion, bf16[10368,384,1,1]{1,0,3,2:T(8,128)(2,1)S(1)} %bitcast.47, pred[8]{0:T(512)(128)(4,1)S(1)} %iota_compare_fusion.1), kind=kOutput, calls=%fused_computation.197 | convolution fusion | flops 1019314176 | bytes 10715144 | tf_op jit(solution)/shard_map/dot_general | solution.py:30
  22.8 1.3 %collective-permute-start.4 = (bf16[8,2,8,384]{3,2,1,0:T(8,128)(2,1)S(1)}, bf16[8,2,8,384]{3,2,1,0:T(8,128)(2,1)S(1)}, u32[]{:S(2)}, u32[]{:S(2)}) collective-permute-start(bf16[8,2,8,384]{3,2,1,0:T(8,128)(2,1)S(1)} %fusion), channel_id=1, source_target_pairs={{0,64},{1,65},{2,66},{3,67},{4,68},{5,69},{6,70},{7,71},{8,72},{9,... | collective-permute-start | bytes 294920 | tf_op jit(solution)/shard_map/ppermute | solution.py:8
  24.1 1.3 %collective-permute-start.2 = (bf16[8,2,1,384]{3,2,1,0:T(2,128)(2,1)S(1)}, bf16[8,2,1,384]{3,2,1,0:T(2,128)(2,1)S(1)}, u32[]{:S(2)}, u32[]{:S(2)}) collective-permute-start(bf16[8,2,1,384]{3,2,1,0:T(2,128)(2,1)S(1)} %get-tuple-element.24), channel_id=1, source_target_pairs={{1,64},{2,65},{3,66},{4,67},{5,68},{6,69},{7,70},{8,71},{9,72},{10... | collective-permute-start | bytes 36872 | tf_op jit(solution)/shard_map/ppermute | solution.py:8
  25.4 1.3 %collective-permute-start.3 = (bf16[8,2,1,384]{3,2,1,0:T(2,128)(2,1)S(1)}, bf16[8,2,1,384]{3,2,1,0:T(2,128)(2,1)S(1)}, u32[]{:S(2)}, u32[]{:S(2)}) collective-permute-start(bf16[8,2,1,384]{3,2,1,0:T(2,128)(2,1)S(1)} %get-tuple-element.25), channel_id=1, source_target_pairs={{0,65},{1,66},{2,67},{3,68},{4,69},{5,70},{6,71},{7,72},{8,73},{9,... | collective-permute-start | bytes 36872 | tf_op jit(solution)/shard_map/ppermute | solution.py:8
  27.0 1.3 %collective-permute-done.3 = bf16[8,2,1,384]{3,2,1,0:T(2,128)(2,1)S(1)} collective-permute-done((bf16[8,2,1,384]{3,2,1,0:T(2,128)(2,1)S(1)}, bf16[8,2,1,384]{3,2,1,0:T(2,128)(2,1)S(1)}, u32[]{:S(2)}, u32[]{:S(2)}) %collective-permute-start.3) | collective-permute-done | bytes 12320 | tf_op jit(solution)/shard_map/ppermute | solution.py:8
  29.9 1.5 %fusion.5 = bf16[8,2,8,384]{3,2,1,0:T(8,128)(2,1)S(1)} fusion(bf16[8,2,8,10368]{3,2,1,0:T(8,128)(2,1)S(1)} %constant_dynamic-update-slice_fusion.27, bf16[10368,384,1,1]{1,0,3,2:T(8,128)(2,1)S(1)} %bitcast.48, pred[8]{0:T(512)(128)(4,1)S(1)} %iota_compare_fusion.1, bf16[8,2,8,384]{3,2,1,0:T(8,128)(2,1)S(1)} %copy-done.1), kind=kOutput, calls=%fused_computation.202 | convolution fusion | flops 1019461632 | bytes 10813448 | tf_op jit(solution)/shard_map/dot_general | solution.py:30
  31.4 0.7 collective-permute-start.8
  32.8 0.7 collective-permute-start.7
  35.0 1.5 %fusion.2 = bf16[8,2,8,384]{3,2,1,0:T(8,128)(2,1)S(1)} fusion(bf16[8,2,8,10368]{3,2,1,0:T(8,128)(2,1)S(1)} %constant_dynamic-update-slice_fusion.54, bf16[10368,384,1,1]{1,0,3,2:T(8,128)(2,1)S(1)} %bitcast.49, pred[8]{0:T(512)(128)(4,1)S(1)} %iota_compare_fusion.1), kind=kOutput, calls=%fused_computation.199 | convolution fusion | flops 1019314176 | bytes 10715144 | tf_op jit(solution)/shard_map/dot_general | solution.py:30
  36.5 0.7 collective-permute-start.11
  38.6 0.8 collective-permute-start.5
  40.9 1.5 %fusion.70 = bf16[8,2,8,384]{3,2,1,0:T(8,128)(2,1)S(1)} fusion(bf16[8,2,8,384]{3,2,1,0:T(8,128)(2,1)S(1)} %collective-permute-done.5, pred[8]{0:T(512)(128)(4,1)S(1)} %iota_compare_fusion.1, bf16[8,2,8,10368]{3,2,1,0:T(8,128)(2,1)S(1)} %constant_dynamic-update-slice_fusion.81, bf16[10368,384,1,1]{1,0,3,2:T(8,128)(2,1)S(1)} %bitcast.50), kind=kOutput, calls=%fused_computation.510 | convolution fusion | flops 1019412480 | bytes 10813448 | tf_op jit(solution)/shard_map/dot_general | solution.py:30
  42.5 0.7 collective-permute-start.15
  46.0 1.5 %fusion.3 = bf16[8,2,8,384]{3,2,1,0:T(8,128)(2,1)S(1)} fusion(bf16[8,2,8,10368]{3,2,1,0:T(8,128)(2,1)S(1)} %constant_dynamic-update-slice_fusion.108, bf16[10368,384,1,1]{1,0,3,2:T(8,128)(2,1)S(1)} %bitcast.51, pred[8]{0:T(512)(128)(4,1)S(1)} %iota_compare_fusion.1), kind=kOutput, calls=%fused_computation.200 | convolution fusion | flops 1019314176 | bytes 10715144 | tf_op jit(solution)/shard_map/dot_general | solution.py:30
  47.5 0.7 collective-permute-start.18
  49.6 0.7 collective-permute-start.12
  51.8 1.5 %fusion.71 = bf16[8,2,8,384]{3,2,1,0:T(8,128)(2,1)S(1)} fusion(bf16[8,2,8,384]{3,2,1,0:T(8,128)(2,1)S(1)} %collective-permute-done.12, pred[8]{0:T(512)(128)(4,1)S(1)} %iota_compare_fusion.1, bf16[8,2,8,10368]{3,2,1,0:T(8,128)(2,1)S(1)} %constant_dynamic-update-slice_fusion.135, bf16[10368,384,1,1]{1,0,3,2:T(8,128)(2,1)S(1)} %bitcast.52), kind=kOutput, calls=%fused_computation.511 | convolution fusion | flops 1019412480 | bytes 10813448 | tf_op jit(solution)/shard_map/dot_general | solution.py:30
  53.3 0.7 collective-permute-start.22
  54.7 0.9 collective-permute-start.21
  57.1 1.5 %fusion.4 = bf16[8,2,8,384]{3,2,1,0:T(8,128)(2,1)S(1)} fusion(bf16[8,2,8,10368]{3,2,1,0:T(8,128)(2,1)S(1)} %constant_dynamic-update-slice_fusion.162, bf16[10368,384,1,1]{1,0,3,2:T(8,128)(2,1)S(1)} %bitcast.53, pred[8]{0:T(512)(128)(4,1)S(1)} %iota_compare_fusion.1), kind=kOutput, calls=%fused_computation.201 | convolution fusion | flops 1019314176 | bytes 10715144 | tf_op jit(solution)/shard_map/dot_general | solution.py:30
  58.6 0.7 collective-permute-start.25
  60.7 0.7 collective-permute-start.19
  62.8 1.5 %fusion.72 = bf16[8,2,8,384]{3,2,1,0:T(8,128)(2,1)S(1)} fusion(bf16[8,2,8,384]{3,2,1,0:T(8,128)(2,1)S(1)} %collective-permute-done.19, pred[8]{0:T(512)(128)(4,1)S(1)} %iota_compare_fusion.1, bf16[8,2,8,10368]{3,2,1,0:T(8,128)(2,1)S(1)} %constant_dynamic-update-slice_fusion.189, bf16[10368,384,1,1]{1,0,3,2:T(8,128)(2,1)S(1)} %bitcast.54), kind=kOutput, calls=%fused_computation.512 | convolution fusion | flops 1019412480 | bytes 10813448 | tf_op jit(solution)/shard_map/dot_general | solution.py:30
  68.4 1.3 %collective-permute-start.32 = (bf16[1,2,8,384]{3,2,1,0:T(8,128)(2,1)S(1)}, bf16[1,2,8,384]{3,2,1,0:T(8,128)(2,1)S(1)}, u32[]{:S(2)}, u32[]{:S(2)}) collective-permute-start(bf16[1,2,8,384]{3,2,1,0:T(8,128)(2,1)S(1)} %get-tuple-element.5), channel_id=1, source_target_pairs={{448,0},{449,1},{450,2},{451,3},{452,4},{453,5},{454,6},{455,7},{4... | collective-permute-start | bytes 36872 | tf_op jit(solution)/shard_map/ppermute | solution.py:8
  69.8 40.6 %collective-permute-done.32 = bf16[1,2,8,384]{3,2,1,0:T(8,128)(2,1)S(1)} collective-permute-done((bf16[1,2,8,384]{3,2,1,0:T(8,128)(2,1)S(1)}, bf16[1,2,8,384]{3,2,1,0:T(8,128)(2,1)S(1)}, u32[]{:S(2)}, u32[]{:S(2)}) %collective-permute-start.32) | collective-permute-done | bytes 12320 | tf_op jit(solution)/shard_map/ppermute | solution.py:8
  (318 shorter events, 23.3 us)
Async XLA Ops:
  4.2 7.8 %collective-permute-start = (bf16[8,2,1,384]{3,2,1,0:T(2,128)(2,1)S(1)}, bf16[8,2,1,384]{3,2,1,0:T(2,128)(2,1)S(1)}, u32[]{:S(2)}, u32[]{:S(2)}) collective-permute-start(bf16[8,2,1,384]{3,2,1,0:T(2,128)(2,1)S(1)} %get-tuple-element.26), channel_id=1, source_target_pairs={{1,0},{2,1},{3,2},{4,3},{5,4},{6,5},{7,6},{8,7},{9,8},{10,9},{11,1... | collective-permute-start | bytes 36872 | tf_op jit(solution)/shard_map/ppermute | solution.py:8
  8.7 9.0 %collective-permute-start.1 = (bf16[8,2,1,384]{3,2,1,0:T(2,128)(2,1)S(1)}, bf16[8,2,1,384]{3,2,1,0:T(2,128)(2,1)S(1)}, u32[]{:S(2)}, u32[]{:S(2)}) collective-permute-start(bf16[8,2,1,384]{3,2,1,0:T(2,128)(2,1)S(1)} %get-tuple-element.27), channel_id=1, source_target_pairs={{0,1},{1,2},{2,3},{3,4},{4,5},{5,6},{6,7},{7,8},{8,9},{9,10},{10,1... | collective-permute-start | bytes 36872 | tf_op jit(solution)/shard_map/ppermute | solution.py:8
  22.8 5.5 %collective-permute-start.4 = (bf16[8,2,8,384]{3,2,1,0:T(8,128)(2,1)S(1)}, bf16[8,2,8,384]{3,2,1,0:T(8,128)(2,1)S(1)}, u32[]{:S(2)}, u32[]{:S(2)}) collective-permute-start(bf16[8,2,8,384]{3,2,1,0:T(8,128)(2,1)S(1)} %fusion), channel_id=1, source_target_pairs={{0,64},{1,65},{2,66},{3,67},{4,68},{5,69},{6,70},{7,71},{8,72},{9,... | collective-permute-start | bytes 294920 | tf_op jit(solution)/shard_map/ppermute | solution.py:8
  24.1 2.8 %collective-permute-start.2 = (bf16[8,2,1,384]{3,2,1,0:T(2,128)(2,1)S(1)}, bf16[8,2,1,384]{3,2,1,0:T(2,128)(2,1)S(1)}, u32[]{:S(2)}, u32[]{:S(2)}) collective-permute-start(bf16[8,2,1,384]{3,2,1,0:T(2,128)(2,1)S(1)} %get-tuple-element.24), channel_id=1, source_target_pairs={{1,64},{2,65},{3,66},{4,67},{5,68},{6,69},{7,70},{8,71},{9,72},{10... | collective-permute-start | bytes 36872 | tf_op jit(solution)/shard_map/ppermute | solution.py:8
  25.4 2.8 %collective-permute-start.3 = (bf16[8,2,1,384]{3,2,1,0:T(2,128)(2,1)S(1)}, bf16[8,2,1,384]{3,2,1,0:T(2,128)(2,1)S(1)}, u32[]{:S(2)}, u32[]{:S(2)}) collective-permute-start(bf16[8,2,1,384]{3,2,1,0:T(2,128)(2,1)S(1)} %get-tuple-element.25), channel_id=1, source_target_pairs={{0,65},{1,66},{2,67},{3,68},{4,69},{5,70},{6,71},{7,72},{8,73},{9,... | collective-permute-start | bytes 36872 | tf_op jit(solution)/shard_map/ppermute | solution.py:8
  31.4 2.1 %collective-permute-start.8 = (bf16[8,2,8,384]{3,2,1,0:T(8,128)(2,1)S(1)}, bf16[8,2,8,384]{3,2,1,0:T(8,128)(2,1)S(1)}, u32[]{:S(2)}, u32[]{:S(2)}) collective-permute-start(bf16[8,2,8,384]{3,2,1,0:T(8,128)(2,1)S(1)} %fusion.5), channel_id=1, source_target_pairs={{64,128},{65,129},{66,130},{67,131},{68,132},{69,133},{70,134},{71... | collective-permute-start | bytes 294920 | tf_op jit(solution)/shard_map/ppermute | solution.py:8
  32.2 1.3 %collective-permute-start.6 = (bf16[8,2,1,384]{3,2,1,0:T(2,128)(2,1)S(1)}, bf16[8,2,1,384]{3,2,1,0:T(2,128)(2,1)S(1)}, u32[]{:S(2)}, u32[]{:S(2)}) collective-permute-start(bf16[8,2,1,384]{3,2,1,0:T(2,128)(2,1)S(1)} %get-tuple-element.22), channel_id=1, source_target_pairs={{65,128},{66,129},{67,130},{68,131},{69,132},{70,133},{71,134},{72... | collective-permute-start | bytes 36872 | tf_op jit(solution)/shard_map/ppermute | solution.py:8
  32.8 0.7 collective-permute-start.7
  36.5 3.0 %collective-permute-start.11 = (bf16[8,2,8,384]{3,2,1,0:T(8,128)(2,1)S(1)}, bf16[8,2,8,384]{3,2,1,0:T(8,128)(2,1)S(1)}, u32[]{:S(2)}, u32[]{:S(2)}) collective-permute-start(bf16[8,2,8,384]{3,2,1,0:T(8,128)(2,1)S(1)} %fusion.2), channel_id=1, source_target_pairs={{128,192},{129,193},{130,194},{131,195},{132,196},{133,197},{134,1... | collective-permute-start | bytes 294920 | tf_op jit(solution)/shard_map/ppermute | solution.py:8
  37.2 2.2 %collective-permute-start.9 = (bf16[8,2,1,384]{3,2,1,0:T(2,128)(2,1)S(1)}, bf16[8,2,1,384]{3,2,1,0:T(2,128)(2,1)S(1)}, u32[]{:S(2)}, u32[]{:S(2)}) collective-permute-start(bf16[8,2,1,384]{3,2,1,0:T(2,128)(2,1)S(1)} %get-tuple-element.20), channel_id=1, source_target_pairs={{129,192},{130,193},{131,194},{132,195},{133,196},{134,197},{135,1... | collective-permute-start | bytes 36872 | tf_op jit(solution)/shard_map/ppermute | solution.py:8
  37.9 1.6 %collective-permute-start.10 = (bf16[8,2,1,384]{3,2,1,0:T(2,128)(2,1)S(1)}, bf16[8,2,1,384]{3,2,1,0:T(2,128)(2,1)S(1)}, u32[]{:S(2)}, u32[]{:S(2)}) collective-permute-start(bf16[8,2,1,384]{3,2,1,0:T(2,128)(2,1)S(1)} %get-tuple-element.21), channel_id=1, source_target_pairs={{128,193},{129,194},{130,195},{131,196},{132,197},{133,198},{134,1... | collective-permute-start | bytes 36872 | tf_op jit(solution)/shard_map/ppermute | solution.py:8
  38.6 2.3 %collective-permute-start.5 = (bf16[8,2,8,384]{3,2,1,0:T(8,128)(2,1)S(1)}, bf16[8,2,8,384]{3,2,1,0:T(8,128)(2,1)S(1)}, u32[]{:S(2)}, u32[]{:S(2)}) collective-permute-start(bf16[8,2,8,384]{3,2,1,0:T(8,128)(2,1)S(1)} %fusion.5), channel_id=1, source_target_pairs={{64,192},{65,193},{66,194},{67,195},{68,196},{69,197},{70,198},{71... | collective-permute-start | bytes 294920 | tf_op jit(solution)/shard_map/ppermute | solution.py:8
  42.5 2.1 %collective-permute-start.15 = (bf16[8,2,8,384]{3,2,1,0:T(8,128)(2,1)S(1)}, bf16[8,2,8,384]{3,2,1,0:T(8,128)(2,1)S(1)}, u32[]{:S(2)}, u32[]{:S(2)}) collective-permute-start(bf16[8,2,8,384]{3,2,1,0:T(8,128)(2,1)S(1)} %fusion.70), channel_id=1, source_target_pairs={{192,256},{193,257},{194,258},{195,259},{196,260},{197,261},{198,2... | collective-permute-start | bytes 294920 | tf_op jit(solution)/shard_map/ppermute | solution.py:8
  43.2 1.3 %collective-permute-start.13 = (bf16[8,2,1,384]{3,2,1,0:T(2,128)(2,1)S(1)}, bf16[8,2,1,384]{3,2,1,0:T(2,128)(2,1)S(1)}, u32[]{:S(2)}, u32[]{:S(2)}) collective-permute-start(bf16[8,2,1,384]{3,2,1,0:T(2,128)(2,1)S(1)} %get-tuple-element.18), channel_id=1, source_target_pairs={{193,256},{194,257},{195,258},{196,259},{197,260},{198,261},{199,2... | collective-permute-start | bytes 36872 | tf_op jit(solution)/shard_map/ppermute | solution.py:8
  47.5 2.8 %collective-permute-start.18 = (bf16[8,2,8,384]{3,2,1,0:T(8,128)(2,1)S(1)}, bf16[8,2,8,384]{3,2,1,0:T(8,128)(2,1)S(1)}, u32[]{:S(2)}, u32[]{:S(2)}) collective-permute-start(bf16[8,2,8,384]{3,2,1,0:T(8,128)(2,1)S(1)} %fusion.3), channel_id=1, source_target_pairs={{256,320},{257,321},{258,322},{259,323},{260,324},{261,325},{262,3... | collective-permute-start | bytes 294920 | tf_op jit(solution)/shard_map/ppermute | solution.py:8
  48.3 2.0 %collective-permute-start.16 = (bf16[8,2,1,384]{3,2,1,0:T(2,128)(2,1)S(1)}, bf16[8,2,1,384]{3,2,1,0:T(2,128)(2,1)S(1)}, u32[]{:S(2)}, u32[]{:S(2)}) collective-permute-start(bf16[8,2,1,384]{3,2,1,0:T(2,128)(2,1)S(1)} %get-tuple-element.16), channel_id=1, source_target_pairs={{257,320},{258,321},{259,322},{260,323},{261,324},{262,325},{263,3... | collective-permute-start | bytes 36872 | tf_op jit(solution)/shard_map/ppermute | solution.py:8
  48.9 1.4 %collective-permute-start.17 = (bf16[8,2,1,384]{3,2,1,0:T(2,128)(2,1)S(1)}, bf16[8,2,1,384]{3,2,1,0:T(2,128)(2,1)S(1)}, u32[]{:S(2)}, u32[]{:S(2)}) collective-permute-start(bf16[8,2,1,384]{3,2,1,0:T(2,128)(2,1)S(1)} %get-tuple-element.17), channel_id=1, source_target_pairs={{256,321},{257,322},{258,323},{259,324},{260,325},{261,326},{262,3... | collective-permute-start | bytes 36872 | tf_op jit(solution)/shard_map/ppermute | solution.py:8
  49.6 2.1 %collective-permute-start.12 = (bf16[8,2,8,384]{3,2,1,0:T(8,128)(2,1)S(1)}, bf16[8,2,8,384]{3,2,1,0:T(8,128)(2,1)S(1)}, u32[]{:S(2)}, u32[]{:S(2)}) collective-permute-start(bf16[8,2,8,384]{3,2,1,0:T(8,128)(2,1)S(1)} %fusion.70), channel_id=1, source_target_pairs={{192,320},{193,321},{194,322},{195,323},{196,324},{197,325},{198,3... | collective-permute-start | bytes 294920 | tf_op jit(solution)/shard_map/ppermute | solution.py:8
  53.3 2.3 %collective-permute-start.22 = (bf16[8,2,8,384]{3,2,1,0:T(8,128)(2,1)S(1)}, bf16[8,2,8,384]{3,2,1,0:T(8,128)(2,1)S(1)}, u32[]{:S(2)}, u32[]{:S(2)}) collective-permute-start(bf16[8,2,8,384]{3,2,1,0:T(8,128)(2,1)S(1)} %fusion.71), channel_id=1, source_target_pairs={{320,384},{321,385},{322,386},{323,387},{324,388},{325,389},{326,3... | collective-permute-start | bytes 294920 | tf_op jit(solution)/shard_map/ppermute | solution.py:8
  54.0 1.6 %collective-permute-start.20 = (bf16[8,2,1,384]{3,2,1,0:T(2,128)(2,1)S(1)}, bf16[8,2,1,384]{3,2,1,0:T(2,128)(2,1)S(1)}, u32[]{:S(2)}, u32[]{:S(2)}) collective-permute-start(bf16[8,2,1,384]{3,2,1,0:T(2,128)(2,1)S(1)} %get-tuple-element.14), channel_id=1, source_target_pairs={{321,384},{322,385},{323,386},{324,387},{325,388},{326,389},{327,3... | collective-permute-start | bytes 36872 | tf_op jit(solution)/shard_map/ppermute | solution.py:8
  54.7 0.9 collective-permute-start.21
  58.6 2.8 %collective-permute-start.25 = (bf16[8,2,8,384]{3,2,1,0:T(8,128)(2,1)S(1)}, bf16[8,2,8,384]{3,2,1,0:T(8,128)(2,1)S(1)}, u32[]{:S(2)}, u32[]{:S(2)}) collective-permute-start(bf16[8,2,8,384]{3,2,1,0:T(8,128)(2,1)S(1)} %fusion.4), channel_id=1, source_target_pairs={{384,448},{385,449},{386,450},{387,451},{388,452},{389,453},{390,4... | collective-permute-start | bytes 294920 | tf_op jit(solution)/shard_map/ppermute | solution.py:8
  59.3 2.0 %collective-permute-start.23 = (bf16[8,2,1,384]{3,2,1,0:T(2,128)(2,1)S(1)}, bf16[8,2,1,384]{3,2,1,0:T(2,128)(2,1)S(1)}, u32[]{:S(2)}, u32[]{:S(2)}) collective-permute-start(bf16[8,2,1,384]{3,2,1,0:T(2,128)(2,1)S(1)} %get-tuple-element.12), channel_id=1, source_target_pairs={{385,448},{386,449},{387,450},{388,451},{389,452},{390,453},{391,4... | collective-permute-start | bytes 36872 | tf_op jit(solution)/shard_map/ppermute | solution.py:8
  60.0 1.4 %collective-permute-start.24 = (bf16[8,2,1,384]{3,2,1,0:T(2,128)(2,1)S(1)}, bf16[8,2,1,384]{3,2,1,0:T(2,128)(2,1)S(1)}, u32[]{:S(2)}, u32[]{:S(2)}) collective-permute-start(bf16[8,2,1,384]{3,2,1,0:T(2,128)(2,1)S(1)} %get-tuple-element.13), channel_id=1, source_target_pairs={{384,449},{385,450},{386,451},{387,452},{388,453},{389,454},{390,4... | collective-permute-start | bytes 36872 | tf_op jit(solution)/shard_map/ppermute | solution.py:8
  60.7 2.1 %collective-permute-start.19 = (bf16[8,2,8,384]{3,2,1,0:T(8,128)(2,1)S(1)}, bf16[8,2,8,384]{3,2,1,0:T(8,128)(2,1)S(1)}, u32[]{:S(2)}, u32[]{:S(2)}) collective-permute-start(bf16[8,2,8,384]{3,2,1,0:T(8,128)(2,1)S(1)} %fusion.71), channel_id=1, source_target_pairs={{320,448},{321,449},{322,450},{323,451},{324,452},{325,453},{326,4... | collective-permute-start | bytes 294920 | tf_op jit(solution)/shard_map/ppermute | solution.py:8
  64.4 3.4 %collective-permute-start.26 = (bf16[1,2,8,384]{3,2,1,0:T(8,128)(2,1)S(1)}, bf16[1,2,8,384]{3,2,1,0:T(8,128)(2,1)S(1)}, u32[]{:S(2)}, u32[]{:S(2)}) collective-permute-start(bf16[1,2,8,384]{3,2,1,0:T(8,128)(2,1)S(1)} %get-tuple-element.11), channel_id=1, source_target_pairs={{448,384},{449,385},{450,386},{451,387},{452,388},{453,389},{454,3... | collective-permute-start | bytes 36872 | tf_op jit(solution)/shard_map/ppermute | solution.py:8
  65.1 3.4 %collective-permute-start.27 = (bf16[1,2,8,384]{3,2,1,0:T(8,128)(2,1)S(1)}, bf16[1,2,8,384]{3,2,1,0:T(8,128)(2,1)S(1)}, u32[]{:S(2)}, u32[]{:S(2)}) collective-permute-start(bf16[1,2,8,384]{3,2,1,0:T(8,128)(2,1)S(1)} %get-tuple-element.10), channel_id=1, source_target_pairs={{448,320},{449,321},{450,322},{451,323},{452,324},{453,325},{454,3... | collective-permute-start | bytes 36872 | tf_op jit(solution)/shard_map/ppermute | solution.py:8
  65.7 4.0 %collective-permute-start.28 = (bf16[1,2,8,384]{3,2,1,0:T(8,128)(2,1)S(1)}, bf16[1,2,8,384]{3,2,1,0:T(8,128)(2,1)S(1)}, u32[]{:S(2)}, u32[]{:S(2)}) collective-permute-start(bf16[1,2,8,384]{3,2,1,0:T(8,128)(2,1)S(1)} %get-tuple-element.9), channel_id=1, source_target_pairs={{448,256},{449,257},{450,258},{451,259},{452,260},{453,261},{454,2... | collective-permute-start | bytes 36872 | tf_op jit(solution)/shard_map/ppermute | solution.py:8
  66.4 3.4 %collective-permute-start.29 = (bf16[1,2,8,384]{3,2,1,0:T(8,128)(2,1)S(1)}, bf16[1,2,8,384]{3,2,1,0:T(8,128)(2,1)S(1)}, u32[]{:S(2)}, u32[]{:S(2)}) collective-permute-start(bf16[1,2,8,384]{3,2,1,0:T(8,128)(2,1)S(1)} %get-tuple-element.8), channel_id=1, source_target_pairs={{448,192},{449,193},{450,194},{451,195},{452,196},{453,197},{454,1... | collective-permute-start | bytes 36872 | tf_op jit(solution)/shard_map/ppermute | solution.py:8
  67.1 2.7 %collective-permute-start.30 = (bf16[1,2,8,384]{3,2,1,0:T(8,128)(2,1)S(1)}, bf16[1,2,8,384]{3,2,1,0:T(8,128)(2,1)S(1)}, u32[]{:S(2)}, u32[]{:S(2)}) collective-permute-start(bf16[1,2,8,384]{3,2,1,0:T(8,128)(2,1)S(1)} %get-tuple-element.7), channel_id=1, source_target_pairs={{448,128},{449,129},{450,130},{451,131},{452,132},{453,133},{454,1... | collective-permute-start | bytes 36872 | tf_op jit(solution)/shard_map/ppermute | solution.py:8
  67.7 2.0 %collective-permute-start.31 = (bf16[1,2,8,384]{3,2,1,0:T(8,128)(2,1)S(1)}, bf16[1,2,8,384]{3,2,1,0:T(8,128)(2,1)S(1)}, u32[]{:S(2)}, u32[]{:S(2)}) collective-permute-start(bf16[1,2,8,384]{3,2,1,0:T(8,128)(2,1)S(1)} %get-tuple-element.6), channel_id=1, source_target_pairs={{448,64},{449,65},{450,66},{451,67},{452,68},{453,69},{454,70},{45... | collective-permute-start | bytes 36872 | tf_op jit(solution)/shard_map/ppermute | solution.py:8
  68.4 41.9 %collective-permute-start.32 = (bf16[1,2,8,384]{3,2,1,0:T(8,128)(2,1)S(1)}, bf16[1,2,8,384]{3,2,1,0:T(8,128)(2,1)S(1)}, u32[]{:S(2)}, u32[]{:S(2)}) collective-permute-start(bf16[1,2,8,384]{3,2,1,0:T(8,128)(2,1)S(1)} %get-tuple-element.5), channel_id=1, source_target_pairs={{448,0},{449,1},{450,2},{451,3},{452,4},{453,5},{454,6},{455,7},{4... | collective-permute-start | bytes 36872 | tf_op jit(solution)/shard_map/ppermute | solution.py:8
  (3 other events, 4.9 us)

commit v2 on v1

--- a/solution.py
+++ b/solution.py
@@ -84,12 +84,8 @@
             residual = hop(produced, [(stage, stage + 2)], "section")
         current = nxt
     final = produced
-    result = final[segments - 1 : segments]
-    for target in range(segments - 1):
-        piece = hop(final[target : target + 1], [(segments - 1, target)], "section")
-        result = jnp.where(segment_index == target, piece, result)
-    return result
-
+    spread = lax.all_to_all(final, "section", 0, 0, tiled=True)
+    return spread[segments - 1 : segments]
 
 def solution(mesh):
     return jax.shard_map(

time: 112 us -> 108 us (0.964)
  blocking collectives: 0 us -> 42.4 us
  waiting for transfers between devices: 47.8 us -> 7.19 us
  starting transfers between devices: 29.9 us -> 24.6 us
    all_to_all x0 -> x1, blocking collectives: none -> 42.4 us  [local(): spread = lax.all_to_all(final, 'section', 0, 0, tiled=True)]
    ppermute x33 -> x26, waiting for transfers between devices: 47.8 us -> 7.19 us  [hop(): return lax.ppermute(block, axes, pairs)]
    ppermute x33 -> x26, starting transfers between devices: 29.9 us -> 24.6 us  [hop(): return lax.ppermute(block, axes, pairs)]
  transfers between devices with their start and end apart: 33 -> 26, of which waited for: 4 -> 3; matrix products, arithmetic and copies ran while one was open for 5% -> 5% of each run, Pallas kernels for 0% -> 0%
where the time goes in v2:
time: 108 us; the launch traced here: 107 us
  blocking collectives  42.4 us (39%)
  starting transfers between devices  24.6 us (23%)
  matrix products  12.2 us (11%)
  local copies, waits for them, and re-layouts  11.2 us (10%)
  waiting for transfers between devices  7.19 us (7%)
  other arithmetic  6.23 us (6%)
  between operations  3.51 us (3%)
    all_to_all x1, blocking collectives, local(): spread = lax.all_to_all(final, 'section', 0, 0, tiled=True)  42.4 us
    ppermute x26, starting transfers between devices, hop(): return lax.ppermute(block, axes, pairs)  24.6 us
    dot_general x8, matrix products, convolve(): out = jnp.dot(joined, flat, preferred_element_type=jnp.float32)  12.2 us
    unnamed x212, local copies, waits for them, and re-layouts  8.52 us
    ppermute x26, waiting for transfers between devices, hop(): return lax.ppermute(block, axes, pairs)  7.19 us
  transfers between devices with their start and end apart: 26, of which 3 were waited for; matrix products, arithmetic and copies ran while one was open for 5% of the time, Pallas kernels for 0%

profile of v2, /device:TPU:256, one launch (start us, length us, event | category | flops | bytes accessed | tf_op | source)
XLA Modules:
  0.0 107.4 jit_solution(16647713533567185779)
XLA Ops:
  0.0 1.2 %dynamic_slice.27 = s32[1]{0:T(128)} dynamic-slice(s32[64]{0:T(128)} %param.5, s32[]{:T(128)S(6)} %select_n.67), dynamic_slice_sizes={1} | dynamic-slice | bytes 12 | tf_op jit(solution)/shard_map/dynamic_slice | solution.py:40
  3.2 1.0 broadcast_select_fusion
  4.2 4.5 %collective-permute-start = (bf16[8,2,1,384]{3,2,1,0:T(2,128)(2,1)S(1)}, bf16[8,2,1,384]{3,2,1,0:T(2,128)(2,1)S(1)}, u32[]{:S(2)}, u32[]{:S(2)}) collective-permute-start(bf16[8,2,1,384]{3,2,1,0:T(2,128)(2,1)S(1)} %get-tuple-element.19), channel_id=1, source_target_pairs={{1,0},{2,1},{3,2},{4,3},{5,4},{6,5},{7,6},{8,7},{9,8},{10,9},{11,1... | collective-permute-start | bytes 36872 | tf_op jit(solution)/shard_map/ppermute | solution.py:8
  8.7 1.9 %collective-permute-start.1 = (bf16[8,2,1,384]{3,2,1,0:T(2,128)(2,1)S(1)}, bf16[8,2,1,384]{3,2,1,0:T(2,128)(2,1)S(1)}, u32[]{:S(2)}, u32[]{:S(2)}) collective-permute-start(bf16[8,2,1,384]{3,2,1,0:T(2,128)(2,1)S(1)} %get-tuple-element.20), channel_id=1, source_target_pairs={{0,1},{1,2},{2,3},{3,4},{4,5},{5,6},{6,7},{7,8},{8,9},{9,10},{10,1... | collective-permute-start | bytes 36872 | tf_op jit(solution)/shard_map/ppermute | solution.py:8
  11.3 0.7 convert_reduce_fusion
  12.1 5.6 %collective-permute-done.1 = bf16[8,2,1,384]{3,2,1,0:T(2,128)(2,1)S(1)} collective-permute-done((bf16[8,2,1,384]{3,2,1,0:T(2,128)(2,1)S(1)}, bf16[8,2,1,384]{3,2,1,0:T(2,128)(2,1)S(1)}, u32[]{:S(2)}, u32[]{:S(2)}) %collective-permute-start.1) | collective-permute-done | bytes 12320 | tf_op jit(solution)/shard_map/ppermute | solution.py:8
  19.2 2.1 %copy-done = bf16[1,3,3,1152,384]{4,3,2,1,0:T(8,128)(2,1)S(1)} copy-done((bf16[1,3,3,1152,384]{4,3,2,1,0:T(8,128)(2,1)S(1)}, bf16[1,3,3,1152,384]{4,3,2,1,0:T(8,128)(2,1)}, u32[]{:S(2)}) %copy-start) | copy-done | bytes 7962648
  21.3 1.5 %fusion = bf16[8,2,8,384]{3,2,1,0:T(8,128)(2,1)S(1)} fusion(bf16[8,2,8,10368]{3,2,1,0:T(8,128)(2,1)S(1)} %constant_dynamic-update-slice_fusion, bf16[10368,384,1,1]{1,0,3,2:T(8,128)(2,1)S(1)} %bitcast.47, pred[8]{0:T(512)(128)(4,1)S(1)} %iota_compare_fusion.1), kind=kOutput, calls=%fused_computation.197 | convolution fusion | flops 1019314176 | bytes 10715144 | tf_op jit(solution)/shard_map/dot_general | solution.py:30
  22.8 1.3 %collective-permute-start.4 = (bf16[8,2,8,384]{3,2,1,0:T(8,128)(2,1)S(1)}, bf16[8,2,8,384]{3,2,1,0:T(8,128)(2,1)S(1)}, u32[]{:S(2)}, u32[]{:S(2)}) collective-permute-start(bf16[8,2,8,384]{3,2,1,0:T(8,128)(2,1)S(1)} %fusion), channel_id=1, source_target_pairs={{0,64},{1,65},{2,66},{3,67},{4,68},{5,69},{6,70},{7,71},{8,72},{9,... | collective-permute-start | bytes 294920 | tf_op jit(solution)/shard_map/ppermute | solution.py:8
  24.1 1.3 %collective-permute-start.2 = (bf16[8,2,1,384]{3,2,1,0:T(2,128)(2,1)S(1)}, bf16[8,2,1,384]{3,2,1,0:T(2,128)(2,1)S(1)}, u32[]{:S(2)}, u32[]{:S(2)}) collective-permute-start(bf16[8,2,1,384]{3,2,1,0:T(2,128)(2,1)S(1)} %get-tuple-element.17), channel_id=1, source_target_pairs={{1,64},{2,65},{3,66},{4,67},{5,68},{6,69},{7,70},{8,71},{9,72},{10... | collective-permute-start | bytes 36872 | tf_op jit(solution)/shard_map/ppermute | solution.py:8
  25.4 1.3 %collective-permute-start.3 = (bf16[8,2,1,384]{3,2,1,0:T(2,128)(2,1)S(1)}, bf16[8,2,1,384]{3,2,1,0:T(2,128)(2,1)S(1)}, u32[]{:S(2)}, u32[]{:S(2)}) collective-permute-start(bf16[8,2,1,384]{3,2,1,0:T(2,128)(2,1)S(1)} %get-tuple-element.18), channel_id=1, source_target_pairs={{0,65},{1,66},{2,67},{3,68},{4,69},{5,70},{6,71},{7,72},{8,73},{9,... | collective-permute-start | bytes 36872 | tf_op jit(solution)/shard_map/ppermute | solution.py:8
  27.0 1.3 %collective-permute-done.3 = bf16[8,2,1,384]{3,2,1,0:T(2,128)(2,1)S(1)} collective-permute-done((bf16[8,2,1,384]{3,2,1,0:T(2,128)(2,1)S(1)}, bf16[8,2,1,384]{3,2,1,0:T(2,128)(2,1)S(1)}, u32[]{:S(2)}, u32[]{:S(2)}) %collective-permute-start.3) | collective-permute-done | bytes 12320 | tf_op jit(solution)/shard_map/ppermute | solution.py:8
  29.9 1.5 %fusion.5 = bf16[8,2,8,384]{3,2,1,0:T(8,128)(2,1)S(1)} fusion(bf16[8,2,8,10368]{3,2,1,0:T(8,128)(2,1)S(1)} %constant_dynamic-update-slice_fusion.27, bf16[10368,384,1,1]{1,0,3,2:T(8,128)(2,1)S(1)} %bitcast.48, pred[8]{0:T(512)(128)(4,1)S(1)} %iota_compare_fusion.1, bf16[8,2,8,384]{3,2,1,0:T(8,128)(2,1)S(1)} %copy-done.1), kind=kOutput, calls=%fused_computation.202 | convolution fusion | flops 1019461632 | bytes 10813448 | tf_op jit(solution)/shard_map/dot_general | solution.py:30
  31.4 0.7 collective-permute-start.8
  32.8 0.7 collective-permute-start.7
  35.0 1.5 %fusion.2 = bf16[8,2,8,384]{3,2,1,0:T(8,128)(2,1)S(1)} fusion(bf16[8,2,8,10368]{3,2,1,0:T(8,128)(2,1)S(1)} %constant_dynamic-update-slice_fusion.54, bf16[10368,384,1,1]{1,0,3,2:T(8,128)(2,1)S(1)} %bitcast.49, pred[8]{0:T(512)(128)(4,1)S(1)} %iota_compare_fusion.1), kind=kOutput, calls=%fused_computation.199 | convolution fusion | flops 1019314176 | bytes 10715144 | tf_op jit(solution)/shard_map/dot_general | solution.py:30
  36.5 0.7 collective-permute-start.11
  38.6 0.8 collective-permute-start.5
  40.9 1.5 %fusion.70 = bf16[8,2,8,384]{3,2,1,0:T(8,128)(2,1)S(1)} fusion(bf16[8,2,8,384]{3,2,1,0:T(8,128)(2,1)S(1)} %collective-permute-done.5, pred[8]{0:T(512)(128)(4,1)S(1)} %iota_compare_fusion.1, bf16[8,2,8,10368]{3,2,1,0:T(8,128)(2,1)S(1)} %constant_dynamic-update-slice_fusion.81, bf16[10368,384,1,1]{1,0,3,2:T(8,128)(2,1)S(1)} %bitcast.50), kind=kOutput, calls=%fused_computation.510 | convolution fusion | flops 1019412480 | bytes 10813448 | tf_op jit(solution)/shard_map/dot_general | solution.py:30
  42.5 0.7 collective-permute-start.15
  43.9 0.7 collective-permute-start.14
  46.0 1.5 %fusion.3 = bf16[8,2,8,384]{3,2,1,0:T(8,128)(2,1)S(1)} fusion(bf16[8,2,8,10368]{3,2,1,0:T(8,128)(2,1)S(1)} %constant_dynamic-update-slice_fusion.108, bf16[10368,384,1,1]{1,0,3,2:T(8,128)(2,1)S(1)} %bitcast.51, pred[8]{0:T(512)(128)(4,1)S(1)} %iota_compare_fusion.1), kind=kOutput, calls=%fused_computation.200 | convolution fusion | flops 1019314176 | bytes 10715144 | tf_op jit(solution)/shard_map/dot_general | solution.py:30
  47.5 0.7 collective-permute-start.18
  49.6 0.7 collective-permute-start.12
  51.8 1.5 %fusion.71 = bf16[8,2,8,384]{3,2,1,0:T(8,128)(2,1)S(1)} fusion(bf16[8,2,8,384]{3,2,1,0:T(8,128)(2,1)S(1)} %collective-permute-done.12, pred[8]{0:T(512)(128)(4,1)S(1)} %iota_compare_fusion.1, bf16[8,2,8,10368]{3,2,1,0:T(8,128)(2,1)S(1)} %constant_dynamic-update-slice_fusion.135, bf16[10368,384,1,1]{1,0,3,2:T(8,128)(2,1)S(1)} %bitcast.52), kind=kOutput, calls=%fused_computation.511 | convolution fusion | flops 1019412480 | bytes 10813448 | tf_op jit(solution)/shard_map/dot_general | solution.py:30
  53.3 0.7 collective-permute-start.22
  54.7 0.9 collective-permute-start.21
  57.1 1.5 %fusion.4 = bf16[8,2,8,384]{3,2,1,0:T(8,128)(2,1)S(1)} fusion(bf16[8,2,8,10368]{3,2,1,0:T(8,128)(2,1)S(1)} %constant_dynamic-update-slice_fusion.162, bf16[10368,384,1,1]{1,0,3,2:T(8,128)(2,1)S(1)} %bitcast.53, pred[8]{0:T(512)(128)(4,1)S(1)} %iota_compare_fusion.1), kind=kOutput, calls=%fused_computation.201 | convolution fusion | flops 1019314176 | bytes 10715144 | tf_op jit(solution)/shard_map/dot_general | solution.py:30
  58.6 0.7 collective-permute-start.25
  60.7 0.7 collective-permute-start.19
  62.8 1.5 %fusion.72 = bf16[8,2,8,384]{3,2,1,0:T(8,128)(2,1)S(1)} fusion(bf16[8,2,8,384]{3,2,1,0:T(8,128)(2,1)S(1)} %collective-permute-done.19, pred[8]{0:T(512)(128)(4,1)S(1)} %iota_compare_fusion.1, bf16[8,2,8,10368]{3,2,1,0:T(8,128)(2,1)S(1)} %constant_dynamic-update-slice_fusion.189, bf16[10368,384,1,1]{1,0,3,2:T(8,128)(2,1)S(1)} %bitcast.54), kind=kOutput, calls=%fused_computation.512 | convolution fusion | flops 1019412480 | bytes 10813448 | tf_op jit(solution)/shard_map/dot_general | solution.py:30
  64.4 42.4 %all_to_all.5 = bf16[8,2,8,384]{3,2,1,0:T(8,128)(2,1)S(1)} all-to-all(bf16[8,2,8,384]{3,2,1,0:T(8,128)(2,1)S(1)} %fusion.72), channel_id=1, replica_groups=mesh['section'=8,'tile'=64] {'section'}, dimensions={0} | all-to-all | bytes 196608 | tf_op jit(solution)/shard_map/all_to_all | solution.py:87
  (304 shorter events, 18.6 us)
Async XLA Ops:
  4.2 7.8 %collective-permute-start = (bf16[8,2,1,384]{3,2,1,0:T(2,128)(2,1)S(1)}, bf16[8,2,1,384]{3,2,1,0:T(2,128)(2,1)S(1)}, u32[]{:S(2)}, u32[]{:S(2)}) collective-permute-start(bf16[8,2,1,384]{3,2,1,0:T(2,128)(2,1)S(1)} %get-tuple-element.19), channel_id=1, source_target_pairs={{1,0},{2,1},{3,2},{4,3},{5,4},{6,5},{7,6},{8,7},{9,8},{10,9},{11,1... | collective-permute-start | bytes 36872 | tf_op jit(solution)/shard_map/ppermute | solution.py:8
  8.7 9.0 %collective-permute-start.1 = (bf16[8,2,1,384]{3,2,1,0:T(2,128)(2,1)S(1)}, bf16[8,2,1,384]{3,2,1,0:T(2,128)(2,1)S(1)}, u32[]{:S(2)}, u32[]{:S(2)}) collective-permute-start(bf16[8,2,1,384]{3,2,1,0:T(2,128)(2,1)S(1)} %get-tuple-element.20), channel_id=1, source_target_pairs={{0,1},{1,2},{2,3},{3,4},{4,5},{5,6},{6,7},{7,8},{8,9},{9,10},{10,1... | collective-permute-start | bytes 36872 | tf_op jit(solution)/shard_map/ppermute | solution.py:8
  18.0 3.3 %copy-start = (bf16[1,3,3,1152,384]{4,3,2,1,0:T(8,128)(2,1)S(1)}, bf16[1,3,3,1152,384]{4,3,2,1,0:T(8,128)(2,1)}, u32[]{:S(2)}) copy-start(bf16[1,3,3,1152,384]{4,3,2,1,0:T(8,128)(2,1)} %param.6) | copy-start | bytes 23887876
  22.8 5.5 %collective-permute-start.4 = (bf16[8,2,8,384]{3,2,1,0:T(8,128)(2,1)S(1)}, bf16[8,2,8,384]{3,2,1,0:T(8,128)(2,1)S(1)}, u32[]{:S(2)}, u32[]{:S(2)}) collective-permute-start(bf16[8,2,8,384]{3,2,1,0:T(8,128)(2,1)S(1)} %fusion), channel_id=1, source_target_pairs={{0,64},{1,65},{2,66},{3,67},{4,68},{5,69},{6,70},{7,71},{8,72},{9,... | collective-permute-start | bytes 294920 | tf_op jit(solution)/shard_map/ppermute | solution.py:8
  24.1 2.8 %collective-permute-start.2 = (bf16[8,2,1,384]{3,2,1,0:T(2,128)(2,1)S(1)}, bf16[8,2,1,384]{3,2,1,0:T(2,128)(2,1)S(1)}, u32[]{:S(2)}, u32[]{:S(2)}) collective-permute-start(bf16[8,2,1,384]{3,2,1,0:T(2,128)(2,1)S(1)} %get-tuple-element.17), channel_id=1, source_target_pairs={{1,64},{2,65},{3,66},{4,67},{5,68},{6,69},{7,70},{8,71},{9,72},{10... | collective-permute-start | bytes 36872 | tf_op jit(solution)/shard_map/ppermute | solution.py:8
  25.4 2.8 %collective-permute-start.3 = (bf16[8,2,1,384]{3,2,1,0:T(2,128)(2,1)S(1)}, bf16[8,2,1,384]{3,2,1,0:T(2,128)(2,1)S(1)}, u32[]{:S(2)}, u32[]{:S(2)}) collective-permute-start(bf16[8,2,1,384]{3,2,1,0:T(2,128)(2,1)S(1)} %get-tuple-element.18), channel_id=1, source_target_pairs={{0,65},{1,66},{2,67},{3,68},{4,69},{5,70},{6,71},{7,72},{8,73},{9,... | collective-permute-start | bytes 36872 | tf_op jit(solution)/shard_map/ppermute | solution.py:8
  29.0 0.9 copy-start.1
  31.4 2.1 %collective-permute-start.8 = (bf16[8,2,8,384]{3,2,1,0:T(8,128)(2,1)S(1)}, bf16[8,2,8,384]{3,2,1,0:T(8,128)(2,1)S(1)}, u32[]{:S(2)}, u32[]{:S(2)}) collective-permute-start(bf16[8,2,8,384]{3,2,1,0:T(8,128)(2,1)S(1)} %fusion.5), channel_id=1, source_target_pairs={{64,128},{65,129},{66,130},{67,131},{68,132},{69,133},{70,134},{71... | collective-permute-start | bytes 294920 | tf_op jit(solution)/shard_map/ppermute | solution.py:8
  32.2 1.3 %collective-permute-start.6 = (bf16[8,2,1,384]{3,2,1,0:T(2,128)(2,1)S(1)}, bf16[8,2,1,384]{3,2,1,0:T(2,128)(2,1)S(1)}, u32[]{:S(2)}, u32[]{:S(2)}) collective-permute-start(bf16[8,2,1,384]{3,2,1,0:T(2,128)(2,1)S(1)} %get-tuple-element.15), channel_id=1, source_target_pairs={{65,128},{66,129},{67,130},{68,131},{69,132},{70,133},{71,134},{72... | collective-permute-start | bytes 36872 | tf_op jit(solution)/shard_map/ppermute | solution.py:8
  32.8 0.7 collective-permute-start.7
  36.5 3.0 %collective-permute-start.11 = (bf16[8,2,8,384]{3,2,1,0:T(8,128)(2,1)S(1)}, bf16[8,2,8,384]{3,2,1,0:T(8,128)(2,1)S(1)}, u32[]{:S(2)}, u32[]{:S(2)}) collective-permute-start(bf16[8,2,8,384]{3,2,1,0:T(8,128)(2,1)S(1)} %fusion.2), channel_id=1, source_target_pairs={{128,192},{129,193},{130,194},{131,195},{132,196},{133,197},{134,1... | collective-permute-start | bytes 294920 | tf_op jit(solution)/shard_map/ppermute | solution.py:8
  37.2 2.2 %collective-permute-start.9 = (bf16[8,2,1,384]{3,2,1,0:T(2,128)(2,1)S(1)}, bf16[8,2,1,384]{3,2,1,0:T(2,128)(2,1)S(1)}, u32[]{:S(2)}, u32[]{:S(2)}) collective-permute-start(bf16[8,2,1,384]{3,2,1,0:T(2,128)(2,1)S(1)} %get-tuple-element.13), channel_id=1, source_target_pairs={{129,192},{130,193},{131,194},{132,195},{133,196},{134,197},{135,1... | collective-permute-start | bytes 36872 | tf_op jit(solution)/shard_map/ppermute | solution.py:8
  37.9 1.6 %collective-permute-start.10 = (bf16[8,2,1,384]{3,2,1,0:T(2,128)(2,1)S(1)}, bf16[8,2,1,384]{3,2,1,0:T(2,128)(2,1)S(1)}, u32[]{:S(2)}, u32[]{:S(2)}) collective-permute-start(bf16[8,2,1,384]{3,2,1,0:T(2,128)(2,1)S(1)} %get-tuple-element.14), channel_id=1, source_target_pairs={{128,193},{129,194},{130,195},{131,196},{132,197},{133,198},{134,1... | collective-permute-start | bytes 36872 | tf_op jit(solution)/shard_map/ppermute | solution.py:8
  38.6 2.3 %collective-permute-start.5 = (bf16[8,2,8,384]{3,2,1,0:T(8,128)(2,1)S(1)}, bf16[8,2,8,384]{3,2,1,0:T(8,128)(2,1)S(1)}, u32[]{:S(2)}, u32[]{:S(2)}) collective-permute-start(bf16[8,2,8,384]{3,2,1,0:T(8,128)(2,1)S(1)} %fusion.5), channel_id=1, source_target_pairs={{64,192},{65,193},{66,194},{67,195},{68,196},{69,197},{70,198},{71... | collective-permute-start | bytes 294920 | tf_op jit(solution)/shard_map/ppermute | solution.py:8
  42.5 2.1 %collective-permute-start.15 = (bf16[8,2,8,384]{3,2,1,0:T(8,128)(2,1)S(1)}, bf16[8,2,8,384]{3,2,1,0:T(8,128)(2,1)S(1)}, u32[]{:S(2)}, u32[]{:S(2)}) collective-permute-start(bf16[8,2,8,384]{3,2,1,0:T(8,128)(2,1)S(1)} %fusion.70), channel_id=1, source_target_pairs={{192,256},{193,257},{194,258},{195,259},{196,260},{197,261},{198,2... | collective-permute-start | bytes 294920 | tf_op jit(solution)/shard_map/ppermute | solution.py:8
  43.2 1.3 %collective-permute-start.13 = (bf16[8,2,1,384]{3,2,1,0:T(2,128)(2,1)S(1)}, bf16[8,2,1,384]{3,2,1,0:T(2,128)(2,1)S(1)}, u32[]{:S(2)}, u32[]{:S(2)}) collective-permute-start(bf16[8,2,1,384]{3,2,1,0:T(2,128)(2,1)S(1)} %get-tuple-element.11), channel_id=1, source_target_pairs={{193,256},{194,257},{195,258},{196,259},{197,260},{198,261},{199,2... | collective-permute-start | bytes 36872 | tf_op jit(solution)/shard_map/ppermute | solution.py:8
  43.9 0.7 collective-permute-start.14
  47.5 2.8 %collective-permute-start.18 = (bf16[8,2,8,384]{3,2,1,0:T(8,128)(2,1)S(1)}, bf16[8,2,8,384]{3,2,1,0:T(8,128)(2,1)S(1)}, u32[]{:S(2)}, u32[]{:S(2)}) collective-permute-start(bf16[8,2,8,384]{3,2,1,0:T(8,128)(2,1)S(1)} %fusion.3), channel_id=1, source_target_pairs={{256,320},{257,321},{258,322},{259,323},{260,324},{261,325},{262,3... | collective-permute-start | bytes 294920 | tf_op jit(solution)/shard_map/ppermute | solution.py:8
  48.3 2.0 %collective-permute-start.16 = (bf16[8,2,1,384]{3,2,1,0:T(2,128)(2,1)S(1)}, bf16[8,2,1,384]{3,2,1,0:T(2,128)(2,1)S(1)}, u32[]{:S(2)}, u32[]{:S(2)}) collective-permute-start(bf16[8,2,1,384]{3,2,1,0:T(2,128)(2,1)S(1)} %get-tuple-element.9), channel_id=1, source_target_pairs={{257,320},{258,321},{259,322},{260,323},{261,324},{262,325},{263,3... | collective-permute-start | bytes 36872 | tf_op jit(solution)/shard_map/ppermute | solution.py:8
  48.9 1.4 %collective-permute-start.17 = (bf16[8,2,1,384]{3,2,1,0:T(2,128)(2,1)S(1)}, bf16[8,2,1,384]{3,2,1,0:T(2,128)(2,1)S(1)}, u32[]{:S(2)}, u32[]{:S(2)}) collective-permute-start(bf16[8,2,1,384]{3,2,1,0:T(2,128)(2,1)S(1)} %get-tuple-element.10), channel_id=1, source_target_pairs={{256,321},{257,322},{258,323},{259,324},{260,325},{261,326},{262,3... | collective-permute-start | bytes 36872 | tf_op jit(solution)/shard_map/ppermute | solution.py:8
  49.6 2.1 %collective-permute-start.12 = (bf16[8,2,8,384]{3,2,1,0:T(8,128)(2,1)S(1)}, bf16[8,2,8,384]{3,2,1,0:T(8,128)(2,1)S(1)}, u32[]{:S(2)}, u32[]{:S(2)}) collective-permute-start(bf16[8,2,8,384]{3,2,1,0:T(8,128)(2,1)S(1)} %fusion.70), channel_id=1, source_target_pairs={{192,320},{193,321},{194,322},{195,323},{196,324},{197,325},{198,3... | collective-permute-start | bytes 294920 | tf_op jit(solution)/shard_map/ppermute | solution.py:8
  53.3 2.3 %collective-permute-start.22 = (bf16[8,2,8,384]{3,2,1,0:T(8,128)(2,1)S(1)}, bf16[8,2,8,384]{3,2,1,0:T(8,128)(2,1)S(1)}, u32[]{:S(2)}, u32[]{:S(2)}) collective-permute-start(bf16[8,2,8,384]{3,2,1,0:T(8,128)(2,1)S(1)} %fusion.71), channel_id=1, source_target_pairs={{320,384},{321,385},{322,386},{323,387},{324,388},{325,389},{326,3... | collective-permute-start | bytes 294920 | tf_op jit(solution)/shard_map/ppermute | solution.py:8
  54.0 1.6 %collective-permute-start.20 = (bf16[8,2,1,384]{3,2,1,0:T(2,128)(2,1)S(1)}, bf16[8,2,1,384]{3,2,1,0:T(2,128)(2,1)S(1)}, u32[]{:S(2)}, u32[]{:S(2)}) collective-permute-start(bf16[8,2,1,384]{3,2,1,0:T(2,128)(2,1)S(1)} %get-tuple-element.7), channel_id=1, source_target_pairs={{321,384},{322,385},{323,386},{324,387},{325,388},{326,389},{327,3... | collective-permute-start | bytes 36872 | tf_op jit(solution)/shard_map/ppermute | solution.py:8
  54.7 0.9 collective-permute-start.21
  58.6 2.8 %collective-permute-start.25 = (bf16[8,2,8,384]{3,2,1,0:T(8,128)(2,1)S(1)}, bf16[8,2,8,384]{3,2,1,0:T(8,128)(2,1)S(1)}, u32[]{:S(2)}, u32[]{:S(2)}) collective-permute-start(bf16[8,2,8,384]{3,2,1,0:T(8,128)(2,1)S(1)} %fusion.4), channel_id=1, source_target_pairs={{384,448},{385,449},{386,450},{387,451},{388,452},{389,453},{390,4... | collective-permute-start | bytes 294920 | tf_op jit(solution)/shard_map/ppermute | solution.py:8
  59.3 2.0 %collective-permute-start.23 = (bf16[8,2,1,384]{3,2,1,0:T(2,128)(2,1)S(1)}, bf16[8,2,1,384]{3,2,1,0:T(2,128)(2,1)S(1)}, u32[]{:S(2)}, u32[]{:S(2)}) collective-permute-start(bf16[8,2,1,384]{3,2,1,0:T(2,128)(2,1)S(1)} %get-tuple-element.5), channel_id=1, source_target_pairs={{385,448},{386,449},{387,450},{388,451},{389,452},{390,453},{391,4... | collective-permute-start | bytes 36872 | tf_op jit(solution)/shard_map/ppermute | solution.py:8
  60.0 1.4 %collective-permute-start.24 = (bf16[8,2,1,384]{3,2,1,0:T(2,128)(2,1)S(1)}, bf16[8,2,1,384]{3,2,1,0:T(2,128)(2,1)S(1)}, u32[]{:S(2)}, u32[]{:S(2)}) collective-permute-start(bf16[8,2,1,384]{3,2,1,0:T(2,128)(2,1)S(1)} %get-tuple-element.6), channel_id=1, source_target_pairs={{384,449},{385,450},{386,451},{387,452},{388,453},{389,454},{390,4... | collective-permute-start | bytes 36872 | tf_op jit(solution)/shard_map/ppermute | solution.py:8
  60.7 2.1 %collective-permute-start.19 = (bf16[8,2,8,384]{3,2,1,0:T(8,128)(2,1)S(1)}, bf16[8,2,8,384]{3,2,1,0:T(8,128)(2,1)S(1)}, u32[]{:S(2)}, u32[]{:S(2)}) collective-permute-start(bf16[8,2,8,384]{3,2,1,0:T(8,128)(2,1)S(1)} %fusion.71), channel_id=1, source_target_pairs={{320,448},{321,449},{322,450},{323,451},{324,452},{325,453},{326,4... | collective-permute-start | bytes 294920 | tf_op jit(solution)/shard_map/ppermute | solution.py:8

commit v3 on v2

--- a/solution.py
+++ b/solution.py
@@ -60,10 +60,12 @@
         right = hop(first, [(src + t + 1, dst + t) for t in range(tiles - 1)], both)
         return left, right
 
+    from_left = hop(latents, [(t - 1, t) for t in range(1, tiles)], "tile")
+    from_right = hop(latents[:, :, 0:1], [(t + 1, t) for t in range(tiles - 1)], "tile")
+    left_count = col_counts[jnp.maximum(tile_index - 1, 0)]
+    left = lax.dynamic_slice_in_dim(from_left, left_count - 1, 1, 2)
+    right = from_right
     stream = jnp.where(col_live, latents, zero)
-    first, last = edges(stream)
-    left = hop(last, [(t - 1, t) for t in range(1, tiles)], "tile")
-    right = hop(first, [(t + 1, t) for t in range(tiles - 1)], "tile")
     current = stream
     residual = stream
     for stage in range(segments):

time: 108 us -> 108 us (level)
  waiting for transfers between devices: 7.19 us -> 1.54 us
  starting transfers between devices: 24.6 us -> 27.4 us
  between operations: 3.51 us -> 4.76 us
    ppermute x26, waiting for transfers between devices: 7.19 us -> 1.54 us  [hop(): return lax.ppermute(block, axes, pairs)]
    ppermute x26, starting transfers between devices: 24.6 us -> 27.4 us  [hop(): return lax.ppermute(block, axes, pairs)]
    unnamed x212 -> x213, local copies, waits for them, and re-layouts: 8.52 us -> 8.52 us
  transfers between devices with their start and end apart: 26 -> 26, of which waited for: 3 -> 2; matrix products, arithmetic and copies ran while one was open for 5% -> 8% of each run, Pallas kernels for 0% -> 0%
where the time goes in v3:
time: 108 us
  blocking collectives  43.2 us (40%)
  starting transfers between devices  27.4 us (25%)
  local copies, waits for them, and re-layouts  12.2 us (11%)
  matrix products  12.2 us (11%)
  other arithmetic  6.22 us (6%)
  between operations  4.76 us (4%)
  waiting for transfers between devices  1.54 us (1%)
    all_to_all x1, blocking collectives, local(): spread = lax.all_to_all(final, 'section', 0, 0, tiled=True)  43.2 us
    ppermute x26, starting transfers between devices, hop(): return lax.ppermute(block, axes, pairs)  27.4 us
    dot_general x8, matrix products, convolve(): out = jnp.dot(joined, flat, preferred_element_type=jnp.float32)  12.2 us
    unnamed x213, local copies, waits for them, and re-layouts  8.52 us
  transfers between devices with their start and end apart: 26, of which 2 were waited for; matrix products, arithmetic and copies ran while one was open for 8% of the time, Pallas kernels for 0%

profile of v3, /device:TPU:256, one launch (start us, length us, event | category | flops | bytes accessed | tf_op | source)
XLA Modules:
  0.0 107.6 jit_solution(8572619916308595713)
XLA Ops:
  0.0 3.5 %collective-permute-start.1 = (bf16[8,2,8,384]{3,2,1,0:T(8,128)(2,1)}, bf16[8,2,8,384]{3,2,1,0:T(8,128)(2,1)S(1)}, u32[]{:S(2)}, u32[]{:S(2)}) collective-permute-start(bf16[8,2,8,384]{3,2,1,0:T(8,128)(2,1)} %param.4), channel_id=1, source_target_pairs={{0,1},{1,2},{2,3},{3,4},{4,5},{5,6},{6,7},{7,8},{8,9},{9,10},{10,1... | collective-permute-start | bytes 294920 | tf_op jit(solution)/shard_map/ppermute | solution.py:8
  3.5 0.9 slice.699
  4.4 5.7 %collective-permute-start = (bf16[8,2,1,384]{3,0,2,1:T(8,128)(2,1)S(1)}, bf16[8,2,1,384]{3,0,2,1:T(8,128)(2,1)S(1)}, u32[]{:S(2)}, u32[]{:S(2)}) collective-permute-start(bf16[8,2,1,384]{3,0,2,1:T(8,128)(2,1)S(1)} %copy.22), channel_id=1, source_target_pairs={{1,0},{2,1},{3,2},{4,3},{5,4},{6,5},{7,6},{8,7},{9,8},{10,9},{11,1... | collective-permute-start | bytes 36872 | tf_op jit(solution)/shard_map/ppermute | solution.py:8
  10.1 1.4 %fusion.80 = (s32[1]{0:T(128)}, s32[1]{0:T(128)}) fusion(s32[64]{0:T(128)} %param.5, s32[]{:T(128)S(6)} %max.3, s32[]{:T(128)S(6)} %select_n.70), kind=kLoop, calls=%fused_computation.547 | loop fusion | bytes 24 | tf_op jit(solution)/shard_map/dynamic_slice | solution.py:65
  12.7 0.7 convert_reduce_fusion
  13.4 1.0 broadcast_select_fusion
  18.6 2.1 %copy-done = bf16[1,3,3,1152,384]{4,3,2,1,0:T(8,128)(2,1)S(1)} copy-done((bf16[1,3,3,1152,384]{4,3,2,1,0:T(8,128)(2,1)S(1)}, bf16[1,3,3,1152,384]{4,3,2,1,0:T(8,128)(2,1)}, u32[]{:S(2)}) %copy-start) | copy-done | bytes 7962648
  20.6 1.5 %fusion = bf16[8,2,8,384]{3,2,1,0:T(8,128)(2,1)S(1)} fusion(bf16[8,2,8,10368]{3,2,1,0:T(8,128)(2,1)S(1)} %constant_dynamic-update-slice_fusion, bf16[10368,384,1,1]{1,0,3,2:T(8,128)(2,1)S(1)} %bitcast.47, pred[8]{0:T(512)(128)(4,1)S(1)} %iota_compare_fusion.1), kind=kOutput, calls=%fused_computation.197 | convolution fusion | flops 1019314176 | bytes 10715144 | tf_op jit(solution)/shard_map/dot_general | solution.py:30
  22.2 1.3 %collective-permute-start.4 = (bf16[8,2,8,384]{3,2,1,0:T(8,128)(2,1)S(1)}, bf16[8,2,8,384]{3,2,1,0:T(8,128)(2,1)S(1)}, u32[]{:S(2)}, u32[]{:S(2)}) collective-permute-start(bf16[8,2,8,384]{3,2,1,0:T(8,128)(2,1)S(1)} %fusion), channel_id=1, source_target_pairs={{0,64},{1,65},{2,66},{3,67},{4,68},{5,69},{6,70},{7,71},{8,72},{9,... | collective-permute-start | bytes 294920 | tf_op jit(solution)/shard_map/ppermute | solution.py:8
  23.5 1.3 %collective-permute-start.2 = (bf16[8,2,1,384]{3,2,1,0:T(2,128)(2,1)S(1)}, bf16[8,2,1,384]{3,2,1,0:T(2,128)(2,1)S(1)}, u32[]{:S(2)}, u32[]{:S(2)}) collective-permute-start(bf16[8,2,1,384]{3,2,1,0:T(2,128)(2,1)S(1)} %get-tuple-element.17), channel_id=1, source_target_pairs={{1,64},{2,65},{3,66},{4,67},{5,68},{6,69},{7,70},{8,71},{9,72},{10... | collective-permute-start | bytes 36872 | tf_op jit(solution)/shard_map/ppermute | solution.py:8
  24.8 1.3 %collective-permute-start.3 = (bf16[8,2,1,384]{3,2,1,0:T(2,128)(2,1)S(1)}, bf16[8,2,1,384]{3,2,1,0:T(2,128)(2,1)S(1)}, u32[]{:S(2)}, u32[]{:S(2)}) collective-permute-start(bf16[8,2,1,384]{3,2,1,0:T(2,128)(2,1)S(1)} %get-tuple-element.18), channel_id=1, source_target_pairs={{0,65},{1,66},{2,67},{3,68},{4,69},{5,70},{6,71},{7,72},{8,73},{9,... | collective-permute-start | bytes 36872 | tf_op jit(solution)/shard_map/ppermute | solution.py:8
  26.4 1.3 %collective-permute-done.3 = bf16[8,2,1,384]{3,2,1,0:T(2,128)(2,1)S(1)} collective-permute-done((bf16[8,2,1,384]{3,2,1,0:T(2,128)(2,1)S(1)}, bf16[8,2,1,384]{3,2,1,0:T(2,128)(2,1)S(1)}, u32[]{:S(2)}, u32[]{:S(2)}) %collective-permute-start.3) | collective-permute-done | bytes 12320 | tf_op jit(solution)/shard_map/ppermute | solution.py:8
  29.3 1.5 %fusion.5 = bf16[8,2,8,384]{3,2,1,0:T(8,128)(2,1)S(1)} fusion(bf16[8,2,8,10368]{3,2,1,0:T(8,128)(2,1)S(1)} %constant_dynamic-update-slice_fusion.27, bf16[10368,384,1,1]{1,0,3,2:T(8,128)(2,1)S(1)} %bitcast.48, pred[8]{0:T(512)(128)(4,1)S(1)} %iota_compare_fusion.1, bf16[8,2,8,384]{3,2,1,0:T(8,128)(2,1)S(1)} %copy-done.1), kind=kOutput, calls=%fused_computation.202 | convolution fusion | flops 1019461632 | bytes 10813448 | tf_op jit(solution)/shard_map/dot_general | solution.py:30
  30.8 0.7 collective-permute-start.8
  32.2 0.7 collective-permute-start.7
  34.4 1.5 %fusion.2 = bf16[8,2,8,384]{3,2,1,0:T(8,128)(2,1)S(1)} fusion(bf16[8,2,8,10368]{3,2,1,0:T(8,128)(2,1)S(1)} %constant_dynamic-update-slice_fusion.54, bf16[10368,384,1,1]{1,0,3,2:T(8,128)(2,1)S(1)} %bitcast.49, pred[8]{0:T(512)(128)(4,1)S(1)} %iota_compare_fusion.1), kind=kOutput, calls=%fused_computation.199 | convolution fusion | flops 1019314176 | bytes 10715144 | tf_op jit(solution)/shard_map/dot_general | solution.py:30
  35.9 0.7 collective-permute-start.11
  36.6 0.7 collective-permute-start.9
  38.0 0.8 collective-permute-start.5
  40.3 1.5 %fusion.70 = bf16[8,2,8,384]{3,2,1,0:T(8,128)(2,1)S(1)} fusion(bf16[8,2,8,384]{3,2,1,0:T(8,128)(2,1)S(1)} %collective-permute-done.5, pred[8]{0:T(512)(128)(4,1)S(1)} %iota_compare_fusion.1, bf16[8,2,8,10368]{3,2,1,0:T(8,128)(2,1)S(1)} %constant_dynamic-update-slice_fusion.81, bf16[10368,384,1,1]{1,0,3,2:T(8,128)(2,1)S(1)} %bitcast.50), kind=kOutput, calls=%fused_computation.510 | convolution fusion | flops 1019412480 | bytes 10813448 | tf_op jit(solution)/shard_map/dot_general | solution.py:30
  41.9 0.7 collective-permute-start.15
  45.4 1.5 %fusion.3 = bf16[8,2,8,384]{3,2,1,0:T(8,128)(2,1)S(1)} fusion(bf16[8,2,8,10368]{3,2,1,0:T(8,128)(2,1)S(1)} %constant_dynamic-update-slice_fusion.108, bf16[10368,384,1,1]{1,0,3,2:T(8,128)(2,1)S(1)} %bitcast.51, pred[8]{0:T(512)(128)(4,1)S(1)} %iota_compare_fusion.1), kind=kOutput, calls=%fused_computation.200 | convolution fusion | flops 1019314176 | bytes 10715144 | tf_op jit(solution)/shard_map/dot_general | solution.py:30
  46.9 0.7 collective-permute-start.18
  49.0 0.7 collective-permute-start.12
  51.2 1.5 %fusion.71 = bf16[8,2,8,384]{3,2,1,0:T(8,128)(2,1)S(1)} fusion(bf16[8,2,8,384]{3,2,1,0:T(8,128)(2,1)S(1)} %collective-permute-done.12, pred[8]{0:T(512)(128)(4,1)S(1)} %iota_compare_fusion.1, bf16[8,2,8,10368]{3,2,1,0:T(8,128)(2,1)S(1)} %constant_dynamic-update-slice_fusion.135, bf16[10368,384,1,1]{1,0,3,2:T(8,128)(2,1)S(1)} %bitcast.52), kind=kOutput, calls=%fused_computation.511 | convolution fusion | flops 1019412480 | bytes 10813448 | tf_op jit(solution)/shard_map/dot_general | solution.py:30
  52.7 0.7 collective-permute-start.22
  54.1 0.9 collective-permute-start.21
  56.5 1.5 %fusion.4 = bf16[8,2,8,384]{3,2,1,0:T(8,128)(2,1)S(1)} fusion(bf16[8,2,8,10368]{3,2,1,0:T(8,128)(2,1)S(1)} %constant_dynamic-update-slice_fusion.162, bf16[10368,384,1,1]{1,0,3,2:T(8,128)(2,1)S(1)} %bitcast.53, pred[8]{0:T(512)(128)(4,1)S(1)} %iota_compare_fusion.1), kind=kOutput, calls=%fused_computation.201 | convolution fusion | flops 1019314176 | bytes 10715144 | tf_op jit(solution)/shard_map/dot_general | solution.py:30
  58.0 0.7 collective-permute-start.25
  60.1 0.7 collective-permute-start.19
  62.2 1.5 %fusion.72 = bf16[8,2,8,384]{3,2,1,0:T(8,128)(2,1)S(1)} fusion(bf16[8,2,8,384]{3,2,1,0:T(8,128)(2,1)S(1)} %collective-permute-done.19, pred[8]{0:T(512)(128)(4,1)S(1)} %iota_compare_fusion.1, bf16[8,2,8,10368]{3,2,1,0:T(8,128)(2,1)S(1)} %constant_dynamic-update-slice_fusion.189, bf16[10368,384,1,1]{1,0,3,2:T(8,128)(2,1)S(1)} %bitcast.54), kind=kOutput, calls=%fused_computation.512 | convolution fusion | flops 1019412480 | bytes 10813448 | tf_op jit(solution)/shard_map/dot_general | solution.py:30
  63.8 43.2 %all_to_all.5 = bf16[8,2,8,384]{3,2,1,0:T(8,128)(2,1)S(1)} all-to-all(bf16[8,2,8,384]{3,2,1,0:T(8,128)(2,1)S(1)} %fusion.72), channel_id=1, replica_groups=mesh['section'=8,'tile'=64] {'section'}, dimensions={0} | all-to-all | bytes 196608 | tf_op jit(solution)/shard_map/all_to_all | solution.py:89
  (305 shorter events, 18.6 us)
Async XLA Ops:
  0.0 17.1 %collective-permute-start.1 = (bf16[8,2,8,384]{3,2,1,0:T(8,128)(2,1)}, bf16[8,2,8,384]{3,2,1,0:T(8,128)(2,1)S(1)}, u32[]{:S(2)}, u32[]{:S(2)}) collective-permute-start(bf16[8,2,8,384]{3,2,1,0:T(8,128)(2,1)} %param.4), channel_id=1, source_target_pairs={{0,1},{1,2},{2,3},{3,4},{4,5},{5,6},{6,7},{7,8},{8,9},{9,10},{10,1... | collective-permute-start | bytes 294920 | tf_op jit(solution)/shard_map/ppermute | solution.py:8
  4.4 12.6 %collective-permute-start = (bf16[8,2,1,384]{3,0,2,1:T(8,128)(2,1)S(1)}, bf16[8,2,1,384]{3,0,2,1:T(8,128)(2,1)S(1)}, u32[]{:S(2)}, u32[]{:S(2)}) collective-permute-start(bf16[8,2,1,384]{3,0,2,1:T(8,128)(2,1)S(1)} %copy.22), channel_id=1, source_target_pairs={{1,0},{2,1},{3,2},{4,3},{5,4},{6,5},{7,6},{8,7},{9,8},{10,9},{11,1... | collective-permute-start | bytes 36872 | tf_op jit(solution)/shard_map/ppermute | solution.py:8
  17.4 3.3 %copy-start = (bf16[1,3,3,1152,384]{4,3,2,1,0:T(8,128)(2,1)S(1)}, bf16[1,3,3,1152,384]{4,3,2,1,0:T(8,128)(2,1)}, u32[]{:S(2)}) copy-start(bf16[1,3,3,1152,384]{4,3,2,1,0:T(8,128)(2,1)} %param.6) | copy-start | bytes 23887876
  22.2 5.5 %collective-permute-start.4 = (bf16[8,2,8,384]{3,2,1,0:T(8,128)(2,1)S(1)}, bf16[8,2,8,384]{3,2,1,0:T(8,128)(2,1)S(1)}, u32[]{:S(2)}, u32[]{:S(2)}) collective-permute-start(bf16[8,2,8,384]{3,2,1,0:T(8,128)(2,1)S(1)} %fusion), channel_id=1, source_target_pairs={{0,64},{1,65},{2,66},{3,67},{4,68},{5,69},{6,70},{7,71},{8,72},{9,... | collective-permute-start | bytes 294920 | tf_op jit(solution)/shard_map/ppermute | solution.py:8
  23.5 2.8 %collective-permute-start.2 = (bf16[8,2,1,384]{3,2,1,0:T(2,128)(2,1)S(1)}, bf16[8,2,1,384]{3,2,1,0:T(2,128)(2,1)S(1)}, u32[]{:S(2)}, u32[]{:S(2)}) collective-permute-start(bf16[8,2,1,384]{3,2,1,0:T(2,128)(2,1)S(1)} %get-tuple-element.17), channel_id=1, source_target_pairs={{1,64},{2,65},{3,66},{4,67},{5,68},{6,69},{7,70},{8,71},{9,72},{10... | collective-permute-start | bytes 36872 | tf_op jit(solution)/shard_map/ppermute | solution.py:8
  24.8 2.8 %collective-permute-start.3 = (bf16[8,2,1,384]{3,2,1,0:T(2,128)(2,1)S(1)}, bf16[8,2,1,384]{3,2,1,0:T(2,128)(2,1)S(1)}, u32[]{:S(2)}, u32[]{:S(2)}) collective-permute-start(bf16[8,2,1,384]{3,2,1,0:T(2,128)(2,1)S(1)} %get-tuple-element.18), channel_id=1, source_target_pairs={{0,65},{1,66},{2,67},{3,68},{4,69},{5,70},{6,71},{7,72},{8,73},{9,... | collective-permute-start | bytes 36872 | tf_op jit(solution)/shard_map/ppermute | solution.py:8
  28.4 0.9 copy-start.1
  30.8 2.1 %collective-permute-start.8 = (bf16[8,2,8,384]{3,2,1,0:T(8,128)(2,1)S(1)}, bf16[8,2,8,384]{3,2,1,0:T(8,128)(2,1)S(1)}, u32[]{:S(2)}, u32[]{:S(2)}) collective-permute-start(bf16[8,2,8,384]{3,2,1,0:T(8,128)(2,1)S(1)} %fusion.5), channel_id=1, source_target_pairs={{64,128},{65,129},{66,130},{67,131},{68,132},{69,133},{70,134},{71... | collective-permute-start | bytes 294920 | tf_op jit(solution)/shard_map/ppermute | solution.py:8
  31.6 1.3 %collective-permute-start.6 = (bf16[8,2,1,384]{3,2,1,0:T(2,128)(2,1)S(1)}, bf16[8,2,1,384]{3,2,1,0:T(2,128)(2,1)S(1)}, u32[]{:S(2)}, u32[]{:S(2)}) collective-permute-start(bf16[8,2,1,384]{3,2,1,0:T(2,128)(2,1)S(1)} %get-tuple-element.15), channel_id=1, source_target_pairs={{65,128},{66,129},{67,130},{68,131},{69,132},{70,133},{71,134},{72... | collective-permute-start | bytes 36872 | tf_op jit(solution)/shard_map/ppermute | solution.py:8
  32.2 0.7 collective-permute-start.7
  35.9 3.0 %collective-permute-start.11 = (bf16[8,2,8,384]{3,2,1,0:T(8,128)(2,1)S(1)}, bf16[8,2,8,384]{3,2,1,0:T(8,128)(2,1)S(1)}, u32[]{:S(2)}, u32[]{:S(2)}) collective-permute-start(bf16[8,2,8,384]{3,2,1,0:T(8,128)(2,1)S(1)} %fusion.2), channel_id=1, source_target_pairs={{128,192},{129,193},{130,194},{131,195},{132,196},{133,197},{134,1... | collective-permute-start | bytes 294920 | tf_op jit(solution)/shard_map/ppermute | solution.py:8
  36.6 2.2 %collective-permute-start.9 = (bf16[8,2,1,384]{3,2,1,0:T(2,128)(2,1)S(1)}, bf16[8,2,1,384]{3,2,1,0:T(2,128)(2,1)S(1)}, u32[]{:S(2)}, u32[]{:S(2)}) collective-permute-start(bf16[8,2,1,384]{3,2,1,0:T(2,128)(2,1)S(1)} %get-tuple-element.13), channel_id=1, source_target_pairs={{129,192},{130,193},{131,194},{132,195},{133,196},{134,197},{135,1... | collective-permute-start | bytes 36872 | tf_op jit(solution)/shard_map/ppermute | solution.py:8
  37.3 1.6 %collective-permute-start.10 = (bf16[8,2,1,384]{3,2,1,0:T(2,128)(2,1)S(1)}, bf16[8,2,1,384]{3,2,1,0:T(2,128)(2,1)S(1)}, u32[]{:S(2)}, u32[]{:S(2)}) collective-permute-start(bf16[8,2,1,384]{3,2,1,0:T(2,128)(2,1)S(1)} %get-tuple-element.14), channel_id=1, source_target_pairs={{128,193},{129,194},{130,195},{131,196},{132,197},{133,198},{134,1... | collective-permute-start | bytes 36872 | tf_op jit(solution)/shard_map/ppermute | solution.py:8
  38.0 2.3 %collective-permute-start.5 = (bf16[8,2,8,384]{3,2,1,0:T(8,128)(2,1)S(1)}, bf16[8,2,8,384]{3,2,1,0:T(8,128)(2,1)S(1)}, u32[]{:S(2)}, u32[]{:S(2)}) collective-permute-start(bf16[8,2,8,384]{3,2,1,0:T(8,128)(2,1)S(1)} %fusion.5), channel_id=1, source_target_pairs={{64,192},{65,193},{66,194},{67,195},{68,196},{69,197},{70,198},{71... | collective-permute-start | bytes 294920 | tf_op jit(solution)/shard_map/ppermute | solution.py:8
  41.9 2.1 %collective-permute-start.15 = (bf16[8,2,8,384]{3,2,1,0:T(8,128)(2,1)S(1)}, bf16[8,2,8,384]{3,2,1,0:T(8,128)(2,1)S(1)}, u32[]{:S(2)}, u32[]{:S(2)}) collective-permute-start(bf16[8,2,8,384]{3,2,1,0:T(8,128)(2,1)S(1)} %fusion.70), channel_id=1, source_target_pairs={{192,256},{193,257},{194,258},{195,259},{196,260},{197,261},{198,2... | collective-permute-start | bytes 294920 | tf_op jit(solution)/shard_map/ppermute | solution.py:8
  42.6 1.3 %collective-permute-start.13 = (bf16[8,2,1,384]{3,2,1,0:T(2,128)(2,1)S(1)}, bf16[8,2,1,384]{3,2,1,0:T(2,128)(2,1)S(1)}, u32[]{:S(2)}, u32[]{:S(2)}) collective-permute-start(bf16[8,2,1,384]{3,2,1,0:T(2,128)(2,1)S(1)} %get-tuple-element.11), channel_id=1, source_target_pairs={{193,256},{194,257},{195,258},{196,259},{197,260},{198,261},{199,2... | collective-permute-start | bytes 36872 | tf_op jit(solution)/shard_map/ppermute | solution.py:8
  43.3 0.7 collective-permute-start.14
  46.9 2.8 %collective-permute-start.18 = (bf16[8,2,8,384]{3,2,1,0:T(8,128)(2,1)S(1)}, bf16[8,2,8,384]{3,2,1,0:T(8,128)(2,1)S(1)}, u32[]{:S(2)}, u32[]{:S(2)}) collective-permute-start(bf16[8,2,8,384]{3,2,1,0:T(8,128)(2,1)S(1)} %fusion.3), channel_id=1, source_target_pairs={{256,320},{257,321},{258,322},{259,323},{260,324},{261,325},{262,3... | collective-permute-start | bytes 294920 | tf_op jit(solution)/shard_map/ppermute | solution.py:8
  47.7 2.0 %collective-permute-start.16 = (bf16[8,2,1,384]{3,2,1,0:T(2,128)(2,1)S(1)}, bf16[8,2,1,384]{3,2,1,0:T(2,128)(2,1)S(1)}, u32[]{:S(2)}, u32[]{:S(2)}) collective-permute-start(bf16[8,2,1,384]{3,2,1,0:T(2,128)(2,1)S(1)} %get-tuple-element.9), channel_id=1, source_target_pairs={{257,320},{258,321},{259,322},{260,323},{261,324},{262,325},{263,3... | collective-permute-start | bytes 36872 | tf_op jit(solution)/shard_map/ppermute | solution.py:8
  48.3 1.4 %collective-permute-start.17 = (bf16[8,2,1,384]{3,2,1,0:T(2,128)(2,1)S(1)}, bf16[8,2,1,384]{3,2,1,0:T(2,128)(2,1)S(1)}, u32[]{:S(2)}, u32[]{:S(2)}) collective-permute-start(bf16[8,2,1,384]{3,2,1,0:T(2,128)(2,1)S(1)} %get-tuple-element.10), channel_id=1, source_target_pairs={{256,321},{257,322},{258,323},{259,324},{260,325},{261,326},{262,3... | collective-permute-start | bytes 36872 | tf_op jit(solution)/shard_map/ppermute | solution.py:8
  49.0 2.1 %collective-permute-start.12 = (bf16[8,2,8,384]{3,2,1,0:T(8,128)(2,1)S(1)}, bf16[8,2,8,384]{3,2,1,0:T(8,128)(2,1)S(1)}, u32[]{:S(2)}, u32[]{:S(2)}) collective-permute-start(bf16[8,2,8,384]{3,2,1,0:T(8,128)(2,1)S(1)} %fusion.70), channel_id=1, source_target_pairs={{192,320},{193,321},{194,322},{195,323},{196,324},{197,325},{198,3... | collective-permute-start | bytes 294920 | tf_op jit(solution)/shard_map/ppermute | solution.py:8
  52.7 2.3 %collective-permute-start.22 = (bf16[8,2,8,384]{3,2,1,0:T(8,128)(2,1)S(1)}, bf16[8,2,8,384]{3,2,1,0:T(8,128)(2,1)S(1)}, u32[]{:S(2)}, u32[]{:S(2)}) collective-permute-start(bf16[8,2,8,384]{3,2,1,0:T(8,128)(2,1)S(1)} %fusion.71), channel_id=1, source_target_pairs={{320,384},{321,385},{322,386},{323,387},{324,388},{325,389},{326,3... | collective-permute-start | bytes 294920 | tf_op jit(solution)/shard_map/ppermute | solution.py:8
  53.4 1.6 %collective-permute-start.20 = (bf16[8,2,1,384]{3,2,1,0:T(2,128)(2,1)S(1)}, bf16[8,2,1,384]{3,2,1,0:T(2,128)(2,1)S(1)}, u32[]{:S(2)}, u32[]{:S(2)}) collective-permute-start(bf16[8,2,1,384]{3,2,1,0:T(2,128)(2,1)S(1)} %get-tuple-element.7), channel_id=1, source_target_pairs={{321,384},{322,385},{323,386},{324,387},{325,388},{326,389},{327,3... | collective-permute-start | bytes 36872 | tf_op jit(solution)/shard_map/ppermute | solution.py:8
  54.1 0.9 collective-permute-start.21
  58.0 2.8 %collective-permute-start.25 = (bf16[8,2,8,384]{3,2,1,0:T(8,128)(2,1)S(1)}, bf16[8,2,8,384]{3,2,1,0:T(8,128)(2,1)S(1)}, u32[]{:S(2)}, u32[]{:S(2)}) collective-permute-start(bf16[8,2,8,384]{3,2,1,0:T(8,128)(2,1)S(1)} %fusion.4), channel_id=1, source_target_pairs={{384,448},{385,449},{386,450},{387,451},{388,452},{389,453},{390,4... | collective-permute-start | bytes 294920 | tf_op jit(solution)/shard_map/ppermute | solution.py:8
  58.7 2.0 %collective-permute-start.23 = (bf16[8,2,1,384]{3,2,1,0:T(2,128)(2,1)S(1)}, bf16[8,2,1,384]{3,2,1,0:T(2,128)(2,1)S(1)}, u32[]{:S(2)}, u32[]{:S(2)}) collective-permute-start(bf16[8,2,1,384]{3,2,1,0:T(2,128)(2,1)S(1)} %get-tuple-element.5), channel_id=1, source_target_pairs={{385,448},{386,449},{387,450},{388,451},{389,452},{390,453},{391,4... | collective-permute-start | bytes 36872 | tf_op jit(solution)/shard_map/ppermute | solution.py:8
  59.4 1.4 %collective-permute-start.24 = (bf16[8,2,1,384]{3,2,1,0:T(2,128)(2,1)S(1)}, bf16[8,2,1,384]{3,2,1,0:T(2,128)(2,1)S(1)}, u32[]{:S(2)}, u32[]{:S(2)}) collective-permute-start(bf16[8,2,1,384]{3,2,1,0:T(2,128)(2,1)S(1)} %get-tuple-element.6), channel_id=1, source_target_pairs={{384,449},{385,450},{386,451},{387,452},{388,453},{389,454},{390,4... | collective-permute-start | bytes 36872 | tf_op jit(solution)/shard_map/ppermute | solution.py:8
  60.1 2.1 %collective-permute-start.19 = (bf16[8,2,8,384]{3,2,1,0:T(8,128)(2,1)S(1)}, bf16[8,2,8,384]{3,2,1,0:T(8,128)(2,1)S(1)}, u32[]{:S(2)}, u32[]{:S(2)}) collective-permute-start(bf16[8,2,8,384]{3,2,1,0:T(8,128)(2,1)S(1)} %fusion.71), channel_id=1, source_target_pairs={{320,448},{321,449},{322,450},{323,451},{324,452},{325,453},{326,4... | collective-permute-start | bytes 294920 | tf_op jit(solution)/shard_map/ppermute | solution.py:8

commit v4 on v3

--- a/solution.py
+++ b/solution.py
@@ -18,13 +18,13 @@
     frames, rows, cols_ext, channels = activated.shape
     cols = cols_ext - 2
     padded = jnp.pad(activated, ((2, 0), (1, 1), (0, 0), (0, 0)))
-    taps = []
-    for frame_tap in range(3):
-        for row_tap in range(3):
-            for col_tap in range(3):
-                taps.append(
-                    padded[frame_tap : frame_tap + frames, row_tap : row_tap + rows, col_tap : col_tap + cols]
-                )
+    shifted = jnp.concatenate([padded[:, :, k : k + cols] for k in range(3)], axis=-1)
+    shifted = lax.optimization_barrier(shifted)
+    taps = [
+        shifted[frame_tap : frame_tap + frames, row_tap : row_tap + rows]
+        for frame_tap in range(3)
+        for row_tap in range(3)
+    ]
     joined = jnp.concatenate(taps, axis=-1).reshape(frames * rows * cols, 27 * channels)
     flat = kernel.reshape(27 * channels, kernel.shape[-1])
     out = jnp.dot(joined, flat, preferred_element_type=jnp.float32)

time: 108 us -> 106 us (0.981)
  local copies, waits for them, and re-layouts: 12.2 us -> 9.42 us
    unnamed x213 -> x69, local copies, waits for them, and re-layouts: 8.52 us -> 5.04 us
  transfers between devices with their start and end apart: 26 -> 26, of which waited for: 2 -> 2; matrix products, arithmetic and copies ran while one was open for 8% -> 10% of each run, Pallas kernels for 0% -> 0%
where the time goes in v4:
time: 106 us; the launch traced here: 105 us
  blocking collectives  43.5 us (41%)
  starting transfers between devices  27.2 us (26%)
  matrix products  12.2 us (12%)
  local copies, waits for them, and re-layouts  9.42 us (9%)
  other arithmetic  6.83 us (6%)
  between operations  4.32 us (4%)
  waiting for transfers between devices  1.54 us (1%)
    all_to_all x1, blocking collectives, local(): spread = lax.all_to_all(final, 'section', 0, 0, tiled=True)  43.5 us
    ppermute x26, starting transfers between devices, hop(): return lax.ppermute(block, axes, pairs)  27.2 us
    dot_general x8, matrix products, convolve(): out = jnp.dot(joined, flat, preferred_element_type=jnp.float32)  12.2 us
    unnamed x69, local copies, waits for them, and re-layouts  5.04 us
  transfers between devices with their start and end apart: 26, of which 2 were waited for; matrix products, arithmetic and copies ran while one was open for 10% of the time, Pallas kernels for 0%

profile of v4, /device:TPU:256, one launch (start us, length us, event | category | flops | bytes accessed | tf_op | source)
XLA Modules:
  0.0 105.0 jit_solution(2288678379299430604)
XLA Ops:
  0.0 3.5 %collective-permute-start.1 = (bf16[8,2,8,384]{3,2,1,0:T(8,128)(2,1)}, bf16[8,2,8,384]{3,2,1,0:T(8,128)(2,1)S(1)}, u32[]{:S(2)}, u32[]{:S(2)}) collective-permute-start(bf16[8,2,8,384]{3,2,1,0:T(8,128)(2,1)} %param.4), channel_id=1, source_target_pairs={{0,1},{1,2},{2,3},{3,4},{4,5},{5,6},{6,7},{7,8},{8,9},{9,10},{10,1... | collective-permute-start | bytes 294920 | tf_op jit(solution)/shard_map/ppermute | solution.py:8
  3.5 0.9 slice.315
  4.4 5.7 %collective-permute-start = (bf16[8,2,1,384]{3,0,2,1:T(8,128)(2,1)S(1)}, bf16[8,2,1,384]{3,0,2,1:T(8,128)(2,1)S(1)}, u32[]{:S(2)}, u32[]{:S(2)}) collective-permute-start(bf16[8,2,1,384]{3,0,2,1:T(8,128)(2,1)S(1)} %copy.22), channel_id=1, source_target_pairs={{1,0},{2,1},{3,2},{4,3},{5,4},{6,5},{7,6},{8,7},{9,8},{10,9},{11,1... | collective-permute-start | bytes 36872 | tf_op jit(solution)/shard_map/ppermute | solution.py:8
  10.1 1.3 %fusion.80 = (s32[1]{0:T(128)}, s32[1]{0:T(128)}) fusion(s32[64]{0:T(128)} %param.5, s32[]{:T(128)S(6)} %max.3, s32[]{:T(128)S(6)} %select_n.70), kind=kLoop, calls=%fused_computation.243 | loop fusion | bytes 24 | tf_op jit(solution)/shard_map/dynamic_slice | solution.py:65
  12.5 0.7 convert_reduce_fusion
  13.2 1.0 broadcast_select_fusion
  17.8 2.5 %copy-done = bf16[1,3,3,1152,384]{4,3,2,1,0:T(8,128)(2,1)S(1)} copy-done((bf16[1,3,3,1152,384]{4,3,2,1,0:T(8,128)(2,1)S(1)}, bf16[1,3,3,1152,384]{4,3,2,1,0:T(8,128)(2,1)}, u32[]{:S(2)}) %copy-start) | copy-done | bytes 7962648
  20.3 1.5 %fusion = bf16[8,2,8,384]{3,2,1,0:T(8,128)(2,1)S(1)} fusion(bf16[8,2,8,10368]{3,2,1,0:T(8,128)(2,1)S(1)} %slice_dynamic-update-slice_fusion.63, bf16[10368,384,1,1]{1,0,3,2:T(8,128)(2,1)S(1)} %bitcast.47, pred[8]{0:T(512)(128)(4,1)S(1)} %iota_compare_fusion.1), kind=kOutput, calls=%fused_computation.5 | convolution fusion | flops 1019314176 | bytes 10715144 | tf_op jit(solution)/shard_map/dot_general | solution.py:30
  21.8 1.3 %collective-permute-start.4 = (bf16[8,2,8,384]{3,2,1,0:T(8,128)(2,1)S(1)}, bf16[8,2,8,384]{3,2,1,0:T(8,128)(2,1)S(1)}, u32[]{:S(2)}, u32[]{:S(2)}) collective-permute-start(bf16[8,2,8,384]{3,2,1,0:T(8,128)(2,1)S(1)} %fusion), channel_id=1, source_target_pairs={{0,64},{1,65},{2,66},{3,67},{4,68},{5,69},{6,70},{7,71},{8,72},{9,... | collective-permute-start | bytes 294920 | tf_op jit(solution)/shard_map/ppermute | solution.py:8
  23.2 1.3 %collective-permute-start.2 = (bf16[8,2,1,384]{3,2,1,0:T(2,128)(2,1)S(1)}, bf16[8,2,1,384]{3,2,1,0:T(2,128)(2,1)S(1)}, u32[]{:S(2)}, u32[]{:S(2)}) collective-permute-start(bf16[8,2,1,384]{3,2,1,0:T(2,128)(2,1)S(1)} %get-tuple-element.41), channel_id=1, source_target_pairs={{1,64},{2,65},{3,66},{4,67},{5,68},{6,69},{7,70},{8,71},{9,72},{10... | collective-permute-start | bytes 36872 | tf_op jit(solution)/shard_map/ppermute | solution.py:8
  24.5 1.3 %collective-permute-start.3 = (bf16[8,2,1,384]{3,2,1,0:T(2,128)(2,1)S(1)}, bf16[8,2,1,384]{3,2,1,0:T(2,128)(2,1)S(1)}, u32[]{:S(2)}, u32[]{:S(2)}) collective-permute-start(bf16[8,2,1,384]{3,2,1,0:T(2,128)(2,1)S(1)} %get-tuple-element.42), channel_id=1, source_target_pairs={{0,65},{1,66},{2,67},{3,68},{4,69},{5,70},{6,71},{7,72},{8,73},{9,... | collective-permute-start | bytes 36872 | tf_op jit(solution)/shard_map/ppermute | solution.py:8
  26.0 1.3 %collective-permute-done.3 = bf16[8,2,1,384]{3,2,1,0:T(2,128)(2,1)S(1)} collective-permute-done((bf16[8,2,1,384]{3,2,1,0:T(2,128)(2,1)S(1)}, bf16[8,2,1,384]{3,2,1,0:T(2,128)(2,1)S(1)}, u32[]{:S(2)}, u32[]{:S(2)}) %collective-permute-start.3) | collective-permute-done | bytes 12320 | tf_op jit(solution)/shard_map/ppermute | solution.py:8
  28.8 1.5 %fusion.5 = bf16[8,2,8,384]{3,2,1,0:T(8,128)(2,1)S(1)} fusion(bf16[8,2,8,10368]{3,2,1,0:T(8,128)(2,1)S(1)} %slice_dynamic-update-slice_fusion.54, bf16[10368,384,1,1]{1,0,3,2:T(8,128)(2,1)S(1)} %bitcast.48, pred[8]{0:T(512)(128)(4,1)S(1)} %iota_compare_fusion.1, bf16[8,2,8,384]{3,2,1,0:T(8,128)(2,1)S(1)} %copy-done.1), kind=kOutput, calls=%fused_computation.10 | convolution fusion | flops 1019461632 | bytes 10813448 | tf_op jit(solution)/shard_map/dot_general | solution.py:30
  30.4 0.7 collective-permute-start.8
  31.1 0.7 collective-permute-start.6
  33.5 1.5 %fusion.2 = bf16[8,2,8,384]{3,2,1,0:T(8,128)(2,1)S(1)} fusion(bf16[8,2,8,10368]{3,2,1,0:T(8,128)(2,1)S(1)} %slice_dynamic-update-slice_fusion.45, bf16[10368,384,1,1]{1,0,3,2:T(8,128)(2,1)S(1)} %bitcast.49, pred[8]{0:T(512)(128)(4,1)S(1)} %iota_compare_fusion.1), kind=kOutput, calls=%fused_computation.7 | convolution fusion | flops 1019314176 | bytes 10715144 | tf_op jit(solution)/shard_map/dot_general | solution.py:30
  35.1 0.7 collective-permute-start.11
  35.8 0.7 collective-permute-start.9
  37.1 0.7 collective-permute-start.5
  38.9 1.5 %fusion.70 = bf16[8,2,8,384]{3,2,1,0:T(8,128)(2,1)S(1)} fusion(bf16[8,2,8,384]{3,2,1,0:T(8,128)(2,1)S(1)} %collective-permute-done.5, pred[8]{0:T(512)(128)(4,1)S(1)} %iota_compare_fusion.1, bf16[8,2,8,10368]{3,2,1,0:T(8,128)(2,1)S(1)} %slice_dynamic-update-slice_fusion.36, bf16[10368,384,1,1]{1,0,3,2:T(8,128)(2,1)S(1)} %bitcast.50), kind=kOutput, calls=%fused_computation.206 | convolution fusion | flops 1019412480 | bytes 10813448 | tf_op jit(solution)/shard_map/dot_general | solution.py:30
  40.4 0.7 collective-permute-start.15
  41.8 0.8 collective-permute-start.14
  43.8 1.5 %fusion.3 = bf16[8,2,8,384]{3,2,1,0:T(8,128)(2,1)S(1)} fusion(bf16[8,2,8,10368]{3,2,1,0:T(8,128)(2,1)S(1)} %slice_dynamic-update-slice_fusion.27, bf16[10368,384,1,1]{1,0,3,2:T(8,128)(2,1)S(1)} %bitcast.51, pred[8]{0:T(512)(128)(4,1)S(1)} %iota_compare_fusion.1), kind=kOutput, calls=%fused_computation.8 | convolution fusion | flops 1019314176 | bytes 10715144 | tf_op jit(solution)/shard_map/dot_general | solution.py:30
  45.3 0.7 collective-permute-start.18
  47.4 0.7 collective-permute-start.12
  49.1 1.5 %fusion.81 = f32[8,2,8,384]{3,2,1,0:T(8,128)S(1)} fusion(bf16[8,2,8,10368]{3,2,1,0:T(8,128)(2,1)S(1)} %slice_dynamic-update-slice_fusion.18, bf16[10368,384,1,1]{1,0,3,2:T(8,128)(2,1)S(1)} %bitcast.52), kind=kOutput, calls=%fused_computation.244 | convolution fusion | flops 1019215872 | bytes 10813440 | tf_op jit(solution)/shard_map/dot_general | solution.py:30
  50.8 0.7 collective-permute-start.22
  53.9 1.5 %fusion.4 = bf16[8,2,8,384]{3,2,1,0:T(8,128)(2,1)S(1)} fusion(bf16[8,2,8,10368]{3,2,1,0:T(8,128)(2,1)S(1)} %slice_dynamic-update-slice_fusion.9, bf16[10368,384,1,1]{1,0,3,2:T(8,128)(2,1)S(1)} %bitcast.53, pred[8]{0:T(512)(128)(4,1)S(1)} %iota_compare_fusion.1), kind=kOutput, calls=%fused_computation.9 | convolution fusion | flops 1019314176 | bytes 10715144 | tf_op jit(solution)/shard_map/dot_general | solution.py:30
  55.5 0.7 collective-permute-start.25
  57.5 0.7 collective-permute-start.19
  59.3 1.5 %fusion.82 = f32[8,2,8,384]{3,2,1,0:T(8,128)S(1)} fusion(bf16[8,2,8,10368]{3,2,1,0:T(8,128)(2,1)S(1)} %slice_dynamic-update-slice_fusion, bf16[10368,384,1,1]{1,0,3,2:T(8,128)(2,1)S(1)} %bitcast.54), kind=kOutput, calls=%fused_computation.245 | convolution fusion | flops 1019215872 | bytes 10813440 | tf_op jit(solution)/shard_map/dot_general | solution.py:30
  60.9 43.5 %all_to_all.5 = bf16[8,2,8,384]{3,2,1,0:T(8,128)(2,1)S(1)} all-to-all(bf16[8,2,8,384]{3,2,1,0:T(8,128)(2,1)S(1)} %fusion.72), channel_id=1, replica_groups=mesh['section'=8,'tile'=64] {'section'}, dimensions={0} | all-to-all | bytes 196608 | tf_op jit(solution)/shard_map/all_to_all | solution.py:89
  (179 shorter events, 16.1 us)
Async XLA Ops:
  0.0 16.7 %collective-permute-start.1 = (bf16[8,2,8,384]{3,2,1,0:T(8,128)(2,1)}, bf16[8,2,8,384]{3,2,1,0:T(8,128)(2,1)S(1)}, u32[]{:S(2)}, u32[]{:S(2)}) collective-permute-start(bf16[8,2,8,384]{3,2,1,0:T(8,128)(2,1)} %param.4), channel_id=1, source_target_pairs={{0,1},{1,2},{2,3},{3,4},{4,5},{5,6},{6,7},{7,8},{8,9},{9,10},{10,1... | collective-permute-start | bytes 294920 | tf_op jit(solution)/shard_map/ppermute | solution.py:8
  4.4 12.3 %collective-permute-start = (bf16[8,2,1,384]{3,0,2,1:T(8,128)(2,1)S(1)}, bf16[8,2,1,384]{3,0,2,1:T(8,128)(2,1)S(1)}, u32[]{:S(2)}, u32[]{:S(2)}) collective-permute-start(bf16[8,2,1,384]{3,0,2,1:T(8,128)(2,1)S(1)} %copy.22), channel_id=1, source_target_pairs={{1,0},{2,1},{3,2},{4,3},{5,4},{6,5},{7,6},{8,7},{9,8},{10,9},{11,1... | collective-permute-start | bytes 36872 | tf_op jit(solution)/shard_map/ppermute | solution.py:8
  17.0 3.3 %copy-start = (bf16[1,3,3,1152,384]{4,3,2,1,0:T(8,128)(2,1)S(1)}, bf16[1,3,3,1152,384]{4,3,2,1,0:T(8,128)(2,1)}, u32[]{:S(2)}) copy-start(bf16[1,3,3,1152,384]{4,3,2,1,0:T(8,128)(2,1)} %param.6) | copy-start | bytes 23887876
  21.8 5.5 %collective-permute-start.4 = (bf16[8,2,8,384]{3,2,1,0:T(8,128)(2,1)S(1)}, bf16[8,2,8,384]{3,2,1,0:T(8,128)(2,1)S(1)}, u32[]{:S(2)}, u32[]{:S(2)}) collective-permute-start(bf16[8,2,8,384]{3,2,1,0:T(8,128)(2,1)S(1)} %fusion), channel_id=1, source_target_pairs={{0,64},{1,65},{2,66},{3,67},{4,68},{5,69},{6,70},{7,71},{8,72},{9,... | collective-permute-start | bytes 294920 | tf_op jit(solution)/shard_map/ppermute | solution.py:8
  23.2 2.8 %collective-permute-start.2 = (bf16[8,2,1,384]{3,2,1,0:T(2,128)(2,1)S(1)}, bf16[8,2,1,384]{3,2,1,0:T(2,128)(2,1)S(1)}, u32[]{:S(2)}, u32[]{:S(2)}) collective-permute-start(bf16[8,2,1,384]{3,2,1,0:T(2,128)(2,1)S(1)} %get-tuple-element.41), channel_id=1, source_target_pairs={{1,64},{2,65},{3,66},{4,67},{5,68},{6,69},{7,70},{8,71},{9,72},{10... | collective-permute-start | bytes 36872 | tf_op jit(solution)/shard_map/ppermute | solution.py:8
  24.5 2.8 %collective-permute-start.3 = (bf16[8,2,1,384]{3,2,1,0:T(2,128)(2,1)S(1)}, bf16[8,2,1,384]{3,2,1,0:T(2,128)(2,1)S(1)}, u32[]{:S(2)}, u32[]{:S(2)}) collective-permute-start(bf16[8,2,1,384]{3,2,1,0:T(2,128)(2,1)S(1)} %get-tuple-element.42), channel_id=1, source_target_pairs={{0,65},{1,66},{2,67},{3,68},{4,69},{5,70},{6,71},{7,72},{8,73},{9,... | collective-permute-start | bytes 36872 | tf_op jit(solution)/shard_map/ppermute | solution.py:8
  27.9 0.9 copy-start.1
  30.4 2.1 %collective-permute-start.8 = (bf16[8,2,8,384]{3,2,1,0:T(8,128)(2,1)S(1)}, bf16[8,2,8,384]{3,2,1,0:T(8,128)(2,1)S(1)}, u32[]{:S(2)}, u32[]{:S(2)}) collective-permute-start(bf16[8,2,8,384]{3,2,1,0:T(8,128)(2,1)S(1)} %fusion.5), channel_id=1, source_target_pairs={{64,128},{65,129},{66,130},{67,131},{68,132},{69,133},{70,134},{71... | collective-permute-start | bytes 294920 | tf_op jit(solution)/shard_map/ppermute | solution.py:8
  31.1 1.3 %collective-permute-start.6 = (bf16[8,2,1,384]{3,2,1,0:T(2,128)(2,1)S(1)}, bf16[8,2,1,384]{3,2,1,0:T(2,128)(2,1)S(1)}, u32[]{:S(2)}, u32[]{:S(2)}) collective-permute-start(bf16[8,2,1,384]{3,2,1,0:T(2,128)(2,1)S(1)} %get-tuple-element.39), channel_id=1, source_target_pairs={{65,128},{66,129},{67,130},{68,131},{69,132},{70,133},{71,134},{72... | collective-permute-start | bytes 36872 | tf_op jit(solution)/shard_map/ppermute | solution.py:8
  31.8 0.7 collective-permute-start.7
  35.1 2.8 %collective-permute-start.11 = (bf16[8,2,8,384]{3,2,1,0:T(8,128)(2,1)S(1)}, bf16[8,2,8,384]{3,2,1,0:T(8,128)(2,1)S(1)}, u32[]{:S(2)}, u32[]{:S(2)}) collective-permute-start(bf16[8,2,8,384]{3,2,1,0:T(8,128)(2,1)S(1)} %fusion.2), channel_id=1, source_target_pairs={{128,192},{129,193},{130,194},{131,195},{132,196},{133,197},{134,1... | collective-permute-start | bytes 294920 | tf_op jit(solution)/shard_map/ppermute | solution.py:8
  35.8 2.0 %collective-permute-start.9 = (bf16[8,2,1,384]{3,2,1,0:T(2,128)(2,1)S(1)}, bf16[8,2,1,384]{3,2,1,0:T(2,128)(2,1)S(1)}, u32[]{:S(2)}, u32[]{:S(2)}) collective-permute-start(bf16[8,2,1,384]{3,2,1,0:T(2,128)(2,1)S(1)} %get-tuple-element.37), channel_id=1, source_target_pairs={{129,192},{130,193},{131,194},{132,195},{133,196},{134,197},{135,1... | collective-permute-start | bytes 36872 | tf_op jit(solution)/shard_map/ppermute | solution.py:8
  36.5 1.4 %collective-permute-start.10 = (bf16[8,2,1,384]{3,2,1,0:T(2,128)(2,1)S(1)}, bf16[8,2,1,384]{3,2,1,0:T(2,128)(2,1)S(1)}, u32[]{:S(2)}, u32[]{:S(2)}) collective-permute-start(bf16[8,2,1,384]{3,2,1,0:T(2,128)(2,1)S(1)} %get-tuple-element.38), channel_id=1, source_target_pairs={{128,193},{129,194},{130,195},{131,196},{132,197},{133,198},{134,1... | collective-permute-start | bytes 36872 | tf_op jit(solution)/shard_map/ppermute | solution.py:8
  37.1 1.8 %collective-permute-start.5 = (bf16[8,2,8,384]{3,2,1,0:T(8,128)(2,1)S(1)}, bf16[8,2,8,384]{3,2,1,0:T(8,128)(2,1)S(1)}, u32[]{:S(2)}, u32[]{:S(2)}) collective-permute-start(bf16[8,2,8,384]{3,2,1,0:T(8,128)(2,1)S(1)} %fusion.5), channel_id=1, source_target_pairs={{64,192},{65,193},{66,194},{67,195},{68,196},{69,197},{70,198},{71... | collective-permute-start | bytes 294920 | tf_op jit(solution)/shard_map/ppermute | solution.py:8
  40.4 2.3 %collective-permute-start.15 = (bf16[8,2,8,384]{3,2,1,0:T(8,128)(2,1)S(1)}, bf16[8,2,8,384]{3,2,1,0:T(8,128)(2,1)S(1)}, u32[]{:S(2)}, u32[]{:S(2)}) collective-permute-start(bf16[8,2,8,384]{3,2,1,0:T(8,128)(2,1)S(1)} %fusion.70), channel_id=1, source_target_pairs={{192,256},{193,257},{194,258},{195,259},{196,260},{197,261},{198,2... | collective-permute-start | bytes 294920 | tf_op jit(solution)/shard_map/ppermute | solution.py:8
  41.2 1.5 %collective-permute-start.13 = (bf16[8,2,1,384]{3,2,1,0:T(2,128)(2,1)S(1)}, bf16[8,2,1,384]{3,2,1,0:T(2,128)(2,1)S(1)}, u32[]{:S(2)}, u32[]{:S(2)}) collective-permute-start(bf16[8,2,1,384]{3,2,1,0:T(2,128)(2,1)S(1)} %get-tuple-element.35), channel_id=1, source_target_pairs={{193,256},{194,257},{195,258},{196,259},{197,260},{198,261},{199,2... | collective-permute-start | bytes 36872 | tf_op jit(solution)/shard_map/ppermute | solution.py:8
  41.8 0.9 collective-permute-start.14
  45.3 2.8 %collective-permute-start.18 = (bf16[8,2,8,384]{3,2,1,0:T(8,128)(2,1)S(1)}, bf16[8,2,8,384]{3,2,1,0:T(8,128)(2,1)S(1)}, u32[]{:S(2)}, u32[]{:S(2)}) collective-permute-start(bf16[8,2,8,384]{3,2,1,0:T(8,128)(2,1)S(1)} %fusion.3), channel_id=1, source_target_pairs={{256,320},{257,321},{258,322},{259,323},{260,324},{261,325},{262,3... | collective-permute-start | bytes 294920 | tf_op jit(solution)/shard_map/ppermute | solution.py:8
  46.0 2.0 %collective-permute-start.16 = (bf16[8,2,1,384]{3,2,1,0:T(2,128)(2,1)S(1)}, bf16[8,2,1,384]{3,2,1,0:T(2,128)(2,1)S(1)}, u32[]{:S(2)}, u32[]{:S(2)}) collective-permute-start(bf16[8,2,1,384]{3,2,1,0:T(2,128)(2,1)S(1)} %get-tuple-element.33), channel_id=1, source_target_pairs={{257,320},{258,321},{259,322},{260,323},{261,324},{262,325},{263,3... | collective-permute-start | bytes 36872 | tf_op jit(solution)/shard_map/ppermute | solution.py:8
  46.7 1.4 %collective-permute-start.17 = (bf16[8,2,1,384]{3,2,1,0:T(2,128)(2,1)S(1)}, bf16[8,2,1,384]{3,2,1,0:T(2,128)(2,1)S(1)}, u32[]{:S(2)}, u32[]{:S(2)}) collective-permute-start(bf16[8,2,1,384]{3,2,1,0:T(2,128)(2,1)S(1)} %get-tuple-element.34), channel_id=1, source_target_pairs={{256,321},{257,322},{258,323},{259,324},{260,325},{261,326},{262,3... | collective-permute-start | bytes 36872 | tf_op jit(solution)/shard_map/ppermute | solution.py:8
  47.4 3.3 %collective-permute-start.12 = (bf16[8,2,8,384]{3,2,1,0:T(8,128)(2,1)S(1)}, bf16[8,2,8,384]{3,2,1,0:T(8,128)(2,1)S(1)}, u32[]{:S(2)}, u32[]{:S(2)}) collective-permute-start(bf16[8,2,8,384]{3,2,1,0:T(8,128)(2,1)S(1)} %fusion.70), channel_id=1, source_target_pairs={{192,320},{193,321},{194,322},{195,323},{196,324},{197,325},{198,3... | collective-permute-start | bytes 294920 | tf_op jit(solution)/shard_map/ppermute | solution.py:8
  50.8 2.1 %collective-permute-start.22 = (bf16[8,2,8,384]{3,2,1,0:T(8,128)(2,1)S(1)}, bf16[8,2,8,384]{3,2,1,0:T(8,128)(2,1)S(1)}, u32[]{:S(2)}, u32[]{:S(2)}) collective-permute-start(bf16[8,2,8,384]{3,2,1,0:T(8,128)(2,1)S(1)} %fusion.71), channel_id=1, source_target_pairs={{320,384},{321,385},{322,386},{323,387},{324,388},{325,389},{326,3... | collective-permute-start | bytes 294920 | tf_op jit(solution)/shard_map/ppermute | solution.py:8
  51.5 1.3 %collective-permute-start.20 = (bf16[8,2,1,384]{3,2,1,0:T(2,128)(2,1)S(1)}, bf16[8,2,1,384]{3,2,1,0:T(2,128)(2,1)S(1)}, u32[]{:S(2)}, u32[]{:S(2)}) collective-permute-start(bf16[8,2,1,384]{3,2,1,0:T(2,128)(2,1)S(1)} %get-tuple-element.31), channel_id=1, source_target_pairs={{321,384},{322,385},{323,386},{324,387},{325,388},{326,389},{327,3... | collective-permute-start | bytes 36872 | tf_op jit(solution)/shard_map/ppermute | solution.py:8
  52.2 0.7 collective-permute-start.21
  55.5 2.8 %collective-permute-start.25 = (bf16[8,2,8,384]{3,2,1,0:T(8,128)(2,1)S(1)}, bf16[8,2,8,384]{3,2,1,0:T(8,128)(2,1)S(1)}, u32[]{:S(2)}, u32[]{:S(2)}) collective-permute-start(bf16[8,2,8,384]{3,2,1,0:T(8,128)(2,1)S(1)} %fusion.4), channel_id=1, source_target_pairs={{384,448},{385,449},{386,450},{387,451},{388,452},{389,453},{390,4... | collective-permute-start | bytes 294920 | tf_op jit(solution)/shard_map/ppermute | solution.py:8
  56.2 2.0 %collective-permute-start.23 = (bf16[8,2,1,384]{3,2,1,0:T(2,128)(2,1)S(1)}, bf16[8,2,1,384]{3,2,1,0:T(2,128)(2,1)S(1)}, u32[]{:S(2)}, u32[]{:S(2)}) collective-permute-start(bf16[8,2,1,384]{3,2,1,0:T(2,128)(2,1)S(1)} %get-tuple-element.29), channel_id=1, source_target_pairs={{385,448},{386,449},{387,450},{388,451},{389,452},{390,453},{391,4... | collective-permute-start | bytes 36872 | tf_op jit(solution)/shard_map/ppermute | solution.py:8
  56.8 1.4 %collective-permute-start.24 = (bf16[8,2,1,384]{3,2,1,0:T(2,128)(2,1)S(1)}, bf16[8,2,1,384]{3,2,1,0:T(2,128)(2,1)S(1)}, u32[]{:S(2)}, u32[]{:S(2)}) collective-permute-start(bf16[8,2,1,384]{3,2,1,0:T(2,128)(2,1)S(1)} %get-tuple-element.30), channel_id=1, source_target_pairs={{384,449},{385,450},{386,451},{387,452},{388,453},{389,454},{390,4... | collective-permute-start | bytes 36872 | tf_op jit(solution)/shard_map/ppermute | solution.py:8
  57.5 3.3 %collective-permute-start.19 = (bf16[8,2,8,384]{3,2,1,0:T(8,128)(2,1)S(1)}, bf16[8,2,8,384]{3,2,1,0:T(8,128)(2,1)S(1)}, u32[]{:S(2)}, u32[]{:S(2)}) collective-permute-start(bf16[8,2,8,384]{3,2,1,0:T(8,128)(2,1)S(1)} %fusion.71), channel_id=1, source_target_pairs={{320,448},{321,449},{322,450},{323,451},{324,452},{325,453},{326,4... | collective-permute-start | bytes 294920 | tf_op jit(solution)/shard_map/ppermute | solution.py:8

commit v5 on v4

--- a/solution.py
+++ b/solution.py
@@ -69,7 +69,8 @@
     current = stream
     residual = stream
     for stage in range(segments):
-        activated = activate(extend(current, left, right), gain)
+        strip = lax.optimization_barrier(activate(current, gain))
+        activated = extend(strip, activate(left, gain), activate(right, gain))
         conv_out = convolve(activated, kernel)
         if stage % 2 == 0:
             produced = jnp.where(col_live, conv_out, 0.0).astype(jnp.bfloat16)

time: 106 us -> 109 us (1.028)
  blocking collectives: 43.5 us -> 40.6 us
  local copies, waits for them, and re-layouts: 9.42 us -> 12.3 us
  other arithmetic: 6.83 us -> 9.58 us
    unnamed x69, local copies, waits for them, and re-layouts: 5.04 us -> 8.41 us
    all_to_all x1, blocking collectives: 43.5 us -> 40.6 us  [local(): spread = lax.all_to_all(final, 'section', 0, 0, tiled=True)]
    reduce_sum x8 -> x24, other arithmetic: 1.82 us -> 3.21 us  [activate(): jnp.mean(widened * widened, axis=-1, keepdims=True) + 1e-06]
  transfers between devices with their start and end apart: 26 -> 26, of which waited for: 2 -> 1; matrix products, arithmetic and copies ran while one was open for 10% -> 13% of each run, Pallas kernels for 0% -> 0%
where the time goes in v5:
time: 109 us; the launch traced here: 108 us
  blocking collectives  40.6 us (37%)
  starting transfers between devices  27.4 us (25%)
  local copies, waits for them, and re-layouts  12.3 us (11%)
  matrix products  12.2 us (11%)
  other arithmetic  9.58 us (9%)
  between operations  4.52 us (4%)
  waiting for transfers between devices  1.34 us (1%)
    all_to_all x1, blocking collectives, local(): spread = lax.all_to_all(final, 'section', 0, 0, tiled=True)  40.6 us
    ppermute x26, starting transfers between devices, hop(): return lax.ppermute(block, axes, pairs)  27.4 us
    dot_general x8, matrix products, convolve(): out = jnp.dot(joined, flat, preferred_element_type=jnp.float32)  12.2 us
    unnamed x69, local copies, waits for them, and re-layouts  8.41 us
    reduce_sum x24, other arithmetic, activate(): jnp.mean(widened * widened, axis=-1, keepdims=True) + 1e-06  3.21 us
  transfers between devices with their start and end apart: 26, of which 1 were waited for; matrix products, arithmetic and copies ran while one was open for 13% of the time, Pallas kernels for 0%

profile of v5, /device:TPU:256, one launch (start us, length us, event | category | flops | bytes accessed | tf_op | source)
XLA Modules:
  0.0 108.0 jit_solution(1864583733032648645)
XLA Ops:
  0.0 0.9 copy.41
  0.9 3.5 %collective-permute-start.1 = (bf16[8,2,8,384]{3,0,2,1:T(8,128)(2,1)S(1)}, bf16[8,2,8,384]{3,0,2,1:T(8,128)(2,1)S(1)}, u32[]{:S(2)}, u32[]{:S(2)}) collective-permute-start(bf16[8,2,8,384]{3,0,2,1:T(8,128)(2,1)S(1)} %copy.41), channel_id=1, source_target_pairs={{0,1},{1,2},{2,3},{3,4},{4,5},{5,6},{6,7},{7,8},{8,9},{9,10},{10,1... | collective-permute-start | bytes 294920 | tf_op jit(solution)/shard_map/ppermute | solution.py:8
  4.4 5.7 %collective-permute-start = (bf16[8,2,1,384]{3,0,2,1:T(8,128)(2,1)S(1)}, bf16[8,2,1,384]{3,0,2,1:T(8,128)(2,1)S(1)}, u32[]{:S(2)}, u32[]{:S(2)}) collective-permute-start(bf16[8,2,1,384]{3,0,2,1:T(8,128)(2,1)S(1)} %slice.420), channel_id=1, source_target_pairs={{1,0},{2,1},{3,2},{4,3},{5,4},{6,5},{7,6},{8,7},{9,8},{10,9},{11,1... | collective-permute-start | bytes 36872 | tf_op jit(solution)/shard_map/ppermute | solution.py:8
  10.1 1.4 %fusion.216 = (s32[1]{0:T(128)}, s32[1]{0:T(128)}) fusion(s32[64]{0:T(128)} %param.5, s32[]{:T(128)S(6)} %max.3, s32[]{:T(128)S(6)} %select_n.70), kind=kLoop, calls=%fused_computation.419 | loop fusion | bytes 24 | tf_op jit(solution)/shard_map/dynamic_slice | solution.py:65
  11.5 0.7 iota_compare_fusion.1
  12.9 0.7 convert_reduce_fusion
  13.6 1.1 fusion.62
  14.7 1.0 fusion.69
  20.0 2.2 %copy-done = bf16[1,3,3,1152,384]{4,3,2,1,0:T(8,128)(2,1)S(1)} copy-done((bf16[1,3,3,1152,384]{4,3,2,1,0:T(8,128)(2,1)S(1)}, bf16[1,3,3,1152,384]{4,3,2,1,0:T(8,128)(2,1)}, u32[]{:S(2)}) %copy-start) | copy-done | bytes 7962648
  22.2 1.5 %fusion = bf16[8,2,8,384]{3,0,2,1:T(8,128)(2,1)S(1)} fusion(bf16[8,2,8,10368]{3,0,2,1:T(8,128)(2,1)S(1)} %slice_dynamic-update-slice_fusion.63, bf16[10368,384,1,1]{1,0,3,2:T(8,128)(2,1)S(1)} %bitcast.41, pred[8]{0:T(512)(128)(4,1)S(1)} %iota_compare_fusion.1), kind=kOutput, calls=%fused_computation.13 | convolution fusion | flops 1019314176 | bytes 10715144 | tf_op jit(solution)/shard_map/dot_general | solution.py:30
  23.7 1.3 %collective-permute-start.2 = (bf16[8,2,1,384]{3,0,2,1:T(8,128)(2,1)S(1)}, bf16[8,2,1,384]{3,0,2,1:T(8,128)(2,1)S(1)}, u32[]{:S(2)}, u32[]{:S(2)}) collective-permute-start(bf16[8,2,1,384]{3,0,2,1:T(8,128)(2,1)S(1)} %get-tuple-element.41), channel_id=1, source_target_pairs={{1,64},{2,65},{3,66},{4,67},{5,68},{6,69},{7,70},{8,71},{9,72},{10... | collective-permute-start | bytes 36872 | tf_op jit(solution)/shard_map/ppermute | solution.py:8
  25.0 1.3 %collective-permute-start.4 = (bf16[8,2,8,384]{3,0,2,1:T(8,128)(2,1)S(1)}, bf16[8,2,8,384]{3,0,2,1:T(8,128)(2,1)S(1)}, u32[]{:S(2)}, u32[]{:S(2)}) collective-permute-start(bf16[8,2,8,384]{3,0,2,1:T(8,128)(2,1)S(1)} %fusion), channel_id=1, source_target_pairs={{0,64},{1,65},{2,66},{3,67},{4,68},{5,69},{6,70},{7,71},{8,72},{9,... | collective-permute-start | bytes 294920 | tf_op jit(solution)/shard_map/ppermute | solution.py:8
  26.3 1.3 %collective-permute-start.3 = (bf16[8,2,1,384]{3,0,2,1:T(8,128)(2,1)S(1)}, bf16[8,2,1,384]{3,0,2,1:T(8,128)(2,1)S(1)}, u32[]{:S(2)}, u32[]{:S(2)}) collective-permute-start(bf16[8,2,1,384]{3,0,2,1:T(8,128)(2,1)S(1)} %get-tuple-element.42), channel_id=1, source_target_pairs={{0,65},{1,66},{2,67},{3,68},{4,69},{5,70},{6,71},{7,72},{8,73},{9,... | collective-permute-start | bytes 36872 | tf_op jit(solution)/shard_map/ppermute | solution.py:8
  27.8 1.3 %collective-permute-done.3 = bf16[8,2,1,384]{3,0,2,1:T(8,128)(2,1)S(1)} collective-permute-done((bf16[8,2,1,384]{3,0,2,1:T(8,128)(2,1)S(1)}, bf16[8,2,1,384]{3,0,2,1:T(8,128)(2,1)S(1)}, u32[]{:S(2)}, u32[]{:S(2)}) %collective-permute-start.3) | collective-permute-done | bytes 12320 | tf_op jit(solution)/shard_map/ppermute | solution.py:8
  30.8 1.5 %fusion.5 = bf16[8,2,8,384]{3,0,2,1:T(8,128)(2,1)S(1)} fusion(bf16[8,2,8,10368]{3,0,2,1:T(8,128)(2,1)S(1)} %slice_dynamic-update-slice_fusion.54, bf16[10368,384,1,1]{1,0,3,2:T(8,128)(2,1)S(1)} %bitcast.42, pred[8]{0:T(512)(128)(4,1)S(1)} %iota_compare_fusion.1, bf16[8,2,8,384]{3,2,1,0:T(8,128)(2,1)S(1)} %copy-done.1), kind=kOutput, calls=%fused_computation.18 | convolution fusion | flops 1019461632 | bytes 10813448 | tf_op jit(solution)/shard_map/dot_general | solution.py:30
  33.0 0.7 collective-permute-start.8
  36.1 1.5 %fusion.2 = bf16[8,2,8,384]{3,0,2,1:T(8,128)(2,1)S(1)} fusion(bf16[8,2,8,10368]{3,0,2,1:T(8,128)(2,1)S(1)} %slice_dynamic-update-slice_fusion.45, bf16[10368,384,1,1]{1,0,3,2:T(8,128)(2,1)S(1)} %bitcast.43, pred[8]{0:T(512)(128)(4,1)S(1)} %iota_compare_fusion.1), kind=kOutput, calls=%fused_computation.15 | convolution fusion | flops 1019314176 | bytes 10715144 | tf_op jit(solution)/shard_map/dot_general | solution.py:30
  38.3 0.7 collective-permute-start.5
  39.0 0.7 collective-permute-start.11
  39.6 0.8 collective-permute-start.10
  42.2 1.5 %fusion.70 = bf16[8,2,8,384]{3,0,2,1:T(8,128)(2,1)S(1)} fusion(bf16[8,2,8,384]{3,0,2,1:T(8,128)(2,1)S(1)} %collective-permute-done.5, pred[8]{0:T(512)(128)(4,1)S(1)} %iota_compare_fusion.1, bf16[8,2,8,10368]{3,0,2,1:T(8,128)(2,1)S(1)} %slice_dynamic-update-slice_fusion.36, bf16[10368,384,1,1]{1,0,3,2:T(8,128)(2,1)S(1)} %bitcast.44), kind=kOutput, calls=%fused_computation.206 | convolution fusion | flops 1019412480 | bytes 10813448 | tf_op jit(solution)/shard_map/dot_general | solution.py:30
  44.5 0.7 collective-permute-start.15
  47.5 1.5 %fusion.3 = bf16[8,2,8,384]{3,0,2,1:T(8,128)(2,1)S(1)} fusion(bf16[8,2,8,10368]{3,0,2,1:T(8,128)(2,1)S(1)} %slice_dynamic-update-slice_fusion.27, bf16[10368,384,1,1]{1,0,3,2:T(8,128)(2,1)S(1)} %bitcast.45, pred[8]{0:T(512)(128)(4,1)S(1)} %iota_compare_fusion.1), kind=kOutput, calls=%fused_computation.16 | convolution fusion | flops 1019314176 | bytes 10715144 | tf_op jit(solution)/shard_map/dot_general | solution.py:30
  49.8 0.7 collective-permute-start.12
  50.4 0.7 collective-permute-start.18
  53.5 1.5 %fusion.217 = f32[8,2,8,384]{3,0,2,1:T(8,128)S(1)} fusion(bf16[8,2,8,10368]{3,0,2,1:T(8,128)(2,1)S(1)} %slice_dynamic-update-slice_fusion.18, bf16[10368,384,1,1]{1,0,3,2:T(8,128)(2,1)S(1)} %bitcast.46), kind=kOutput, calls=%fused_computation.420 | convolution fusion | flops 1019215872 | bytes 10813440 | tf_op jit(solution)/shard_map/dot_general | solution.py:30
  55.8 0.7 collective-permute-start.22
  58.9 1.5 %fusion.4 = bf16[8,2,8,384]{3,0,2,1:T(8,128)(2,1)S(1)} fusion(bf16[8,2,8,10368]{3,0,2,1:T(8,128)(2,1)S(1)} %slice_dynamic-update-slice_fusion.9, bf16[10368,384,1,1]{1,0,3,2:T(8,128)(2,1)S(1)} %bitcast.47, pred[8]{0:T(512)(128)(4,1)S(1)} %iota_compare_fusion.1), kind=kOutput, calls=%fused_computation.17 | convolution fusion | flops 1019314176 | bytes 10715144 | tf_op jit(solution)/shard_map/dot_general | solution.py:30
  60.5 0.9 collective-permute-start.23
  62.0 0.7 collective-permute-start.25
  65.1 1.5 %fusion.218 = f32[8,2,8,384]{3,0,2,1:T(8,128)S(1)} fusion(bf16[8,2,8,10368]{3,0,2,1:T(8,128)(2,1)S(1)} %slice_dynamic-update-slice_fusion, bf16[10368,384,1,1]{1,0,3,2:T(8,128)(2,1)S(1)} %bitcast.48), kind=kOutput, calls=%fused_computation.421 | convolution fusion | flops 1019215872 | bytes 10813440 | tf_op jit(solution)/shard_map/dot_general | solution.py:30
  66.8 40.6 %all_to_all.5 = bf16[8,2,8,384]{3,2,1,0:T(8,128)(2,1)S(1)} all-to-all(bf16[8,2,8,384]{3,2,1,0:T(8,128)(2,1)S(1)} %copy.44), channel_id=1, replica_groups=mesh['section'=8,'tile'=64] {'section'}, dimensions={0} | all-to-all | bytes 196608 | tf_op jit(solution)/shard_map/all_to_all | solution.py:90
  (211 shorter events, 21.2 us)
Async XLA Ops:
  0.9 17.7 %collective-permute-start.1 = (bf16[8,2,8,384]{3,0,2,1:T(8,128)(2,1)S(1)}, bf16[8,2,8,384]{3,0,2,1:T(8,128)(2,1)S(1)}, u32[]{:S(2)}, u32[]{:S(2)}) collective-permute-start(bf16[8,2,8,384]{3,0,2,1:T(8,128)(2,1)S(1)} %copy.41), channel_id=1, source_target_pairs={{0,1},{1,2},{2,3},{3,4},{4,5},{5,6},{6,7},{7,8},{8,9},{9,10},{10,1... | collective-permute-start | bytes 294920 | tf_op jit(solution)/shard_map/ppermute | solution.py:8
  4.4 14.1 %collective-permute-start = (bf16[8,2,1,384]{3,0,2,1:T(8,128)(2,1)S(1)}, bf16[8,2,1,384]{3,0,2,1:T(8,128)(2,1)S(1)}, u32[]{:S(2)}, u32[]{:S(2)}) collective-permute-start(bf16[8,2,1,384]{3,0,2,1:T(8,128)(2,1)S(1)} %slice.420), channel_id=1, source_target_pairs={{1,0},{2,1},{3,2},{4,3},{5,4},{6,5},{7,6},{8,7},{9,8},{10,9},{11,1... | collective-permute-start | bytes 36872 | tf_op jit(solution)/shard_map/ppermute | solution.py:8
  18.9 3.3 %copy-start = (bf16[1,3,3,1152,384]{4,3,2,1,0:T(8,128)(2,1)S(1)}, bf16[1,3,3,1152,384]{4,3,2,1,0:T(8,128)(2,1)}, u32[]{:S(2)}) copy-start(bf16[1,3,3,1152,384]{4,3,2,1,0:T(8,128)(2,1)} %param.6) | copy-start | bytes 23887876
  23.7 3.9 %collective-permute-start.2 = (bf16[8,2,1,384]{3,0,2,1:T(8,128)(2,1)S(1)}, bf16[8,2,1,384]{3,0,2,1:T(8,128)(2,1)S(1)}, u32[]{:S(2)}, u32[]{:S(2)}) collective-permute-start(bf16[8,2,1,384]{3,0,2,1:T(8,128)(2,1)S(1)} %get-tuple-element.41), channel_id=1, source_target_pairs={{1,64},{2,65},{3,66},{4,67},{5,68},{6,69},{7,70},{8,71},{9,72},{10... | collective-permute-start | bytes 36872 | tf_op jit(solution)/shard_map/ppermute | solution.py:8
  25.0 4.2 %collective-permute-start.4 = (bf16[8,2,8,384]{3,0,2,1:T(8,128)(2,1)S(1)}, bf16[8,2,8,384]{3,0,2,1:T(8,128)(2,1)S(1)}, u32[]{:S(2)}, u32[]{:S(2)}) collective-permute-start(bf16[8,2,8,384]{3,0,2,1:T(8,128)(2,1)S(1)} %fusion), channel_id=1, source_target_pairs={{0,64},{1,65},{2,66},{3,67},{4,68},{5,69},{6,70},{7,71},{8,72},{9,... | collective-permute-start | bytes 294920 | tf_op jit(solution)/shard_map/ppermute | solution.py:8
  26.3 2.7 %collective-permute-start.3 = (bf16[8,2,1,384]{3,0,2,1:T(8,128)(2,1)S(1)}, bf16[8,2,1,384]{3,0,2,1:T(8,128)(2,1)S(1)}, u32[]{:S(2)}, u32[]{:S(2)}) collective-permute-start(bf16[8,2,1,384]{3,0,2,1:T(8,128)(2,1)S(1)} %get-tuple-element.42), channel_id=1, source_target_pairs={{0,65},{1,66},{2,67},{3,68},{4,69},{5,70},{6,71},{7,72},{8,73},{9,... | collective-permute-start | bytes 36872 | tf_op jit(solution)/shard_map/ppermute | solution.py:8
  29.9 0.9 copy-start.1
  32.3 2.0 %collective-permute-start.6 = (bf16[8,2,1,384]{3,0,2,1:T(8,128)(2,1)S(1)}, bf16[8,2,1,384]{3,0,2,1:T(8,128)(2,1)S(1)}, u32[]{:S(2)}, u32[]{:S(2)}) collective-permute-start(bf16[8,2,1,384]{3,0,2,1:T(8,128)(2,1)S(1)} %get-tuple-element.39), channel_id=1, source_target_pairs={{65,128},{66,129},{67,130},{68,131},{69,132},{70,133},{71,134},{72... | collective-permute-start | bytes 36872 | tf_op jit(solution)/shard_map/ppermute | solution.py:8
  33.0 1.7 %collective-permute-start.8 = (bf16[8,2,8,384]{3,0,2,1:T(8,128)(2,1)S(1)}, bf16[8,2,8,384]{3,0,2,1:T(8,128)(2,1)S(1)}, u32[]{:S(2)}, u32[]{:S(2)}) collective-permute-start(bf16[8,2,8,384]{3,0,2,1:T(8,128)(2,1)S(1)} %fusion.5), channel_id=1, source_target_pairs={{64,128},{65,129},{66,130},{67,131},{68,132},{69,133},{70,134},{71... | collective-permute-start | bytes 294920 | tf_op jit(solution)/shard_map/ppermute | solution.py:8
  33.7 0.8 collective-permute-start.7
  37.6 2.9 %collective-permute-start.9 = (bf16[8,2,1,384]{3,0,2,1:T(8,128)(2,1)S(1)}, bf16[8,2,1,384]{3,0,2,1:T(8,128)(2,1)S(1)}, u32[]{:S(2)}, u32[]{:S(2)}) collective-permute-start(bf16[8,2,1,384]{3,0,2,1:T(8,128)(2,1)S(1)} %get-tuple-element.37), channel_id=1, source_target_pairs={{129,192},{130,193},{131,194},{132,195},{133,196},{134,197},{135,1... | collective-permute-start | bytes 36872 | tf_op jit(solution)/shard_map/ppermute | solution.py:8
  38.3 3.9 %collective-permute-start.5 = (bf16[8,2,8,384]{3,0,2,1:T(8,128)(2,1)S(1)}, bf16[8,2,8,384]{3,0,2,1:T(8,128)(2,1)S(1)}, u32[]{:S(2)}, u32[]{:S(2)}) collective-permute-start(bf16[8,2,8,384]{3,0,2,1:T(8,128)(2,1)S(1)} %fusion.5), channel_id=1, source_target_pairs={{64,192},{65,193},{66,194},{67,195},{68,196},{69,197},{70,198},{71... | collective-permute-start | bytes 294920 | tf_op jit(solution)/shard_map/ppermute | solution.py:8
  39.0 1.9 %collective-permute-start.11 = (bf16[8,2,8,384]{3,0,2,1:T(8,128)(2,1)S(1)}, bf16[8,2,8,384]{3,0,2,1:T(8,128)(2,1)S(1)}, u32[]{:S(2)}, u32[]{:S(2)}) collective-permute-start(bf16[8,2,8,384]{3,0,2,1:T(8,128)(2,1)S(1)} %fusion.2), channel_id=1, source_target_pairs={{128,192},{129,193},{130,194},{131,195},{132,196},{133,197},{134,1... | collective-permute-start | bytes 294920 | tf_op jit(solution)/shard_map/ppermute | solution.py:8
  39.6 1.0 collective-permute-start.10
  43.8 2.0 %collective-permute-start.13 = (bf16[8,2,1,384]{3,0,2,1:T(8,128)(2,1)S(1)}, bf16[8,2,1,384]{3,0,2,1:T(8,128)(2,1)S(1)}, u32[]{:S(2)}, u32[]{:S(2)}) collective-permute-start(bf16[8,2,1,384]{3,0,2,1:T(8,128)(2,1)S(1)} %get-tuple-element.35), channel_id=1, source_target_pairs={{193,256},{194,257},{195,258},{196,259},{197,260},{198,261},{199,2... | collective-permute-start | bytes 36872 | tf_op jit(solution)/shard_map/ppermute | solution.py:8
  44.5 1.7 %collective-permute-start.15 = (bf16[8,2,8,384]{3,0,2,1:T(8,128)(2,1)S(1)}, bf16[8,2,8,384]{3,0,2,1:T(8,128)(2,1)S(1)}, u32[]{:S(2)}, u32[]{:S(2)}) collective-permute-start(bf16[8,2,8,384]{3,0,2,1:T(8,128)(2,1)S(1)} %fusion.70), channel_id=1, source_target_pairs={{192,256},{193,257},{194,258},{195,259},{196,260},{197,261},{198,2... | collective-permute-start | bytes 294920 | tf_op jit(solution)/shard_map/ppermute | solution.py:8
  45.1 0.8 collective-permute-start.14
  49.1 2.7 %collective-permute-start.16 = (bf16[8,2,1,384]{3,0,2,1:T(8,128)(2,1)S(1)}, bf16[8,2,1,384]{3,0,2,1:T(8,128)(2,1)S(1)}, u32[]{:S(2)}, u32[]{:S(2)}) collective-permute-start(bf16[8,2,1,384]{3,0,2,1:T(8,128)(2,1)S(1)} %get-tuple-element.33), channel_id=1, source_target_pairs={{257,320},{258,321},{259,322},{260,323},{261,324},{262,325},{263,3... | collective-permute-start | bytes 36872 | tf_op jit(solution)/shard_map/ppermute | solution.py:8
  49.8 5.3 %collective-permute-start.12 = (bf16[8,2,8,384]{3,0,2,1:T(8,128)(2,1)S(1)}, bf16[8,2,8,384]{3,0,2,1:T(8,128)(2,1)S(1)}, u32[]{:S(2)}, u32[]{:S(2)}) collective-permute-start(bf16[8,2,8,384]{3,0,2,1:T(8,128)(2,1)S(1)} %fusion.70), channel_id=1, source_target_pairs={{192,320},{193,321},{194,322},{195,323},{196,324},{197,325},{198,3... | collective-permute-start | bytes 294920 | tf_op jit(solution)/shard_map/ppermute | solution.py:8
  50.4 1.7 %collective-permute-start.18 = (bf16[8,2,8,384]{3,0,2,1:T(8,128)(2,1)S(1)}, bf16[8,2,8,384]{3,0,2,1:T(8,128)(2,1)S(1)}, u32[]{:S(2)}, u32[]{:S(2)}) collective-permute-start(bf16[8,2,8,384]{3,0,2,1:T(8,128)(2,1)S(1)} %fusion.3), channel_id=1, source_target_pairs={{256,320},{257,321},{258,322},{259,323},{260,324},{261,325},{262,3... | collective-permute-start | bytes 294920 | tf_op jit(solution)/shard_map/ppermute | solution.py:8
  51.1 0.8 collective-permute-start.17
  55.2 2.0 %collective-permute-start.20 = (bf16[8,2,1,384]{3,0,2,1:T(8,128)(2,1)S(1)}, bf16[8,2,1,384]{3,0,2,1:T(8,128)(2,1)S(1)}, u32[]{:S(2)}, u32[]{:S(2)}) collective-permute-start(bf16[8,2,1,384]{3,0,2,1:T(8,128)(2,1)S(1)} %get-tuple-element.31), channel_id=1, source_target_pairs={{321,384},{322,385},{323,386},{324,387},{325,388},{326,389},{327,3... | collective-permute-start | bytes 36872 | tf_op jit(solution)/shard_map/ppermute | solution.py:8
  55.8 1.7 %collective-permute-start.22 = (bf16[8,2,8,384]{3,0,2,1:T(8,128)(2,1)S(1)}, bf16[8,2,8,384]{3,0,2,1:T(8,128)(2,1)S(1)}, u32[]{:S(2)}, u32[]{:S(2)}) collective-permute-start(bf16[8,2,8,384]{3,0,2,1:T(8,128)(2,1)S(1)} %fusion.71), channel_id=1, source_target_pairs={{320,384},{321,385},{322,386},{323,387},{324,388},{325,389},{326,3... | collective-permute-start | bytes 294920 | tf_op jit(solution)/shard_map/ppermute | solution.py:8
  56.5 0.8 collective-permute-start.21
  60.5 2.9 %collective-permute-start.23 = (bf16[8,2,1,384]{3,0,2,1:T(8,128)(2,1)S(1)}, bf16[8,2,1,384]{3,0,2,1:T(8,128)(2,1)S(1)}, u32[]{:S(2)}, u32[]{:S(2)}) collective-permute-start(bf16[8,2,1,384]{3,0,2,1:T(8,128)(2,1)S(1)} %get-tuple-element.29), channel_id=1, source_target_pairs={{385,448},{386,449},{387,450},{388,451},{389,452},{390,453},{391,4... | collective-permute-start | bytes 36872 | tf_op jit(solution)/shard_map/ppermute | solution.py:8
  61.4 5.3 %collective-permute-start.19 = (bf16[8,2,8,384]{3,0,2,1:T(8,128)(2,1)S(1)}, bf16[8,2,8,384]{3,0,2,1:T(8,128)(2,1)S(1)}, u32[]{:S(2)}, u32[]{:S(2)}) collective-permute-start(bf16[8,2,8,384]{3,0,2,1:T(8,128)(2,1)S(1)} %fusion.71), channel_id=1, source_target_pairs={{320,448},{321,449},{322,450},{323,451},{324,452},{325,453},{326,4... | collective-permute-start | bytes 294920 | tf_op jit(solution)/shard_map/ppermute | solution.py:8
  62.0 1.7 %collective-permute-start.25 = (bf16[8,2,8,384]{3,0,2,1:T(8,128)(2,1)S(1)}, bf16[8,2,8,384]{3,0,2,1:T(8,128)(2,1)S(1)}, u32[]{:S(2)}, u32[]{:S(2)}) collective-permute-start(bf16[8,2,8,384]{3,0,2,1:T(8,128)(2,1)S(1)} %fusion.4), channel_id=1, source_target_pairs={{384,448},{385,449},{386,450},{387,451},{388,452},{389,453},{390,4... | collective-permute-start | bytes 294920 | tf_op jit(solution)/shard_map/ppermute | solution.py:8
  62.7 0.8 collective-permute-start.24

commit v6 on v4

--- a/solution.py
+++ b/solution.py
@@ -20,12 +20,10 @@
     padded = jnp.pad(activated, ((2, 0), (1, 1), (0, 0), (0, 0)))
     shifted = jnp.concatenate([padded[:, :, k : k + cols] for k in range(3)], axis=-1)
     shifted = lax.optimization_barrier(shifted)
-    taps = [
-        shifted[frame_tap : frame_tap + frames, row_tap : row_tap + rows]
-        for frame_tap in range(3)
-        for row_tap in range(3)
-    ]
-    joined = jnp.concatenate(taps, axis=-1).reshape(frames * rows * cols, 27 * channels)
+    stacked = jnp.concatenate([shifted[:, j : j + rows] for j in range(3)], axis=-1)
+    stacked = lax.optimization_barrier(stacked)
+    joined = jnp.concatenate([stacked[i : i + frames] for i in range(3)], axis=-1)
+    joined = joined.reshape(frames * rows * cols, 27 * channels)
     flat = kernel.reshape(27 * channels, kernel.shape[-1])
     out = jnp.dot(joined, flat, preferred_element_type=jnp.float32)
     return out.reshape(frames, rows, cols, kernel.shape[-1])

time: 106 us -> 107 us (level)
    slice x0 -> x16, local copies, waits for them, and re-layouts: none -> 2.09 us  [the longest x8 1.44 us: convolve(): joined = jnp.concatenate([stacked[i:i + frames] for i in range(3)], axis=-1)]
    unnamed x69 -> x5, local copies, waits for them, and re-layouts: 5.04 us -> 3.6 us
  transfers between devices with their start and end apart: 26 -> 26, of which waited for: 2 -> 2; matrix products, arithmetic and copies ran while one was open for 10% -> 11% of each run, Pallas kernels for 0% -> 0%
where the time goes in v6:
time: 107 us
  blocking collectives  43.5 us (41%)
  starting transfers between devices  27.2 us (25%)
  matrix products  12.6 us (12%)
  local copies, waits for them, and re-layouts  9.88 us (9%)
  other arithmetic  7.58 us (7%)
  between operations  4.32 us (4%)
  waiting for transfers between devices  1.54 us (1%)
    all_to_all x1, blocking collectives, local(): spread = lax.all_to_all(final, 'section', 0, 0, tiled=True)  43.5 us
    ppermute x26, starting transfers between devices, hop(): return lax.ppermute(block, axes, pairs)  27.2 us
    dot_general x8, matrix products, convolve(): out = jnp.dot(joined, flat, preferred_element_type=jnp.float32)  12.6 us
    unnamed x5, local copies, waits for them, and re-layouts  3.6 us
  transfers between devices with their start and end apart: 26, of which 2 were waited for; matrix products, arithmetic and copies ran while one was open for 11% of the time, Pallas kernels for 0%

profile of v6, /device:TPU:256, one launch (start us, length us, event | category | flops | bytes accessed | tf_op | source)
XLA Modules:
  0.0 106.6 jit_solution(3720622341121825705)
XLA Ops:
  0.0 3.5 %collective-permute-start.1 = (bf16[8,2,8,384]{3,2,1,0:T(8,128)(2,1)}, bf16[8,2,8,384]{3,2,1,0:T(8,128)(2,1)S(1)}, u32[]{:S(2)}, u32[]{:S(2)}) collective-permute-start(bf16[8,2,8,384]{3,2,1,0:T(8,128)(2,1)} %param.4), channel_id=1, source_target_pairs={{0,1},{1,2},{2,3},{3,4},{4,5},{5,6},{6,7},{7,8},{8,9},{9,10},{10,1... | collective-permute-start | bytes 294920 | tf_op jit(solution)/shard_map/ppermute | solution.py:8
  3.5 0.9 slice.243
  4.4 5.7 %collective-permute-start = (bf16[8,2,1,384]{3,0,2,1:T(8,128)(2,1)S(1)}, bf16[8,2,1,384]{3,0,2,1:T(8,128)(2,1)S(1)}, u32[]{:S(2)}, u32[]{:S(2)}) collective-permute-start(bf16[8,2,1,384]{3,0,2,1:T(8,128)(2,1)S(1)} %copy.22), channel_id=1, source_target_pairs={{1,0},{2,1},{3,2},{4,3},{5,4},{6,5},{7,6},{8,7},{9,8},{10,9},{11,1... | collective-permute-start | bytes 36872 | tf_op jit(solution)/shard_map/ppermute | solution.py:8
  10.1 1.4 %fusion.181 = (s32[1]{0:T(128)}, s32[1]{0:T(128)}) fusion(s32[64]{0:T(128)} %param.5, s32[]{:T(128)S(6)} %max.3, s32[]{:T(128)S(6)} %select_n.70), kind=kLoop, calls=%fused_computation.251 | loop fusion | bytes 24 | tf_op jit(solution)/shard_map/dynamic_slice | solution.py:63
  12.8 0.7 convert_reduce_fusion
  13.5 1.0 broadcast_select_fusion
  18.2 2.9 %copy-done.1 = bf16[1,3,3,1152,384]{4,3,2,1,0:T(8,128)(2,1)S(1)} copy-done((bf16[1,3,3,1152,384]{4,3,2,1,0:T(8,128)(2,1)S(1)}, bf16[1,3,3,1152,384]{4,3,2,1,0:T(8,128)(2,1)}, u32[]{:S(2)}) %copy-start.1) | copy-done | bytes 7962648
  21.1 1.6 %fusion.75 = bf16[8,2,8,384]{3,2,1,0:T(8,128)(2,1)S(1)} fusion(bf16[10368,384,1,1]{1,0,3,2:T(8,128)(2,1)S(1)} %bitcast.47, bf16[8,2,8,3456]{3,2,1,0:T(8,128)(2,1)S(1)} %get-tuple-element.27, bf16[8,2,8,3456]{3,2,1,0:T(8,128)(2,1)S(1)} %get-tuple-element.28, bf16[8,2,8,3456]{3,2,1,0:T(8,128)(2,1)S(1)} %get-tuple-element.26, ...), kind=kOutput, calls=%fused_computation.57 | convolution fusion | flops 1027276800 | bytes 10715144 | tf_op jit(solution)/shard_map/dot_general | solution.py:28
  22.7 1.3 %collective-permute-start.4 = (bf16[8,2,8,384]{3,2,1,0:T(8,128)(2,1)S(1)}, bf16[8,2,8,384]{3,2,1,0:T(8,128)(2,1)S(1)}, u32[]{:S(2)}, u32[]{:S(2)}) collective-permute-start(bf16[8,2,8,384]{3,2,1,0:T(8,128)(2,1)S(1)} %fusion.75), channel_id=1, source_target_pairs={{0,64},{1,65},{2,66},{3,67},{4,68},{5,69},{6,70},{7,71},{8,72},{9,... | collective-permute-start | bytes 294920 | tf_op jit(solution)/shard_map/ppermute | solution.py:8
  24.1 1.3 %collective-permute-start.2 = (bf16[8,2,1,384]{3,2,1,0:T(2,128)(2,1)S(1)}, bf16[8,2,1,384]{3,2,1,0:T(2,128)(2,1)S(1)}, u32[]{:S(2)}, u32[]{:S(2)}) collective-permute-start(bf16[8,2,1,384]{3,2,1,0:T(2,128)(2,1)S(1)} %get-tuple-element.89), channel_id=1, source_target_pairs={{1,64},{2,65},{3,66},{4,67},{5,68},{6,69},{7,70},{8,71},{9,72},{10... | collective-permute-start | bytes 36872 | tf_op jit(solution)/shard_map/ppermute | solution.py:8
  25.4 1.3 %collective-permute-start.3 = (bf16[8,2,1,384]{3,2,1,0:T(2,128)(2,1)S(1)}, bf16[8,2,1,384]{3,2,1,0:T(2,128)(2,1)S(1)}, u32[]{:S(2)}, u32[]{:S(2)}) collective-permute-start(bf16[8,2,1,384]{3,2,1,0:T(2,128)(2,1)S(1)} %get-tuple-element.90), channel_id=1, source_target_pairs={{0,65},{1,66},{2,67},{3,68},{4,69},{5,70},{6,71},{7,72},{8,73},{9,... | collective-permute-start | bytes 36872 | tf_op jit(solution)/shard_map/ppermute | solution.py:8
  26.9 1.3 %collective-permute-done.3 = bf16[8,2,1,384]{3,2,1,0:T(2,128)(2,1)S(1)} collective-permute-done((bf16[8,2,1,384]{3,2,1,0:T(2,128)(2,1)S(1)}, bf16[8,2,1,384]{3,2,1,0:T(2,128)(2,1)S(1)}, u32[]{:S(2)}, u32[]{:S(2)}) %collective-permute-start.3) | collective-permute-done | bytes 12320 | tf_op jit(solution)/shard_map/ppermute | solution.py:8
  29.2 0.7 copy-done
  29.9 1.6 %fusion.78 = bf16[8,2,8,384]{3,2,1,0:T(8,128)(2,1)S(1)} fusion(bf16[10368,384,1,1]{1,0,3,2:T(8,128)(2,1)S(1)} %bitcast.48, bf16[8,2,8,3456]{3,2,1,0:T(8,128)(2,1)S(1)} %get-tuple-element.24, bf16[8,2,8,3456]{3,2,1,0:T(8,128)(2,1)S(1)} %get-tuple-element.25, bf16[8,2,8,3456]{3,2,1,0:T(8,128)(2,1)S(1)} %get-tuple-element.23, ...), kind=kOutput, calls=%fused_computation.66 | convolution fusion | flops 1027424256 | bytes 10813448 | tf_op jit(solution)/shard_map/dot_general | solution.py:28
  31.5 0.7 collective-permute-start.8
  32.2 0.7 collective-permute-start.6
  34.7 1.6 %fusion.69 = bf16[8,2,8,384]{3,2,1,0:T(8,128)(2,1)S(1)} fusion(bf16[10368,384,1,1]{1,0,3,2:T(8,128)(2,1)S(1)} %bitcast.49, bf16[8,2,8,3456]{3,2,1,0:T(8,128)(2,1)S(1)} %get-tuple-element.21, bf16[8,2,8,3456]{3,2,1,0:T(8,128)(2,1)S(1)} %get-tuple-element.22, bf16[8,2,8,3456]{3,2,1,0:T(8,128)(2,1)S(1)} %get-tuple-element.20, ...), kind=kOutput, calls=%fused_computation.55 | convolution fusion | flops 1027276800 | bytes 10715144 | tf_op jit(solution)/shard_map/dot_general | solution.py:28
  36.3 0.7 collective-permute-start.11
  38.3 0.7 collective-permute-start.5
  40.1 1.6 %fusion.145 = bf16[8,2,8,384]{3,2,1,0:T(8,128)(2,1)S(1)} fusion(bf16[8,2,8,384]{3,2,1,0:T(8,128)(2,1)S(1)} %collective-permute-done.5, pred[8]{0:T(512)(128)(4,1)S(1)} %iota_compare_fusion.1, bf16[10368,384,1,1]{1,0,3,2:T(8,128)(2,1)S(1)} %bitcast.50, bf16[8,2,8,3456]{3,2,1,0:T(8,128)(2,1)S(1)} %get-tuple-element.18, ...), kind=kOutput, calls=%fused_computation.190 | convolution fusion | flops 1027375104 | bytes 10813448 | tf_op jit(solution)/shard_map/dot_general | solution.py:28
  41.7 0.7 collective-permute-start.15
  43.1 0.8 collective-permute-start.14
  45.1 1.6 %fusion.63 = bf16[8,2,8,384]{3,2,1,0:T(8,128)(2,1)S(1)} fusion(bf16[10368,384,1,1]{1,0,3,2:T(8,128)(2,1)S(1)} %bitcast.51, bf16[8,2,8,3456]{3,2,1,0:T(8,128)(2,1)S(1)} %get-tuple-element.15, bf16[8,2,8,3456]{3,2,1,0:T(8,128)(2,1)S(1)} %get-tuple-element.16, bf16[8,2,8,3456]{3,2,1,0:T(8,128)(2,1)S(1)} %get-tuple-element.14, ...), kind=kOutput, calls=%fused_computation.53 | convolution fusion | flops 1027276800 | bytes 10715144 | tf_op jit(solution)/shard_map/dot_general | solution.py:28
  46.7 0.7 collective-permute-start.18
  48.7 0.7 collective-permute-start.12
  50.5 1.6 %fusion.30 = f32[8,2,8,384]{3,2,1,0:T(8,128)S(1)} fusion(bf16[10368,384,1,1]{1,0,3,2:T(8,128)(2,1)S(1)} %bitcast.52, bf16[8,2,8,3456]{3,2,1,0:T(8,128)(2,1)S(1)} %get-tuple-element.12, bf16[8,2,8,3456]{3,2,1,0:T(8,128)(2,1)S(1)} %get-tuple-element.13, bf16[8,2,8,3456]{3,2,1,0:T(8,128)(2,1)S(1)} %get-tuple-element.11), kind=kOutput, calls=%fused_computation.30 | convolution fusion | flops 1027178496 | bytes 10813440 | tf_op jit(solution)/shard_map/dot_general | solution.py:28
  52.2 0.7 collective-permute-start.22
  55.4 1.6 %fusion.57 = bf16[8,2,8,384]{3,2,1,0:T(8,128)(2,1)S(1)} fusion(bf16[10368,384,1,1]{1,0,3,2:T(8,128)(2,1)S(1)} %bitcast.53, bf16[8,2,8,3456]{3,2,1,0:T(8,128)(2,1)S(1)} %get-tuple-element.9, bf16[8,2,8,3456]{3,2,1,0:T(8,128)(2,1)S(1)} %get-tuple-element.10, bf16[8,2,8,3456]{3,2,1,0:T(8,128)(2,1)S(1)} %get-tuple-element.8, pred[8]{0:T(512)(128)(4,1)S(1)} %iota_compare_fusion.1), kind=kOutput, calls=%fused_computation.51 | convolution fusion | flops 1027276800 | bytes 10715144 | tf_op jit(solution)/shard_map/dot_general | solution.py:28
  57.0 0.7 collective-permute-start.25
  59.0 0.7 collective-permute-start.19
  60.8 1.6 %fusion.42 = f32[8,2,8,384]{3,2,1,0:T(8,128)S(1)} fusion(bf16[10368,384,1,1]{1,0,3,2:T(8,128)(2,1)S(1)} %bitcast.54, bf16[8,2,8,3456]{3,2,1,0:T(8,128)(2,1)S(1)} %get-tuple-element.6, bf16[8,2,8,3456]{3,2,1,0:T(8,128)(2,1)S(1)} %get-tuple-element.7, bf16[8,2,8,3456]{3,2,1,0:T(8,128)(2,1)S(1)} %get-tuple-element.5), kind=kOutput, calls=%fused_computation.42 | convolution fusion | flops 1027178496 | bytes 10813440 | tf_op jit(solution)/shard_map/dot_general | solution.py:28
  62.5 43.5 %all_to_all.5 = bf16[8,2,8,384]{3,2,1,0:T(8,128)(2,1)S(1)} all-to-all(bf16[8,2,8,384]{3,2,1,0:T(8,128)(2,1)S(1)} %fusion.147), channel_id=1, replica_groups=mesh['section'=8,'tile'=64] {'section'}, dimensions={0} | all-to-all | bytes 196608 | tf_op jit(solution)/shard_map/all_to_all | solution.py:87
  (131 shorter events, 16.8 us)
Async XLA Ops:
  0.0 17.1 %collective-permute-start.1 = (bf16[8,2,8,384]{3,2,1,0:T(8,128)(2,1)}, bf16[8,2,8,384]{3,2,1,0:T(8,128)(2,1)S(1)}, u32[]{:S(2)}, u32[]{:S(2)}) collective-permute-start(bf16[8,2,8,384]{3,2,1,0:T(8,128)(2,1)} %param.4), channel_id=1, source_target_pairs={{0,1},{1,2},{2,3},{3,4},{4,5},{5,6},{6,7},{7,8},{8,9},{9,10},{10,1... | collective-permute-start | bytes 294920 | tf_op jit(solution)/shard_map/ppermute | solution.py:8
  4.4 12.7 %collective-permute-start = (bf16[8,2,1,384]{3,0,2,1:T(8,128)(2,1)S(1)}, bf16[8,2,1,384]{3,0,2,1:T(8,128)(2,1)S(1)}, u32[]{:S(2)}, u32[]{:S(2)}) collective-permute-start(bf16[8,2,1,384]{3,0,2,1:T(8,128)(2,1)S(1)} %copy.22), channel_id=1, source_target_pairs={{1,0},{2,1},{3,2},{4,3},{5,4},{6,5},{7,6},{8,7},{9,8},{10,9},{11,1... | collective-permute-start | bytes 36872 | tf_op jit(solution)/shard_map/ppermute | solution.py:8
  17.9 3.3 %copy-start.1 = (bf16[1,3,3,1152,384]{4,3,2,1,0:T(8,128)(2,1)S(1)}, bf16[1,3,3,1152,384]{4,3,2,1,0:T(8,128)(2,1)}, u32[]{:S(2)}) copy-start(bf16[1,3,3,1152,384]{4,3,2,1,0:T(8,128)(2,1)} %param.6) | copy-start | bytes 23887876
  22.7 5.5 %collective-permute-start.4 = (bf16[8,2,8,384]{3,2,1,0:T(8,128)(2,1)S(1)}, bf16[8,2,8,384]{3,2,1,0:T(8,128)(2,1)S(1)}, u32[]{:S(2)}, u32[]{:S(2)}) collective-permute-start(bf16[8,2,8,384]{3,2,1,0:T(8,128)(2,1)S(1)} %fusion.75), channel_id=1, source_target_pairs={{0,64},{1,65},{2,66},{3,67},{4,68},{5,69},{6,70},{7,71},{8,72},{9,... | collective-permute-start | bytes 294920 | tf_op jit(solution)/shard_map/ppermute | solution.py:8
  24.1 2.8 %collective-permute-start.2 = (bf16[8,2,1,384]{3,2,1,0:T(2,128)(2,1)S(1)}, bf16[8,2,1,384]{3,2,1,0:T(2,128)(2,1)S(1)}, u32[]{:S(2)}, u32[]{:S(2)}) collective-permute-start(bf16[8,2,1,384]{3,2,1,0:T(2,128)(2,1)S(1)} %get-tuple-element.89), channel_id=1, source_target_pairs={{1,64},{2,65},{3,66},{4,67},{5,68},{6,69},{7,70},{8,71},{9,72},{10... | collective-permute-start | bytes 36872 | tf_op jit(solution)/shard_map/ppermute | solution.py:8
  25.4 2.8 %collective-permute-start.3 = (bf16[8,2,1,384]{3,2,1,0:T(2,128)(2,1)S(1)}, bf16[8,2,1,384]{3,2,1,0:T(2,128)(2,1)S(1)}, u32[]{:S(2)}, u32[]{:S(2)}) collective-permute-start(bf16[8,2,1,384]{3,2,1,0:T(2,128)(2,1)S(1)} %get-tuple-element.90), channel_id=1, source_target_pairs={{0,65},{1,66},{2,67},{3,68},{4,69},{5,70},{6,71},{7,72},{8,73},{9,... | collective-permute-start | bytes 36872 | tf_op jit(solution)/shard_map/ppermute | solution.py:8
  29.0 0.9 copy-start
  31.5 2.1 %collective-permute-start.8 = (bf16[8,2,8,384]{3,2,1,0:T(8,128)(2,1)S(1)}, bf16[8,2,8,384]{3,2,1,0:T(8,128)(2,1)S(1)}, u32[]{:S(2)}, u32[]{:S(2)}) collective-permute-start(bf16[8,2,8,384]{3,2,1,0:T(8,128)(2,1)S(1)} %fusion.78), channel_id=1, source_target_pairs={{64,128},{65,129},{66,130},{67,131},{68,132},{69,133},{70,134},{71... | collective-permute-start | bytes 294920 | tf_op jit(solution)/shard_map/ppermute | solution.py:8
  32.2 1.3 %collective-permute-start.6 = (bf16[8,2,1,384]{3,2,1,0:T(2,128)(2,1)S(1)}, bf16[8,2,1,384]{3,2,1,0:T(2,128)(2,1)S(1)}, u32[]{:S(2)}, u32[]{:S(2)}) collective-permute-start(bf16[8,2,1,384]{3,2,1,0:T(2,128)(2,1)S(1)} %get-tuple-element.87), channel_id=1, source_target_pairs={{65,128},{66,129},{67,130},{68,131},{69,132},{70,133},{71,134},{72... | collective-permute-start | bytes 36872 | tf_op jit(solution)/shard_map/ppermute | solution.py:8
  32.9 0.7 collective-permute-start.7
  36.3 2.8 %collective-permute-start.11 = (bf16[8,2,8,384]{3,2,1,0:T(8,128)(2,1)S(1)}, bf16[8,2,8,384]{3,2,1,0:T(8,128)(2,1)S(1)}, u32[]{:S(2)}, u32[]{:S(2)}) collective-permute-start(bf16[8,2,8,384]{3,2,1,0:T(8,128)(2,1)S(1)} %fusion.69), channel_id=1, source_target_pairs={{128,192},{129,193},{130,194},{131,195},{132,196},{133,197},{134,1... | collective-permute-start | bytes 294920 | tf_op jit(solution)/shard_map/ppermute | solution.py:8
  37.0 2.0 %collective-permute-start.9 = (bf16[8,2,1,384]{3,2,1,0:T(2,128)(2,1)S(1)}, bf16[8,2,1,384]{3,2,1,0:T(2,128)(2,1)S(1)}, u32[]{:S(2)}, u32[]{:S(2)}) collective-permute-start(bf16[8,2,1,384]{3,2,1,0:T(2,128)(2,1)S(1)} %get-tuple-element.85), channel_id=1, source_target_pairs={{129,192},{130,193},{131,194},{132,195},{133,196},{134,197},{135,1... | collective-permute-start | bytes 36872 | tf_op jit(solution)/shard_map/ppermute | solution.py:8
  37.7 1.4 %collective-permute-start.10 = (bf16[8,2,1,384]{3,2,1,0:T(2,128)(2,1)S(1)}, bf16[8,2,1,384]{3,2,1,0:T(2,128)(2,1)S(1)}, u32[]{:S(2)}, u32[]{:S(2)}) collective-permute-start(bf16[8,2,1,384]{3,2,1,0:T(2,128)(2,1)S(1)} %get-tuple-element.86), channel_id=1, source_target_pairs={{128,193},{129,194},{130,195},{131,196},{132,197},{133,198},{134,1... | collective-permute-start | bytes 36872 | tf_op jit(solution)/shard_map/ppermute | solution.py:8
  38.3 1.8 %collective-permute-start.5 = (bf16[8,2,8,384]{3,2,1,0:T(8,128)(2,1)S(1)}, bf16[8,2,8,384]{3,2,1,0:T(8,128)(2,1)S(1)}, u32[]{:S(2)}, u32[]{:S(2)}) collective-permute-start(bf16[8,2,8,384]{3,2,1,0:T(8,128)(2,1)S(1)} %fusion.78), channel_id=1, source_target_pairs={{64,192},{65,193},{66,194},{67,195},{68,196},{69,197},{70,198},{71... | collective-permute-start | bytes 294920 | tf_op jit(solution)/shard_map/ppermute | solution.py:8
  41.7 2.3 %collective-permute-start.15 = (bf16[8,2,8,384]{3,2,1,0:T(8,128)(2,1)S(1)}, bf16[8,2,8,384]{3,2,1,0:T(8,128)(2,1)S(1)}, u32[]{:S(2)}, u32[]{:S(2)}) collective-permute-start(bf16[8,2,8,384]{3,2,1,0:T(8,128)(2,1)S(1)} %fusion.145), channel_id=1, source_target_pairs={{192,256},{193,257},{194,258},{195,259},{196,260},{197,261},{198,2... | collective-permute-start | bytes 294920 | tf_op jit(solution)/shard_map/ppermute | solution.py:8
  42.5 1.5 %collective-permute-start.13 = (bf16[8,2,1,384]{3,2,1,0:T(2,128)(2,1)S(1)}, bf16[8,2,1,384]{3,2,1,0:T(2,128)(2,1)S(1)}, u32[]{:S(2)}, u32[]{:S(2)}) collective-permute-start(bf16[8,2,1,384]{3,2,1,0:T(2,128)(2,1)S(1)} %get-tuple-element.83), channel_id=1, source_target_pairs={{193,256},{194,257},{195,258},{196,259},{197,260},{198,261},{199,2... | collective-permute-start | bytes 36872 | tf_op jit(solution)/shard_map/ppermute | solution.py:8
  43.1 0.9 collective-permute-start.14
  46.7 2.8 %collective-permute-start.18 = (bf16[8,2,8,384]{3,2,1,0:T(8,128)(2,1)S(1)}, bf16[8,2,8,384]{3,2,1,0:T(8,128)(2,1)S(1)}, u32[]{:S(2)}, u32[]{:S(2)}) collective-permute-start(bf16[8,2,8,384]{3,2,1,0:T(8,128)(2,1)S(1)} %fusion.63), channel_id=1, source_target_pairs={{256,320},{257,321},{258,322},{259,323},{260,324},{261,325},{262,3... | collective-permute-start | bytes 294920 | tf_op jit(solution)/shard_map/ppermute | solution.py:8
  47.4 2.0 %collective-permute-start.16 = (bf16[8,2,1,384]{3,2,1,0:T(2,128)(2,1)S(1)}, bf16[8,2,1,384]{3,2,1,0:T(2,128)(2,1)S(1)}, u32[]{:S(2)}, u32[]{:S(2)}) collective-permute-start(bf16[8,2,1,384]{3,2,1,0:T(2,128)(2,1)S(1)} %get-tuple-element.81), channel_id=1, source_target_pairs={{257,320},{258,321},{259,322},{260,323},{261,324},{262,325},{263,3... | collective-permute-start | bytes 36872 | tf_op jit(solution)/shard_map/ppermute | solution.py:8
  48.1 1.4 %collective-permute-start.17 = (bf16[8,2,1,384]{3,2,1,0:T(2,128)(2,1)S(1)}, bf16[8,2,1,384]{3,2,1,0:T(2,128)(2,1)S(1)}, u32[]{:S(2)}, u32[]{:S(2)}) collective-permute-start(bf16[8,2,1,384]{3,2,1,0:T(2,128)(2,1)S(1)} %get-tuple-element.82), channel_id=1, source_target_pairs={{256,321},{257,322},{258,323},{259,324},{260,325},{261,326},{262,3... | collective-permute-start | bytes 36872 | tf_op jit(solution)/shard_map/ppermute | solution.py:8
  48.7 3.4 %collective-permute-start.12 = (bf16[8,2,8,384]{3,2,1,0:T(8,128)(2,1)S(1)}, bf16[8,2,8,384]{3,2,1,0:T(8,128)(2,1)S(1)}, u32[]{:S(2)}, u32[]{:S(2)}) collective-permute-start(bf16[8,2,8,384]{3,2,1,0:T(8,128)(2,1)S(1)} %fusion.145), channel_id=1, source_target_pairs={{192,320},{193,321},{194,322},{195,323},{196,324},{197,325},{198,3... | collective-permute-start | bytes 294920 | tf_op jit(solution)/shard_map/ppermute | solution.py:8
  52.2 2.1 %collective-permute-start.22 = (bf16[8,2,8,384]{3,2,1,0:T(8,128)(2,1)S(1)}, bf16[8,2,8,384]{3,2,1,0:T(8,128)(2,1)S(1)}, u32[]{:S(2)}, u32[]{:S(2)}) collective-permute-start(bf16[8,2,8,384]{3,2,1,0:T(8,128)(2,1)S(1)} %fusion.146), channel_id=1, source_target_pairs={{320,384},{321,385},{322,386},{323,387},{324,388},{325,389},{326,3... | collective-permute-start | bytes 294920 | tf_op jit(solution)/shard_map/ppermute | solution.py:8
  52.9 1.3 %collective-permute-start.20 = (bf16[8,2,1,384]{3,2,1,0:T(2,128)(2,1)S(1)}, bf16[8,2,1,384]{3,2,1,0:T(2,128)(2,1)S(1)}, u32[]{:S(2)}, u32[]{:S(2)}) collective-permute-start(bf16[8,2,1,384]{3,2,1,0:T(2,128)(2,1)S(1)} %get-tuple-element.79), channel_id=1, source_target_pairs={{321,384},{322,385},{323,386},{324,387},{325,388},{326,389},{327,3... | collective-permute-start | bytes 36872 | tf_op jit(solution)/shard_map/ppermute | solution.py:8
  53.6 0.7 collective-permute-start.21
  57.0 2.8 %collective-permute-start.25 = (bf16[8,2,8,384]{3,2,1,0:T(8,128)(2,1)S(1)}, bf16[8,2,8,384]{3,2,1,0:T(8,128)(2,1)S(1)}, u32[]{:S(2)}, u32[]{:S(2)}) collective-permute-start(bf16[8,2,8,384]{3,2,1,0:T(8,128)(2,1)S(1)} %fusion.57), channel_id=1, source_target_pairs={{384,448},{385,449},{386,450},{387,451},{388,452},{389,453},{390,4... | collective-permute-start | bytes 294920 | tf_op jit(solution)/shard_map/ppermute | solution.py:8
  57.7 2.0 %collective-permute-start.23 = (bf16[8,2,1,384]{3,2,1,0:T(2,128)(2,1)S(1)}, bf16[8,2,1,384]{3,2,1,0:T(2,128)(2,1)S(1)}, u32[]{:S(2)}, u32[]{:S(2)}) collective-permute-start(bf16[8,2,1,384]{3,2,1,0:T(2,128)(2,1)S(1)} %get-tuple-element.77), channel_id=1, source_target_pairs={{385,448},{386,449},{387,450},{388,451},{389,452},{390,453},{391,4... | collective-permute-start | bytes 36872 | tf_op jit(solution)/shard_map/ppermute | solution.py:8
  58.4 1.4 %collective-permute-start.24 = (bf16[8,2,1,384]{3,2,1,0:T(2,128)(2,1)S(1)}, bf16[8,2,1,384]{3,2,1,0:T(2,128)(2,1)S(1)}, u32[]{:S(2)}, u32[]{:S(2)}) collective-permute-start(bf16[8,2,1,384]{3,2,1,0:T(2,128)(2,1)S(1)} %get-tuple-element.78), channel_id=1, source_target_pairs={{384,449},{385,450},{386,451},{387,452},{388,453},{389,454},{390,4... | collective-permute-start | bytes 36872 | tf_op jit(solution)/shard_map/ppermute | solution.py:8
  59.0 3.4 %collective-permute-start.19 = (bf16[8,2,8,384]{3,2,1,0:T(8,128)(2,1)S(1)}, bf16[8,2,8,384]{3,2,1,0:T(8,128)(2,1)S(1)}, u32[]{:S(2)}, u32[]{:S(2)}) collective-permute-start(bf16[8,2,8,384]{3,2,1,0:T(8,128)(2,1)S(1)} %fusion.146), channel_id=1, source_target_pairs={{320,448},{321,449},{322,450},{323,451},{324,452},{325,453},{326,4... | collective-permute-start | bytes 294920 | tf_op jit(solution)/shard_map/ppermute | solution.py:8

commit v7 on v4

--- a/solution.py
+++ b/solution.py
@@ -29,6 +29,12 @@
     flat = kernel.reshape(27 * channels, kernel.shape[-1])
     out = jnp.dot(joined, flat, preferred_element_type=jnp.float32)
     return out.reshape(frames, rows, cols, kernel.shape[-1])
+
+
+def edge_terms(left, right, kernel):
+    gap = jnp.zeros_like(left)
+    out = convolve(jnp.concatenate([left, gap, gap, right], axis=2), kernel)
+    return out[:, :, 0:1], out[:, :, 1:2]
 
 
 def local(latents, col_counts, conv_weight, norm_gain):
@@ -69,8 +75,20 @@
     current = stream
     residual = stream
     for stage in range(segments):
-        activated = activate(extend(current, left, right), gain)
-        conv_out = convolve(activated, kernel)
+        if stage == 0:
+            activated = jnp.pad(activate(current, gain), ((0, 0), (0, 0), (1, 1), (0, 0)))
+            conv_out = convolve(activated, kernel)
+            conv_out, left, right = lax.optimization_barrier((conv_out, left, right))
+            term_left, term_right = edge_terms(activate(left, gain), activate(right, gain), kernel)
+            slot_index = jnp.arange(col_count)[None, None, :, None]
+            conv_out = (
+                conv_out
+                + jnp.where(slot_index == 0, term_left, 0.0)
+                + jnp.where(slot_index == live_cols - 1, term_right, 0.0)
+            )
+        else:
+            activated = activate(extend(current, left, right), gain)
+            conv_out = convolve(activated, kernel)
         if stage % 2 == 0:
             produced = jnp.where(col_live, conv_out, 0.0).astype(jnp.bfloat16)
         else:

time: 106 us -> 113 us (1.066)
  matrix products: 12.2 us -> 20.1 us
  local copies, waits for them, and re-layouts: 9.42 us -> 7.32 us
  other arithmetic: 6.83 us -> 8.07 us
    dot_general x8 -> x9, matrix products: 12.2 us -> 20.1 us  [convolve(): out = jnp.dot(joined, flat, preferred_element_type=jnp.float32)]
    unnamed x69 -> x79, local copies, waits for them, and re-layouts: 5.04 us -> 3.65 us
    reduce_sum x8 -> x9, other arithmetic: 1.82 us -> 2.75 us  [activate(): jnp.mean(widened * widened, axis=-1, keepdims=True) + 1e-06]
    convert_element_type x8 -> x9, other arithmetic: 1.97 us -> 2.85 us  [activate(): return jax.nn.silu(scaled).astype(jnp.bfloat16)]
  transfers between devices with their start and end apart: 26 -> 26, of which waited for: 2 -> 2; matrix products, arithmetic and copies ran while one was open for 10% -> 15% of each run, Pallas kernels for 0% -> 0%
where the time goes in v7:
time: 113 us
  blocking collectives  43.2 us (38%)
  starting transfers between devices  27.7 us (25%)
  matrix products  20.1 us (18%)
  other arithmetic  8.07 us (7%)
  local copies, waits for them, and re-layouts  7.32 us (6%)
  between operations  4.93 us (4%)
  waiting for transfers between devices  1.45 us (1%)
    all_to_all x1, blocking collectives, local(): spread = lax.all_to_all(final, 'section', 0, 0, tiled=True)  43.2 us
    ppermute x26, starting transfers between devices, hop(): return lax.ppermute(block, axes, pairs)  27.7 us
    dot_general x9, matrix products, convolve(): out = jnp.dot(joined, flat, preferred_element_type=jnp.float32)  20.1 us
    unnamed x79, local copies, waits for them, and re-layouts  3.65 us
    convert_element_type x9, other arithmetic, activate(): return jax.nn.silu(scaled).astype(jnp.bfloat16)  2.85 us
    reduce_sum x9, other arithmetic, activate(): jnp.mean(widened * widened, axis=-1, keepdims=True) + 1e-06  2.75 us
  transfers between devices with their start and end apart: 26, of which 2 were waited for; matrix products, arithmetic and copies ran while one was open for 15% of the time, Pallas kernels for 0%

profile of v7, /device:TPU:256, one launch (start us, length us, event | category | flops | bytes accessed | tf_op | source)
XLA Modules:
  0.0 112.8 jit_solution(10823279775379696080)
XLA Ops:
  0.0 0.9 copy.9
  0.9 3.5 %collective-permute-start = (bf16[8,2,8,384]{3,0,2,1:T(8,128)(2,1)S(1)}, bf16[8,2,8,384]{3,0,2,1:T(8,128)(2,1)S(1)}, u32[]{:S(2)}, u32[]{:S(2)}) collective-permute-start(bf16[8,2,8,384]{3,0,2,1:T(8,128)(2,1)S(1)} %copy.9), channel_id=1, source_target_pairs={{0,1},{1,2},{2,3},{3,4},{4,5},{5,6},{6,7},{7,8},{8,9},{9,10},{10,1... | collective-permute-start | bytes 294920 | tf_op jit(solution)/shard_map/ppermute | solution.py:8
  4.4 5.7 %collective-permute-start.1 = (bf16[8,2,1,384]{3,0,2,1:T(8,128)(2,1)S(1)}, bf16[8,2,1,384]{3,0,2,1:T(8,128)(2,1)S(1)}, u32[]{:S(2)}, u32[]{:S(2)}) collective-permute-start(bf16[8,2,1,384]{3,0,2,1:T(8,128)(2,1)S(1)} %slice.485), channel_id=1, source_target_pairs={{1,0},{2,1},{3,2},{4,3},{5,4},{6,5},{7,6},{8,7},{9,8},{10,9},{11,1... | collective-permute-start | bytes 36872 | tf_op jit(solution)/shard_map/ppermute | solution.py:8
  10.1 1.4 %fusion.95 = (s32[1]{0:T(128)}, s32[1]{0:T(128)}) fusion(s32[64]{0:T(128)} %param.5, s32[]{:T(128)S(6)} %max.3, s32[]{:T(128)S(6)} %select_n.74), kind=kLoop, calls=%fused_computation.281 | loop fusion | bytes 24 | tf_op jit(solution)/shard_map/dynamic_slice | solution.py:71
  12.2 0.7 iota_compare_fusion.3
  15.6 0.7 convert_reduce_fusion
  16.3 1.1 fusion.61
  17.4 1.0 fusion.68
  19.0 4.8 %fusion.96 = f32[8,2,8,384]{3,2,1,0:T(8,128)S(1)} fusion(bf16[8,2,8,10368]{3,2,1,0:T(8,128)(2,1)S(1)} %slice_dynamic-update-slice_fusion.63, bf16[10368,384,1,1]{1,0,3,2:T(8,128)(2,1)} %bitcast.52), kind=kOutput, calls=%fused_computation.282 | convolution fusion | flops 1019215872 | bytes 10813440 | tf_op jit(solution)/shard_map/dot_general | solution.py:30
  24.5 4.6 %fusion.97 = f32[8,2,2,384]{3,0,2,1:T(8,128)S(1)} fusion(bf16[8,2,2,10368]{3,0,2,1:T(8,128)(2,1)S(1)} %constant_dynamic-update-slice_fusion, bf16[10368,384,1,1]{1,0,3,2:T(8,128)(2,1)} %bitcast.53), kind=kOutput, calls=%fused_computation.283 | convolution fusion | flops 254803968 | bytes 8675328 | tf_op jit(solution)/shard_map/dot_general | solution.py:30
  29.4 1.6 %collective-permute-start.4 = (bf16[8,2,8,384]{3,2,1,0:T(8,128)(2,1)S(1)}, bf16[8,2,8,384]{3,2,1,0:T(8,128)(2,1)S(1)}, u32[]{:S(2)}, u32[]{:S(2)}) collective-permute-start(bf16[8,2,8,384]{3,2,1,0:T(8,128)(2,1)S(1)} %select_convert_fusion), channel_id=1, source_target_pairs={{0,64},{1,65},{2,66},{3,67},{4,68},{5,69},{6,70},{7,71},{8,72},{9,... | collective-permute-start | bytes 294920 | tf_op jit(solution)/shard_map/ppermute | solution.py:8
  31.0 1.3 %collective-permute-start.2 = (bf16[8,2,1,384]{3,2,1,0:T(2,128)(2,1)S(1)}, bf16[8,2,1,384]{3,2,1,0:T(2,128)(2,1)S(1)}, u32[]{:S(2)}, u32[]{:S(2)}) collective-permute-start(bf16[8,2,1,384]{3,2,1,0:T(2,128)(2,1)S(1)} %get-tuple-element.44), channel_id=1, source_target_pairs={{1,64},{2,65},{3,66},{4,67},{5,68},{6,69},{7,70},{8,71},{9,72},{10... | collective-permute-start | bytes 36872 | tf_op jit(solution)/shard_map/ppermute | solution.py:8
  32.3 1.3 %collective-permute-start.3 = (bf16[8,2,1,384]{3,2,1,0:T(2,128)(2,1)S(1)}, bf16[8,2,1,384]{3,2,1,0:T(2,128)(2,1)S(1)}, u32[]{:S(2)}, u32[]{:S(2)}) collective-permute-start(bf16[8,2,1,384]{3,2,1,0:T(2,128)(2,1)S(1)} %get-tuple-element.45), channel_id=1, source_target_pairs={{0,65},{1,66},{2,67},{3,68},{4,69},{5,70},{6,71},{7,72},{8,73},{9,... | collective-permute-start | bytes 36872 | tf_op jit(solution)/shard_map/ppermute | solution.py:8
  33.8 1.3 %collective-permute-done.3 = bf16[8,2,1,384]{3,2,1,0:T(2,128)(2,1)S(1)} collective-permute-done((bf16[8,2,1,384]{3,2,1,0:T(2,128)(2,1)S(1)}, bf16[8,2,1,384]{3,2,1,0:T(2,128)(2,1)S(1)}, u32[]{:S(2)}, u32[]{:S(2)}) %collective-permute-start.3) | collective-permute-done | bytes 12320 | tf_op jit(solution)/shard_map/ppermute | solution.py:8
  36.7 1.5 %fusion.4 = bf16[8,2,8,384]{3,2,1,0:T(8,128)(2,1)S(1)} fusion(bf16[8,2,8,10368]{3,2,1,0:T(8,128)(2,1)S(1)} %slice_dynamic-update-slice_fusion.54, bf16[10368,384,1,1]{1,0,3,2:T(8,128)(2,1)S(1)} %bitcast.56, pred[8]{0:T(512)(128)(4,1)S(1)} %iota_compare_fusion.3, bf16[8,2,8,384]{3,2,1,0:T(8,128)(2,1)S(1)} %copy-done), kind=kOutput, calls=%fused_computation.8 | convolution fusion | flops 1019461632 | bytes 10813448 | tf_op jit(solution)/shard_map/dot_general | solution.py:30
  38.2 0.7 collective-permute-start.8
  39.6 0.7 collective-permute-start.7
  41.4 1.5 %fusion.1 = bf16[8,2,8,384]{3,2,1,0:T(8,128)(2,1)S(1)} fusion(bf16[8,2,8,10368]{3,2,1,0:T(8,128)(2,1)S(1)} %slice_dynamic-update-slice_fusion.45, bf16[10368,384,1,1]{1,0,3,2:T(8,128)(2,1)S(1)} %bitcast.57, pred[8]{0:T(512)(128)(4,1)S(1)} %iota_compare_fusion.3), kind=kOutput, calls=%fused_computation.5 | convolution fusion | flops 1019314176 | bytes 10715144 | tf_op jit(solution)/shard_map/dot_general | solution.py:30
  42.9 0.7 collective-permute-start.11
  45.0 0.8 collective-permute-start.5
  46.9 1.5 %fusion.69 = bf16[8,2,8,384]{3,2,1,0:T(8,128)(2,1)S(1)} fusion(bf16[8,2,8,384]{3,2,1,0:T(8,128)(2,1)S(1)} %collective-permute-done.5, pred[8]{0:T(512)(128)(4,1)S(1)} %iota_compare_fusion.3, bf16[8,2,8,10368]{3,2,1,0:T(8,128)(2,1)S(1)} %slice_dynamic-update-slice_fusion.36, bf16[10368,384,1,1]{1,0,3,2:T(8,128)(2,1)S(1)} %bitcast.58), kind=kOutput, calls=%fused_computation.217 | convolution fusion | flops 1019412480 | bytes 10813448 | tf_op jit(solution)/shard_map/dot_general | solution.py:30
  48.5 0.7 collective-permute-start.15
  51.6 1.5 %fusion.2 = bf16[8,2,8,384]{3,2,1,0:T(8,128)(2,1)S(1)} fusion(bf16[8,2,8,10368]{3,2,1,0:T(8,128)(2,1)S(1)} %slice_dynamic-update-slice_fusion.27, bf16[10368,384,1,1]{1,0,3,2:T(8,128)(2,1)S(1)} %bitcast.59, pred[8]{0:T(512)(128)(4,1)S(1)} %iota_compare_fusion.3), kind=kOutput, calls=%fused_computation.6 | convolution fusion | flops 1019314176 | bytes 10715144 | tf_op jit(solution)/shard_map/dot_general | solution.py:30
  53.1 0.7 collective-permute-start.18
  55.2 0.7 collective-permute-start.12
  57.0 1.5 %fusion.98 = f32[8,2,8,384]{3,2,1,0:T(8,128)S(1)} fusion(bf16[8,2,8,10368]{3,2,1,0:T(8,128)(2,1)S(1)} %slice_dynamic-update-slice_fusion.18, bf16[10368,384,1,1]{1,0,3,2:T(8,128)(2,1)S(1)} %bitcast.60), kind=kOutput, calls=%fused_computation.284 | convolution fusion | flops 1019215872 | bytes 10813440 | tf_op jit(solution)/shard_map/dot_general | solution.py:30
  58.6 0.7 collective-permute-start.22
  61.7 1.5 %fusion.3 = bf16[8,2,8,384]{3,2,1,0:T(8,128)(2,1)S(1)} fusion(bf16[8,2,8,10368]{3,2,1,0:T(8,128)(2,1)S(1)} %slice_dynamic-update-slice_fusion.9, bf16[10368,384,1,1]{1,0,3,2:T(8,128)(2,1)S(1)} %bitcast.61, pred[8]{0:T(512)(128)(4,1)S(1)} %iota_compare_fusion.3), kind=kOutput, calls=%fused_computation.7 | convolution fusion | flops 1019314176 | bytes 10715144 | tf_op jit(solution)/shard_map/dot_general | solution.py:30
  63.3 0.7 collective-permute-start.25
  65.3 0.9 collective-permute-start.19
  67.3 1.5 %fusion.99 = f32[8,2,8,384]{3,2,1,0:T(8,128)S(1)} fusion(bf16[8,2,8,10368]{3,2,1,0:T(8,128)(2,1)S(1)} %slice_dynamic-update-slice_fusion, bf16[10368,384,1,1]{1,0,3,2:T(8,128)(2,1)S(1)} %bitcast.62), kind=kOutput, calls=%fused_computation.285 | convolution fusion | flops 1019215872 | bytes 10813440 | tf_op jit(solution)/shard_map/dot_general | solution.py:30
  69.0 43.2 %all_to_all.5 = bf16[8,2,8,384]{3,2,1,0:T(8,128)(2,1)S(1)} all-to-all(bf16[8,2,8,384]{3,2,1,0:T(8,128)(2,1)S(1)} %fusion.71), channel_id=1, replica_groups=mesh['section'=8,'tile'=64] {'section'}, dimensions={0} | all-to-all | bytes 196608 | tf_op jit(solution)/shard_map/all_to_all | solution.py:107
  (204 shorter events, 17.0 us)
Async XLA Ops:
  0.9 22.9 %collective-permute-start = (bf16[8,2,8,384]{3,0,2,1:T(8,128)(2,1)S(1)}, bf16[8,2,8,384]{3,0,2,1:T(8,128)(2,1)S(1)}, u32[]{:S(2)}, u32[]{:S(2)}) collective-permute-start(bf16[8,2,8,384]{3,0,2,1:T(8,128)(2,1)S(1)} %copy.9), channel_id=1, source_target_pairs={{0,1},{1,2},{2,3},{3,4},{4,5},{5,6},{6,7},{7,8},{8,9},{9,10},{10,1... | collective-permute-start | bytes 294920 | tf_op jit(solution)/shard_map/ppermute | solution.py:8
  4.4 19.4 %collective-permute-start.1 = (bf16[8,2,1,384]{3,0,2,1:T(8,128)(2,1)S(1)}, bf16[8,2,1,384]{3,0,2,1:T(8,128)(2,1)S(1)}, u32[]{:S(2)}, u32[]{:S(2)}) collective-permute-start(bf16[8,2,1,384]{3,0,2,1:T(8,128)(2,1)S(1)} %slice.485), channel_id=1, source_target_pairs={{1,0},{2,1},{3,2},{4,3},{5,4},{6,5},{7,6},{8,7},{9,8},{10,9},{11,1... | collective-permute-start | bytes 36872 | tf_op jit(solution)/shard_map/ppermute | solution.py:8
  24.5 11.6 %slice-start = ((s8[7962624]{0:T(1024)(128)(4,1)}), s8[4194304]{0:T(1024)(128)(4,1)S(1)}, s32[]{:S(2)}) async-start(s8[7962624]{0:T(1024)(128)(4,1)} %bitcast.54), calls=%async_computation.1 | async-start | bytes 8388608
  29.2 7.0 %slice-start.1 = ((s8[7962624]{0:T(1024)(128)(4,1)}), s8[3768320]{0:T(1024)(128)(4,1)S(1)}, s32[]{:S(2)}) async-start(s8[7962624]{0:T(1024)(128)(4,1)} %bitcast.54), calls=%async_computation.2 | async-start | bytes 7536640
  29.4 5.7 %collective-permute-start.4 = (bf16[8,2,8,384]{3,2,1,0:T(8,128)(2,1)S(1)}, bf16[8,2,8,384]{3,2,1,0:T(8,128)(2,1)S(1)}, u32[]{:S(2)}, u32[]{:S(2)}) collective-permute-start(bf16[8,2,8,384]{3,2,1,0:T(8,128)(2,1)S(1)} %select_convert_fusion), channel_id=1, source_target_pairs={{0,64},{1,65},{2,66},{3,67},{4,68},{5,69},{6,70},{7,71},{8,72},{9,... | collective-permute-start | bytes 294920 | tf_op jit(solution)/shard_map/ppermute | solution.py:8
  31.0 2.8 %collective-permute-start.2 = (bf16[8,2,1,384]{3,2,1,0:T(2,128)(2,1)S(1)}, bf16[8,2,1,384]{3,2,1,0:T(2,128)(2,1)S(1)}, u32[]{:S(2)}, u32[]{:S(2)}) collective-permute-start(bf16[8,2,1,384]{3,2,1,0:T(2,128)(2,1)S(1)} %get-tuple-element.44), channel_id=1, source_target_pairs={{1,64},{2,65},{3,66},{4,67},{5,68},{6,69},{7,70},{8,71},{9,72},{10... | collective-permute-start | bytes 36872 | tf_op jit(solution)/shard_map/ppermute | solution.py:8
  32.3 2.8 %collective-permute-start.3 = (bf16[8,2,1,384]{3,2,1,0:T(2,128)(2,1)S(1)}, bf16[8,2,1,384]{3,2,1,0:T(2,128)(2,1)S(1)}, u32[]{:S(2)}, u32[]{:S(2)}) collective-permute-start(bf16[8,2,1,384]{3,2,1,0:T(2,128)(2,1)S(1)} %get-tuple-element.45), channel_id=1, source_target_pairs={{0,65},{1,66},{2,67},{3,68},{4,69},{5,70},{6,71},{7,72},{8,73},{9,... | collective-permute-start | bytes 36872 | tf_op jit(solution)/shard_map/ppermute | solution.py:8
  35.8 0.9 copy-start
  38.2 2.1 %collective-permute-start.8 = (bf16[8,2,8,384]{3,2,1,0:T(8,128)(2,1)S(1)}, bf16[8,2,8,384]{3,2,1,0:T(8,128)(2,1)S(1)}, u32[]{:S(2)}, u32[]{:S(2)}) collective-permute-start(bf16[8,2,8,384]{3,2,1,0:T(8,128)(2,1)S(1)} %fusion.4), channel_id=1, source_target_pairs={{64,128},{65,129},{66,130},{67,131},{68,132},{69,133},{70,134},{71... | collective-permute-start | bytes 294920 | tf_op jit(solution)/shard_map/ppermute | solution.py:8
  38.9 1.3 %collective-permute-start.6 = (bf16[8,2,1,384]{3,2,1,0:T(2,128)(2,1)S(1)}, bf16[8,2,1,384]{3,2,1,0:T(2,128)(2,1)S(1)}, u32[]{:S(2)}, u32[]{:S(2)}) collective-permute-start(bf16[8,2,1,384]{3,2,1,0:T(2,128)(2,1)S(1)} %get-tuple-element.42), channel_id=1, source_target_pairs={{65,128},{66,129},{67,130},{68,131},{69,132},{70,133},{71,134},{72... | collective-permute-start | bytes 36872 | tf_op jit(solution)/shard_map/ppermute | solution.py:8
  39.6 0.7 collective-permute-start.7
  42.9 3.0 %collective-permute-start.11 = (bf16[8,2,8,384]{3,2,1,0:T(8,128)(2,1)S(1)}, bf16[8,2,8,384]{3,2,1,0:T(8,128)(2,1)S(1)}, u32[]{:S(2)}, u32[]{:S(2)}) collective-permute-start(bf16[8,2,8,384]{3,2,1,0:T(8,128)(2,1)S(1)} %fusion.1), channel_id=1, source_target_pairs={{128,192},{129,193},{130,194},{131,195},{132,196},{133,197},{134,1... | collective-permute-start | bytes 294920 | tf_op jit(solution)/shard_map/ppermute | solution.py:8
  43.6 2.2 %collective-permute-start.9 = (bf16[8,2,1,384]{3,2,1,0:T(2,128)(2,1)S(1)}, bf16[8,2,1,384]{3,2,1,0:T(2,128)(2,1)S(1)}, u32[]{:S(2)}, u32[]{:S(2)}) collective-permute-start(bf16[8,2,1,384]{3,2,1,0:T(2,128)(2,1)S(1)} %get-tuple-element.40), channel_id=1, source_target_pairs={{129,192},{130,193},{131,194},{132,195},{133,196},{134,197},{135,1... | collective-permute-start | bytes 36872 | tf_op jit(solution)/shard_map/ppermute | solution.py:8
  44.3 1.6 %collective-permute-start.10 = (bf16[8,2,1,384]{3,2,1,0:T(2,128)(2,1)S(1)}, bf16[8,2,1,384]{3,2,1,0:T(2,128)(2,1)S(1)}, u32[]{:S(2)}, u32[]{:S(2)}) collective-permute-start(bf16[8,2,1,384]{3,2,1,0:T(2,128)(2,1)S(1)} %get-tuple-element.41), channel_id=1, source_target_pairs={{128,193},{129,194},{130,195},{131,196},{132,197},{133,198},{134,1... | collective-permute-start | bytes 36872 | tf_op jit(solution)/shard_map/ppermute | solution.py:8
  45.0 1.9 %collective-permute-start.5 = (bf16[8,2,8,384]{3,2,1,0:T(8,128)(2,1)S(1)}, bf16[8,2,8,384]{3,2,1,0:T(8,128)(2,1)S(1)}, u32[]{:S(2)}, u32[]{:S(2)}) collective-permute-start(bf16[8,2,8,384]{3,2,1,0:T(8,128)(2,1)S(1)} %fusion.4), channel_id=1, source_target_pairs={{64,192},{65,193},{66,194},{67,195},{68,196},{69,197},{70,198},{71... | collective-permute-start | bytes 294920 | tf_op jit(solution)/shard_map/ppermute | solution.py:8
  48.5 2.1 %collective-permute-start.15 = (bf16[8,2,8,384]{3,2,1,0:T(8,128)(2,1)S(1)}, bf16[8,2,8,384]{3,2,1,0:T(8,128)(2,1)S(1)}, u32[]{:S(2)}, u32[]{:S(2)}) collective-permute-start(bf16[8,2,8,384]{3,2,1,0:T(8,128)(2,1)S(1)} %fusion.69), channel_id=1, source_target_pairs={{192,256},{193,257},{194,258},{195,259},{196,260},{197,261},{198,2... | collective-permute-start | bytes 294920 | tf_op jit(solution)/shard_map/ppermute | solution.py:8
  49.2 1.3 %collective-permute-start.13 = (bf16[8,2,1,384]{3,2,1,0:T(2,128)(2,1)S(1)}, bf16[8,2,1,384]{3,2,1,0:T(2,128)(2,1)S(1)}, u32[]{:S(2)}, u32[]{:S(2)}) collective-permute-start(bf16[8,2,1,384]{3,2,1,0:T(2,128)(2,1)S(1)} %get-tuple-element.38), channel_id=1, source_target_pairs={{193,256},{194,257},{195,258},{196,259},{197,260},{198,261},{199,2... | collective-permute-start | bytes 36872 | tf_op jit(solution)/shard_map/ppermute | solution.py:8
  49.8 0.7 collective-permute-start.14
  53.1 2.8 %collective-permute-start.18 = (bf16[8,2,8,384]{3,2,1,0:T(8,128)(2,1)S(1)}, bf16[8,2,8,384]{3,2,1,0:T(8,128)(2,1)S(1)}, u32[]{:S(2)}, u32[]{:S(2)}) collective-permute-start(bf16[8,2,8,384]{3,2,1,0:T(8,128)(2,1)S(1)} %fusion.2), channel_id=1, source_target_pairs={{256,320},{257,321},{258,322},{259,323},{260,324},{261,325},{262,3... | collective-permute-start | bytes 294920 | tf_op jit(solution)/shard_map/ppermute | solution.py:8
  53.9 2.0 %collective-permute-start.16 = (bf16[8,2,1,384]{3,2,1,0:T(2,128)(2,1)S(1)}, bf16[8,2,1,384]{3,2,1,0:T(2,128)(2,1)S(1)}, u32[]{:S(2)}, u32[]{:S(2)}) collective-permute-start(bf16[8,2,1,384]{3,2,1,0:T(2,128)(2,1)S(1)} %get-tuple-element.36), channel_id=1, source_target_pairs={{257,320},{258,321},{259,322},{260,323},{261,324},{262,325},{263,3... | collective-permute-start | bytes 36872 | tf_op jit(solution)/shard_map/ppermute | solution.py:8
  54.5 1.4 %collective-permute-start.17 = (bf16[8,2,1,384]{3,2,1,0:T(2,128)(2,1)S(1)}, bf16[8,2,1,384]{3,2,1,0:T(2,128)(2,1)S(1)}, u32[]{:S(2)}, u32[]{:S(2)}) collective-permute-start(bf16[8,2,1,384]{3,2,1,0:T(2,128)(2,1)S(1)} %get-tuple-element.37), channel_id=1, source_target_pairs={{256,321},{257,322},{258,323},{259,324},{260,325},{261,326},{262,3... | collective-permute-start | bytes 36872 | tf_op jit(solution)/shard_map/ppermute | solution.py:8
  55.2 3.3 %collective-permute-start.12 = (bf16[8,2,8,384]{3,2,1,0:T(8,128)(2,1)S(1)}, bf16[8,2,8,384]{3,2,1,0:T(8,128)(2,1)S(1)}, u32[]{:S(2)}, u32[]{:S(2)}) collective-permute-start(bf16[8,2,8,384]{3,2,1,0:T(8,128)(2,1)S(1)} %fusion.69), channel_id=1, source_target_pairs={{192,320},{193,321},{194,322},{195,323},{196,324},{197,325},{198,3... | collective-permute-start | bytes 294920 | tf_op jit(solution)/shard_map/ppermute | solution.py:8
  58.6 2.1 %collective-permute-start.22 = (bf16[8,2,8,384]{3,2,1,0:T(8,128)(2,1)S(1)}, bf16[8,2,8,384]{3,2,1,0:T(8,128)(2,1)S(1)}, u32[]{:S(2)}, u32[]{:S(2)}) collective-permute-start(bf16[8,2,8,384]{3,2,1,0:T(8,128)(2,1)S(1)} %fusion.70), channel_id=1, source_target_pairs={{320,384},{321,385},{322,386},{323,387},{324,388},{325,389},{326,3... | collective-permute-start | bytes 294920 | tf_op jit(solution)/shard_map/ppermute | solution.py:8
  59.3 1.3 %collective-permute-start.20 = (bf16[8,2,1,384]{3,2,1,0:T(2,128)(2,1)S(1)}, bf16[8,2,1,384]{3,2,1,0:T(2,128)(2,1)S(1)}, u32[]{:S(2)}, u32[]{:S(2)}) collective-permute-start(bf16[8,2,1,384]{3,2,1,0:T(2,128)(2,1)S(1)} %get-tuple-element.34), channel_id=1, source_target_pairs={{321,384},{322,385},{323,386},{324,387},{325,388},{326,389},{327,3... | collective-permute-start | bytes 36872 | tf_op jit(solution)/shard_map/ppermute | solution.py:8
  60.0 0.7 collective-permute-start.21
  63.3 3.0 %collective-permute-start.25 = (bf16[8,2,8,384]{3,2,1,0:T(8,128)(2,1)S(1)}, bf16[8,2,8,384]{3,2,1,0:T(8,128)(2,1)S(1)}, u32[]{:S(2)}, u32[]{:S(2)}) collective-permute-start(bf16[8,2,8,384]{3,2,1,0:T(8,128)(2,1)S(1)} %fusion.3), channel_id=1, source_target_pairs={{384,448},{385,449},{386,450},{387,451},{388,452},{389,453},{390,4... | collective-permute-start | bytes 294920 | tf_op jit(solution)/shard_map/ppermute | solution.py:8
  64.0 2.2 %collective-permute-start.23 = (bf16[8,2,1,384]{3,2,1,0:T(2,128)(2,1)S(1)}, bf16[8,2,1,384]{3,2,1,0:T(2,128)(2,1)S(1)}, u32[]{:S(2)}, u32[]{:S(2)}) collective-permute-start(bf16[8,2,1,384]{3,2,1,0:T(2,128)(2,1)S(1)} %get-tuple-element.32), channel_id=1, source_target_pairs={{385,448},{386,449},{387,450},{388,451},{389,452},{390,453},{391,4... | collective-permute-start | bytes 36872 | tf_op jit(solution)/shard_map/ppermute | solution.py:8
  64.7 1.6 %collective-permute-start.24 = (bf16[8,2,1,384]{3,2,1,0:T(2,128)(2,1)S(1)}, bf16[8,2,1,384]{3,2,1,0:T(2,128)(2,1)S(1)}, u32[]{:S(2)}, u32[]{:S(2)}) collective-permute-start(bf16[8,2,1,384]{3,2,1,0:T(2,128)(2,1)S(1)} %get-tuple-element.33), channel_id=1, source_target_pairs={{384,449},{385,450},{386,451},{387,452},{388,453},{389,454},{390,4... | collective-permute-start | bytes 36872 | tf_op jit(solution)/shard_map/ppermute | solution.py:8
  65.3 3.5 %collective-permute-start.19 = (bf16[8,2,8,384]{3,2,1,0:T(8,128)(2,1)S(1)}, bf16[8,2,8,384]{3,2,1,0:T(8,128)(2,1)S(1)}, u32[]{:S(2)}, u32[]{:S(2)}) collective-permute-start(bf16[8,2,8,384]{3,2,1,0:T(8,128)(2,1)S(1)} %fusion.70), channel_id=1, source_target_pairs={{320,448},{321,449},{322,450},{323,451},{324,452},{325,453},{326,4... | collective-permute-start | bytes 294920 | tf_op jit(solution)/shard_map/ppermute | solution.py:8

commit v8 on v4

--- a/solution.py
+++ b/solution.py
@@ -14,11 +14,23 @@
     return jax.nn.silu(scaled).astype(jnp.bfloat16)
 
 
-def convolve(activated, kernel):
-    frames, rows, cols_ext, channels = activated.shape
+def norm_factor(values):
+    widened = values.astype(jnp.float32)
+    return lax.rsqrt(jnp.mean(widened * widened, axis=-1, keepdims=True) + 1e-06)
+
+
+def apply_norm(values, factor, gain):
+    return jax.nn.silu(values.astype(jnp.float32) * factor * gain).astype(jnp.bfloat16)
+
+
+def convolve(raw, factor, gain, kernel):
+    frames, rows, cols_ext, channels = raw.shape
     cols = cols_ext - 2
-    padded = jnp.pad(activated, ((2, 0), (1, 1), (0, 0), (0, 0)))
-    shifted = jnp.concatenate([padded[:, :, k : k + cols] for k in range(3)], axis=-1)
+    raw = jnp.pad(raw, ((2, 0), (1, 1), (0, 0), (0, 0)))
+    factor = jnp.pad(factor, ((2, 0), (1, 1), (0, 0), (0, 0)))
+    shifted = jnp.concatenate(
+        [apply_norm(raw[:, :, k : k + cols], factor[:, :, k : k + cols], gain) for k in range(3)], axis=-1
+    )
     shifted = lax.optimization_barrier(shifted)
     taps = [
         shifted[frame_tap : frame_tap + frames, row_tap : row_tap + rows]
@@ -69,8 +81,8 @@
     current = stream
     residual = stream
     for stage in range(segments):
-        activated = activate(extend(current, left, right), gain)
-        conv_out = convolve(activated, kernel)
+        wide = extend(current, left, right)
+        conv_out = convolve(wide, norm_factor(wide), gain, kernel)
         if stage % 2 == 0:
             produced = jnp.where(col_live, conv_out, 0.0).astype(jnp.bfloat16)
         else:

time: 106 us -> 108 us (1.019)
  other arithmetic: 6.83 us -> 9.07 us
    convert_element_type x8, other arithmetic: 1.97 us -> 4.08 us  [apply_norm(): jax.nn.silu(values.astype(jnp.float32) * factor * gain).astype(jnp.bfloat16)]
  transfers between devices with their start and end apart: 26 -> 26, of which waited for: 2 -> 2; matrix products, arithmetic and copies ran while one was open for 10% -> 11% of each run, Pallas kernels for 0% -> 0%
where the time goes in v8:
time: 108 us; the launch traced here: 107 us
  blocking collectives  43.2 us (40%)
  starting transfers between devices  27.4 us (25%)
  matrix products  12.2 us (11%)
  other arithmetic  9.07 us (8%)
  local copies, waits for them, and re-layouts  8.92 us (8%)
  between operations  4.54 us (4%)
  waiting for transfers between devices  1.54 us (1%)
    all_to_all x1, blocking collectives, local(): spread = lax.all_to_all(final, 'section', 0, 0, tiled=True)  43.2 us
    ppermute x26, starting transfers between devices, hop(): return lax.ppermute(block, axes, pairs)  27.4 us
    dot_general x8, matrix products, convolve(): out = jnp.dot(joined, flat, preferred_element_type=jnp.float32)  12.2 us
    unnamed x69, local copies, waits for them, and re-layouts  4.53 us
    convert_element_type x8, other arithmetic, apply_norm(): jax.nn.silu(values.astype(jnp.float32) * factor * gain).astype(jnp.bfloat16)  4.08 us
  transfers between devices with their start and end apart: 26, of which 2 were waited for; matrix products, arithmetic and copies ran while one was open for 11% of the time, Pallas kernels for 0%

profile of v8, /device:TPU:256, one launch (start us, length us, event | category | flops | bytes accessed | tf_op | source)
XLA Modules:
  0.0 106.9 jit_solution(9066816009413004832)
XLA Ops:
  0.0 3.5 %collective-permute-start.1 = (bf16[8,2,8,384]{3,2,1,0:T(8,128)(2,1)}, bf16[8,2,8,384]{3,2,1,0:T(8,128)(2,1)S(1)}, u32[]{:S(2)}, u32[]{:S(2)}) collective-permute-start(bf16[8,2,8,384]{3,2,1,0:T(8,128)(2,1)} %param.4), channel_id=1, source_target_pairs={{0,1},{1,2},{2,3},{3,4},{4,5},{5,6},{6,7},{7,8},{8,9},{9,10},{10,1... | collective-permute-start | bytes 294920 | tf_op jit(solution)/shard_map/ppermute | solution.py:8
  3.5 0.9 slice.387
  4.4 5.7 %collective-permute-start = (bf16[8,2,1,384]{3,0,2,1:T(8,128)(2,1)S(1)}, bf16[8,2,1,384]{3,0,2,1:T(8,128)(2,1)S(1)}, u32[]{:S(2)}, u32[]{:S(2)}) collective-permute-start(bf16[8,2,1,384]{3,0,2,1:T(8,128)(2,1)S(1)} %copy.22), channel_id=1, source_target_pairs={{1,0},{2,1},{3,2},{4,3},{5,4},{6,5},{7,6},{8,7},{9,8},{10,9},{11,1... | collective-permute-start | bytes 36872 | tf_op jit(solution)/shard_map/ppermute | solution.py:8
  10.1 1.4 %fusion.40 = (s32[1]{0:T(128)}, s32[1]{0:T(128)}) fusion(s32[64]{0:T(128)} %param.5, s32[]{:T(128)S(6)} %max.3, s32[]{:T(128)S(6)} %select_n.70), kind=kLoop, calls=%fused_computation.243 | loop fusion | bytes 24 | tf_op jit(solution)/shard_map/dynamic_slice | solution.py:77
  12.8 0.7 convert_reduce_fusion
  13.5 1.0 broadcast_select_fusion
  18.5 2.0 %copy-done = bf16[1,3,3,1152,384]{4,3,2,1,0:T(8,128)(2,1)S(1)} copy-done((bf16[1,3,3,1152,384]{4,3,2,1,0:T(8,128)(2,1)S(1)}, bf16[1,3,3,1152,384]{4,3,2,1,0:T(8,128)(2,1)}, u32[]{:S(2)}) %copy-start) | copy-done | bytes 7962648
  20.5 1.5 %fusion = bf16[8,2,8,384]{3,2,1,0:T(8,128)(2,1)S(1)} fusion(bf16[8,2,8,10368]{3,2,1,0:T(8,128)(2,1)S(1)} %slice_dynamic-update-slice_fusion.63, bf16[10368,384,1,1]{1,0,3,2:T(8,128)(2,1)S(1)} %bitcast.111, pred[8]{0:T(512)(128)(4,1)S(1)} %iota_compare_fusion.1), kind=kOutput, calls=%fused_computation.5 | convolution fusion | flops 1019314176 | bytes 10715144 | tf_op jit(solution)/shard_map/dot_general | solution.py:42
  22.0 1.3 %collective-permute-start.4 = (bf16[8,2,8,384]{3,2,1,0:T(8,128)(2,1)S(1)}, bf16[8,2,8,384]{3,2,1,0:T(8,128)(2,1)S(1)}, u32[]{:S(2)}, u32[]{:S(2)}) collective-permute-start(bf16[8,2,8,384]{3,2,1,0:T(8,128)(2,1)S(1)} %fusion), channel_id=1, source_target_pairs={{0,64},{1,65},{2,66},{3,67},{4,68},{5,69},{6,70},{7,71},{8,72},{9,... | collective-permute-start | bytes 294920 | tf_op jit(solution)/shard_map/ppermute | solution.py:8
  23.4 1.3 %collective-permute-start.2 = (bf16[8,2,1,384]{3,2,1,0:T(2,128)(2,1)S(1)}, bf16[8,2,1,384]{3,2,1,0:T(2,128)(2,1)S(1)}, u32[]{:S(2)}, u32[]{:S(2)}) collective-permute-start(bf16[8,2,1,384]{3,2,1,0:T(2,128)(2,1)S(1)} %get-tuple-element.57), channel_id=1, source_target_pairs={{1,64},{2,65},{3,66},{4,67},{5,68},{6,69},{7,70},{8,71},{9,72},{10... | collective-permute-start | bytes 36872 | tf_op jit(solution)/shard_map/ppermute | solution.py:8
  24.6 1.3 %collective-permute-start.3 = (bf16[8,2,1,384]{3,2,1,0:T(2,128)(2,1)S(1)}, bf16[8,2,1,384]{3,2,1,0:T(2,128)(2,1)S(1)}, u32[]{:S(2)}, u32[]{:S(2)}) collective-permute-start(bf16[8,2,1,384]{3,2,1,0:T(2,128)(2,1)S(1)} %get-tuple-element.58), channel_id=1, source_target_pairs={{0,65},{1,66},{2,67},{3,68},{4,69},{5,70},{6,71},{7,72},{8,73},{9,... | collective-permute-start | bytes 36872 | tf_op jit(solution)/shard_map/ppermute | solution.py:8
  26.2 1.3 %collective-permute-done.3 = bf16[8,2,1,384]{3,2,1,0:T(2,128)(2,1)S(1)} collective-permute-done((bf16[8,2,1,384]{3,2,1,0:T(2,128)(2,1)S(1)}, bf16[8,2,1,384]{3,2,1,0:T(2,128)(2,1)S(1)}, u32[]{:S(2)}, u32[]{:S(2)}) %collective-permute-start.3) | collective-permute-done | bytes 12320 | tf_op jit(solution)/shard_map/ppermute | solution.py:8
  29.3 1.5 %fusion.5 = bf16[8,2,8,384]{3,2,1,0:T(8,128)(2,1)S(1)} fusion(bf16[8,2,8,10368]{3,2,1,0:T(8,128)(2,1)S(1)} %slice_dynamic-update-slice_fusion.54, bf16[10368,384,1,1]{1,0,3,2:T(8,128)(2,1)S(1)} %bitcast.112, pred[8]{0:T(512)(128)(4,1)S(1)} %iota_compare_fusion.1, bf16[8,2,8,384]{3,2,1,0:T(8,128)(2,1)S(1)} %copy-done.1), kind=kOutput, calls=%fused_computation.10 | convolution fusion | flops 1019461632 | bytes 10813448 | tf_op jit(solution)/shard_map/dot_general | solution.py:42
  30.8 0.7 collective-permute-start.8
  31.5 0.7 collective-permute-start.6
  34.2 1.5 %fusion.2 = bf16[8,2,8,384]{3,2,1,0:T(8,128)(2,1)S(1)} fusion(bf16[8,2,8,10368]{3,2,1,0:T(8,128)(2,1)S(1)} %slice_dynamic-update-slice_fusion.45, bf16[10368,384,1,1]{1,0,3,2:T(8,128)(2,1)S(1)} %bitcast.113, pred[8]{0:T(512)(128)(4,1)S(1)} %iota_compare_fusion.1), kind=kOutput, calls=%fused_computation.7 | convolution fusion | flops 1019314176 | bytes 10715144 | tf_op jit(solution)/shard_map/dot_general | solution.py:42
  35.8 0.7 collective-permute-start.11
  36.5 0.7 collective-permute-start.9
  37.8 0.8 collective-permute-start.5
  40.0 1.5 %fusion.6 = bf16[8,2,8,384]{3,2,1,0:T(8,128)(2,1)S(1)} fusion(bf16[8,2,8,384]{3,2,1,0:T(8,128)(2,1)S(1)} %collective-permute-done.5, pred[8]{0:T(512)(128)(4,1)S(1)} %iota_compare_fusion.1, bf16[8,2,8,10368]{3,2,1,0:T(8,128)(2,1)S(1)} %slice_dynamic-update-slice_fusion.36, bf16[10368,384,1,1]{1,0,3,2:T(8,128)(2,1)S(1)} %bitcast.114), kind=kOutput, calls=%fused_computation.158 | convolution fusion | flops 1019412480 | bytes 10813448 | tf_op jit(solution)/shard_map/dot_general | solution.py:42
  41.6 0.7 collective-permute-start.15
  42.3 0.7 collective-permute-start.13
  45.0 1.5 %fusion.3 = bf16[8,2,8,384]{3,2,1,0:T(8,128)(2,1)S(1)} fusion(bf16[8,2,8,10368]{3,2,1,0:T(8,128)(2,1)S(1)} %slice_dynamic-update-slice_fusion.27, bf16[10368,384,1,1]{1,0,3,2:T(8,128)(2,1)S(1)} %bitcast.115, pred[8]{0:T(512)(128)(4,1)S(1)} %iota_compare_fusion.1), kind=kOutput, calls=%fused_computation.8 | convolution fusion | flops 1019314176 | bytes 10715144 | tf_op jit(solution)/shard_map/dot_general | solution.py:42
  46.5 0.7 collective-permute-start.18
  48.6 0.7 collective-permute-start.12
  50.6 1.5 %fusion.41 = f32[8,2,8,384]{3,2,1,0:T(8,128)S(1)} fusion(bf16[8,2,8,10368]{3,2,1,0:T(8,128)(2,1)S(1)} %slice_dynamic-update-slice_fusion.18, bf16[10368,384,1,1]{1,0,3,2:T(8,128)(2,1)S(1)} %bitcast.116), kind=kOutput, calls=%fused_computation.244 | convolution fusion | flops 1019215872 | bytes 10813440 | tf_op jit(solution)/shard_map/dot_general | solution.py:42
  52.2 0.7 collective-permute-start.22
  55.6 1.5 %fusion.4 = bf16[8,2,8,384]{3,2,1,0:T(8,128)(2,1)S(1)} fusion(bf16[8,2,8,10368]{3,2,1,0:T(8,128)(2,1)S(1)} %slice_dynamic-update-slice_fusion.9, bf16[10368,384,1,1]{1,0,3,2:T(8,128)(2,1)S(1)} %bitcast.117, pred[8]{0:T(512)(128)(4,1)S(1)} %iota_compare_fusion.1), kind=kOutput, calls=%fused_computation.9 | convolution fusion | flops 1019314176 | bytes 10715144 | tf_op jit(solution)/shard_map/dot_general | solution.py:42
  57.1 0.7 collective-permute-start.25
  59.2 0.9 collective-permute-start.19
  61.4 1.5 %fusion.42 = f32[8,2,8,384]{3,2,1,0:T(8,128)S(1)} fusion(bf16[8,2,8,10368]{3,2,1,0:T(8,128)(2,1)S(1)} %slice_dynamic-update-slice_fusion, bf16[10368,384,1,1]{1,0,3,2:T(8,128)(2,1)S(1)} %bitcast.118), kind=kOutput, calls=%fused_computation.245 | convolution fusion | flops 1019215872 | bytes 10813440 | tf_op jit(solution)/shard_map/dot_general | solution.py:42
  63.1 43.2 %all_to_all.5 = bf16[8,2,8,384]{3,2,1,0:T(8,128)(2,1)S(1)} all-to-all(bf16[8,2,8,384]{3,2,1,0:T(8,128)(2,1)S(1)} %fusion.8), channel_id=1, replica_groups=mesh['section'=8,'tile'=64] {'section'}, dimensions={0} | all-to-all | bytes 196608 | tf_op jit(solution)/shard_map/all_to_all | solution.py:101
  (179 shorter events, 18.3 us)
Async XLA Ops:
  0.0 17.1 %collective-permute-start.1 = (bf16[8,2,8,384]{3,2,1,0:T(8,128)(2,1)}, bf16[8,2,8,384]{3,2,1,0:T(8,128)(2,1)S(1)}, u32[]{:S(2)}, u32[]{:S(2)}) collective-permute-start(bf16[8,2,8,384]{3,2,1,0:T(8,128)(2,1)} %param.4), channel_id=1, source_target_pairs={{0,1},{1,2},{2,3},{3,4},{4,5},{5,6},{6,7},{7,8},{8,9},{9,10},{10,1... | collective-permute-start | bytes 294920 | tf_op jit(solution)/shard_map/ppermute | solution.py:8
  4.4 12.7 %collective-permute-start = (bf16[8,2,1,384]{3,0,2,1:T(8,128)(2,1)S(1)}, bf16[8,2,1,384]{3,0,2,1:T(8,128)(2,1)S(1)}, u32[]{:S(2)}, u32[]{:S(2)}) collective-permute-start(bf16[8,2,1,384]{3,0,2,1:T(8,128)(2,1)S(1)} %copy.22), channel_id=1, source_target_pairs={{1,0},{2,1},{3,2},{4,3},{5,4},{6,5},{7,6},{8,7},{9,8},{10,9},{11,1... | collective-permute-start | bytes 36872 | tf_op jit(solution)/shard_map/ppermute | solution.py:8
  17.2 3.3 %copy-start = (bf16[1,3,3,1152,384]{4,3,2,1,0:T(8,128)(2,1)S(1)}, bf16[1,3,3,1152,384]{4,3,2,1,0:T(8,128)(2,1)}, u32[]{:S(2)}) copy-start(bf16[1,3,3,1152,384]{4,3,2,1,0:T(8,128)(2,1)} %param.6) | copy-start | bytes 23887876
  22.0 5.5 %collective-permute-start.4 = (bf16[8,2,8,384]{3,2,1,0:T(8,128)(2,1)S(1)}, bf16[8,2,8,384]{3,2,1,0:T(8,128)(2,1)S(1)}, u32[]{:S(2)}, u32[]{:S(2)}) collective-permute-start(bf16[8,2,8,384]{3,2,1,0:T(8,128)(2,1)S(1)} %fusion), channel_id=1, source_target_pairs={{0,64},{1,65},{2,66},{3,67},{4,68},{5,69},{6,70},{7,71},{8,72},{9,... | collective-permute-start | bytes 294920 | tf_op jit(solution)/shard_map/ppermute | solution.py:8
  23.4 2.8 %collective-permute-start.2 = (bf16[8,2,1,384]{3,2,1,0:T(2,128)(2,1)S(1)}, bf16[8,2,1,384]{3,2,1,0:T(2,128)(2,1)S(1)}, u32[]{:S(2)}, u32[]{:S(2)}) collective-permute-start(bf16[8,2,1,384]{3,2,1,0:T(2,128)(2,1)S(1)} %get-tuple-element.57), channel_id=1, source_target_pairs={{1,64},{2,65},{3,66},{4,67},{5,68},{6,69},{7,70},{8,71},{9,72},{10... | collective-permute-start | bytes 36872 | tf_op jit(solution)/shard_map/ppermute | solution.py:8
  24.6 2.8 %collective-permute-start.3 = (bf16[8,2,1,384]{3,2,1,0:T(2,128)(2,1)S(1)}, bf16[8,2,1,384]{3,2,1,0:T(2,128)(2,1)S(1)}, u32[]{:S(2)}, u32[]{:S(2)}) collective-permute-start(bf16[8,2,1,384]{3,2,1,0:T(2,128)(2,1)S(1)} %get-tuple-element.58), channel_id=1, source_target_pairs={{0,65},{1,66},{2,67},{3,68},{4,69},{5,70},{6,71},{7,72},{8,73},{9,... | collective-permute-start | bytes 36872 | tf_op jit(solution)/shard_map/ppermute | solution.py:8
  28.4 0.9 copy-start.1
  30.8 2.1 %collective-permute-start.8 = (bf16[8,2,8,384]{3,2,1,0:T(8,128)(2,1)S(1)}, bf16[8,2,8,384]{3,2,1,0:T(8,128)(2,1)S(1)}, u32[]{:S(2)}, u32[]{:S(2)}) collective-permute-start(bf16[8,2,8,384]{3,2,1,0:T(8,128)(2,1)S(1)} %fusion.5), channel_id=1, source_target_pairs={{64,128},{65,129},{66,130},{67,131},{68,132},{69,133},{70,134},{71... | collective-permute-start | bytes 294920 | tf_op jit(solution)/shard_map/ppermute | solution.py:8
  31.5 1.3 %collective-permute-start.6 = (bf16[8,2,1,384]{3,2,1,0:T(2,128)(2,1)S(1)}, bf16[8,2,1,384]{3,2,1,0:T(2,128)(2,1)S(1)}, u32[]{:S(2)}, u32[]{:S(2)}) collective-permute-start(bf16[8,2,1,384]{3,2,1,0:T(2,128)(2,1)S(1)} %get-tuple-element.55), channel_id=1, source_target_pairs={{65,128},{66,129},{67,130},{68,131},{69,132},{70,133},{71,134},{72... | collective-permute-start | bytes 36872 | tf_op jit(solution)/shard_map/ppermute | solution.py:8
  32.2 0.7 collective-permute-start.7
  35.8 3.0 %collective-permute-start.11 = (bf16[8,2,8,384]{3,2,1,0:T(8,128)(2,1)S(1)}, bf16[8,2,8,384]{3,2,1,0:T(8,128)(2,1)S(1)}, u32[]{:S(2)}, u32[]{:S(2)}) collective-permute-start(bf16[8,2,8,384]{3,2,1,0:T(8,128)(2,1)S(1)} %fusion.2), channel_id=1, source_target_pairs={{128,192},{129,193},{130,194},{131,195},{132,196},{133,197},{134,1... | collective-permute-start | bytes 294920 | tf_op jit(solution)/shard_map/ppermute | solution.py:8
  36.5 2.2 %collective-permute-start.9 = (bf16[8,2,1,384]{3,2,1,0:T(2,128)(2,1)S(1)}, bf16[8,2,1,384]{3,2,1,0:T(2,128)(2,1)S(1)}, u32[]{:S(2)}, u32[]{:S(2)}) collective-permute-start(bf16[8,2,1,384]{3,2,1,0:T(2,128)(2,1)S(1)} %get-tuple-element.53), channel_id=1, source_target_pairs={{129,192},{130,193},{131,194},{132,195},{133,196},{134,197},{135,1... | collective-permute-start | bytes 36872 | tf_op jit(solution)/shard_map/ppermute | solution.py:8
  37.2 1.6 %collective-permute-start.10 = (bf16[8,2,1,384]{3,2,1,0:T(2,128)(2,1)S(1)}, bf16[8,2,1,384]{3,2,1,0:T(2,128)(2,1)S(1)}, u32[]{:S(2)}, u32[]{:S(2)}) collective-permute-start(bf16[8,2,1,384]{3,2,1,0:T(2,128)(2,1)S(1)} %get-tuple-element.54), channel_id=1, source_target_pairs={{128,193},{129,194},{130,195},{131,196},{132,197},{133,198},{134,1... | collective-permute-start | bytes 36872 | tf_op jit(solution)/shard_map/ppermute | solution.py:8
  37.8 2.2 %collective-permute-start.5 = (bf16[8,2,8,384]{3,2,1,0:T(8,128)(2,1)S(1)}, bf16[8,2,8,384]{3,2,1,0:T(8,128)(2,1)S(1)}, u32[]{:S(2)}, u32[]{:S(2)}) collective-permute-start(bf16[8,2,8,384]{3,2,1,0:T(8,128)(2,1)S(1)} %fusion.5), channel_id=1, source_target_pairs={{64,192},{65,193},{66,194},{67,195},{68,196},{69,197},{70,198},{71... | collective-permute-start | bytes 294920 | tf_op jit(solution)/shard_map/ppermute | solution.py:8
  41.6 2.1 %collective-permute-start.15 = (bf16[8,2,8,384]{3,2,1,0:T(8,128)(2,1)S(1)}, bf16[8,2,8,384]{3,2,1,0:T(8,128)(2,1)S(1)}, u32[]{:S(2)}, u32[]{:S(2)}) collective-permute-start(bf16[8,2,8,384]{3,2,1,0:T(8,128)(2,1)S(1)} %fusion.6), channel_id=1, source_target_pairs={{192,256},{193,257},{194,258},{195,259},{196,260},{197,261},{198,2... | collective-permute-start | bytes 294920 | tf_op jit(solution)/shard_map/ppermute | solution.py:8
  42.3 1.3 %collective-permute-start.13 = (bf16[8,2,1,384]{3,2,1,0:T(2,128)(2,1)S(1)}, bf16[8,2,1,384]{3,2,1,0:T(2,128)(2,1)S(1)}, u32[]{:S(2)}, u32[]{:S(2)}) collective-permute-start(bf16[8,2,1,384]{3,2,1,0:T(2,128)(2,1)S(1)} %get-tuple-element.51), channel_id=1, source_target_pairs={{193,256},{194,257},{195,258},{196,259},{197,260},{198,261},{199,2... | collective-permute-start | bytes 36872 | tf_op jit(solution)/shard_map/ppermute | solution.py:8
  43.0 0.7 collective-permute-start.14
  46.5 2.8 %collective-permute-start.18 = (bf16[8,2,8,384]{3,2,1,0:T(8,128)(2,1)S(1)}, bf16[8,2,8,384]{3,2,1,0:T(8,128)(2,1)S(1)}, u32[]{:S(2)}, u32[]{:S(2)}) collective-permute-start(bf16[8,2,8,384]{3,2,1,0:T(8,128)(2,1)S(1)} %fusion.3), channel_id=1, source_target_pairs={{256,320},{257,321},{258,322},{259,323},{260,324},{261,325},{262,3... | collective-permute-start | bytes 294920 | tf_op jit(solution)/shard_map/ppermute | solution.py:8
  47.2 2.0 %collective-permute-start.16 = (bf16[8,2,1,384]{3,2,1,0:T(2,128)(2,1)S(1)}, bf16[8,2,1,384]{3,2,1,0:T(2,128)(2,1)S(1)}, u32[]{:S(2)}, u32[]{:S(2)}) collective-permute-start(bf16[8,2,1,384]{3,2,1,0:T(2,128)(2,1)S(1)} %get-tuple-element.49), channel_id=1, source_target_pairs={{257,320},{258,321},{259,322},{260,323},{261,324},{262,325},{263,3... | collective-permute-start | bytes 36872 | tf_op jit(solution)/shard_map/ppermute | solution.py:8
  47.9 1.4 %collective-permute-start.17 = (bf16[8,2,1,384]{3,2,1,0:T(2,128)(2,1)S(1)}, bf16[8,2,1,384]{3,2,1,0:T(2,128)(2,1)S(1)}, u32[]{:S(2)}, u32[]{:S(2)}) collective-permute-start(bf16[8,2,1,384]{3,2,1,0:T(2,128)(2,1)S(1)} %get-tuple-element.50), channel_id=1, source_target_pairs={{256,321},{257,322},{258,323},{259,324},{260,325},{261,326},{262,3... | collective-permute-start | bytes 36872 | tf_op jit(solution)/shard_map/ppermute | solution.py:8
  48.6 3.5 %collective-permute-start.12 = (bf16[8,2,8,384]{3,2,1,0:T(8,128)(2,1)S(1)}, bf16[8,2,8,384]{3,2,1,0:T(8,128)(2,1)S(1)}, u32[]{:S(2)}, u32[]{:S(2)}) collective-permute-start(bf16[8,2,8,384]{3,2,1,0:T(8,128)(2,1)S(1)} %fusion.6), channel_id=1, source_target_pairs={{192,320},{193,321},{194,322},{195,323},{196,324},{197,325},{198,3... | collective-permute-start | bytes 294920 | tf_op jit(solution)/shard_map/ppermute | solution.py:8
  52.2 2.1 %collective-permute-start.22 = (bf16[8,2,8,384]{3,2,1,0:T(8,128)(2,1)S(1)}, bf16[8,2,8,384]{3,2,1,0:T(8,128)(2,1)S(1)}, u32[]{:S(2)}, u32[]{:S(2)}) collective-permute-start(bf16[8,2,8,384]{3,2,1,0:T(8,128)(2,1)S(1)} %fusion.7), channel_id=1, source_target_pairs={{320,384},{321,385},{322,386},{323,387},{324,388},{325,389},{326,3... | collective-permute-start | bytes 294920 | tf_op jit(solution)/shard_map/ppermute | solution.py:8
  52.9 1.3 %collective-permute-start.20 = (bf16[8,2,1,384]{3,2,1,0:T(2,128)(2,1)S(1)}, bf16[8,2,1,384]{3,2,1,0:T(2,128)(2,1)S(1)}, u32[]{:S(2)}, u32[]{:S(2)}) collective-permute-start(bf16[8,2,1,384]{3,2,1,0:T(2,128)(2,1)S(1)} %get-tuple-element.47), channel_id=1, source_target_pairs={{321,384},{322,385},{323,386},{324,387},{325,388},{326,389},{327,3... | collective-permute-start | bytes 36872 | tf_op jit(solution)/shard_map/ppermute | solution.py:8
  53.6 0.7 collective-permute-start.21
  57.1 3.0 %collective-permute-start.25 = (bf16[8,2,8,384]{3,2,1,0:T(8,128)(2,1)S(1)}, bf16[8,2,8,384]{3,2,1,0:T(8,128)(2,1)S(1)}, u32[]{:S(2)}, u32[]{:S(2)}) collective-permute-start(bf16[8,2,8,384]{3,2,1,0:T(8,128)(2,1)S(1)} %fusion.4), channel_id=1, source_target_pairs={{384,448},{385,449},{386,450},{387,451},{388,452},{389,453},{390,4... | collective-permute-start | bytes 294920 | tf_op jit(solution)/shard_map/ppermute | solution.py:8
  57.9 2.2 %collective-permute-start.23 = (bf16[8,2,1,384]{3,2,1,0:T(2,128)(2,1)S(1)}, bf16[8,2,1,384]{3,2,1,0:T(2,128)(2,1)S(1)}, u32[]{:S(2)}, u32[]{:S(2)}) collective-permute-start(bf16[8,2,1,384]{3,2,1,0:T(2,128)(2,1)S(1)} %get-tuple-element.45), channel_id=1, source_target_pairs={{385,448},{386,449},{387,450},{388,451},{389,452},{390,453},{391,4... | collective-permute-start | bytes 36872 | tf_op jit(solution)/shard_map/ppermute | solution.py:8
  58.5 1.6 %collective-permute-start.24 = (bf16[8,2,1,384]{3,2,1,0:T(2,128)(2,1)S(1)}, bf16[8,2,1,384]{3,2,1,0:T(2,128)(2,1)S(1)}, u32[]{:S(2)}, u32[]{:S(2)}) collective-permute-start(bf16[8,2,1,384]{3,2,1,0:T(2,128)(2,1)S(1)} %get-tuple-element.46), channel_id=1, source_target_pairs={{384,449},{385,450},{386,451},{387,452},{388,453},{389,454},{390,4... | collective-permute-start | bytes 36872 | tf_op jit(solution)/shard_map/ppermute | solution.py:8
  59.2 3.8 %collective-permute-start.19 = (bf16[8,2,8,384]{3,2,1,0:T(8,128)(2,1)S(1)}, bf16[8,2,8,384]{3,2,1,0:T(8,128)(2,1)S(1)}, u32[]{:S(2)}, u32[]{:S(2)}) collective-permute-start(bf16[8,2,8,384]{3,2,1,0:T(8,128)(2,1)S(1)} %fusion.7), channel_id=1, source_target_pairs={{320,448},{321,449},{322,450},{323,451},{324,452},{325,453},{326,4... | collective-permute-start | bytes 294920 | tf_op jit(solution)/shard_map/ppermute | solution.py:8

commit v9 on v4

--- a/solution.py
+++ b/solution.py
@@ -2,6 +2,22 @@
 import jax.numpy as jnp
 from jax import lax
 from jax.sharding import PartitionSpec as P
+from jax.experimental import pallas as pl
+from jax.experimental.pallas import tpu as pltpu
+
+
+def _touch_body(w_ref, o_ref):
+    o_ref[...] = w_ref[0:8, 0:128].astype(jnp.float32)
+
+
+def touch(flat):
+    return pl.pallas_call(
+        _touch_body,
+        out_shape=jax.ShapeDtypeStruct((8, 128), jnp.float32),
+        in_specs=[pl.BlockSpec(memory_space=pltpu.VMEM)],
+        out_specs=pl.BlockSpec(memory_space=pltpu.VMEM),
+        compiler_params=pltpu.CompilerParams(vmem_limit_bytes=48 * 1024 * 1024),
+    )(flat)
 
 
 def hop(block, pairs, axes):
@@ -66,6 +82,8 @@
     left = lax.dynamic_slice_in_dim(from_left, left_count - 1, 1, 2)
     right = from_right
     stream = jnp.where(col_live, latents, zero)
+    touched = touch(kernel.reshape(-1, kernel.shape[-1]))
+    stream, touched = lax.optimization_barrier((stream, touched))
     current = stream
     residual = stream
     for stage in range(segments):
@@ -87,7 +105,7 @@
         current = nxt
     final = produced
     spread = lax.all_to_all(final, "section", 0, 0, tiled=True)
-    return spread[segments - 1 : segments]
+    return spread[segments - 1 : segments] + (touched[0, 0] * 0.0).astype(jnp.bfloat16)
 
 def solution(mesh):
     return jax.shard_map(

time: 106 us -> 111 us (1.047)
  blocking collectives: 43.5 us -> 0 us
  starting transfers between devices: 27.2 us -> 65 us
  waiting for transfers between devices: 1.54 us -> 6.17 us
  matrix products: 12.2 us -> 15.7 us
  Pallas kernels: 0 us -> 3.27 us
  local copies, waits for them, and re-layouts: 9.42 us -> 6.32 us
  other arithmetic: 6.83 us -> 8.16 us
    all_to_all x1 -> x0, blocking collectives: 43.5 us -> none  [local(): spread = lax.all_to_all(final, 'section', 0, 0, tiled=True)]
    all_to_all x0 -> x1, starting transfers between devices: none -> 37.9 us  [local(): spread = lax.all_to_all(final, 'section', 0, 0, tiled=True)]
    all_to_all x0 -> x1, waiting for transfers between devices: none -> 4.63 us  [local(): spread = lax.all_to_all(final, 'section', 0, 0, tiled=True)]
    dot_general x8, matrix products: 12.2 us -> 15.7 us  [convolve(): out = jnp.dot(joined, flat, preferred_element_type=jnp.float32)]
    pallas_call x0 -> x1, Pallas kernels: none -> 3.27 us  [touch(): pl.pallas_call(_touch_body, out_shape=jax.ShapeDtypeStruct((8, 128), jnp....]
    unnamed x69, local copies, waits for them, and re-layouts: 5.04 us -> 2.01 us
  transfers between devices with their start and end apart: 26 -> 27, of which waited for: 2 -> 3; matrix products, arithmetic and copies ran while one was open for 10% -> 10% of each run, Pallas kernels for 0% -> 3%
where the time goes in v9:
time: 111 us; the launch traced here: 110 us
  starting transfers between devices  65 us (59%)
  matrix products  15.7 us (14%)
  other arithmetic  8.16 us (7%)
  local copies, waits for them, and re-layouts  6.32 us (6%)
  waiting for transfers between devices  6.17 us (6%)
  between operations  5.24 us (5%)
  Pallas kernels  3.27 us (3%)
    all_to_all x1, starting transfers between devices, local(): spread = lax.all_to_all(final, 'section', 0, 0, tiled=True)  37.9 us
    ppermute x26, starting transfers between devices, hop(): return lax.ppermute(block, axes, pairs)  27.2 us
    dot_general x8, matrix products, convolve(): out = jnp.dot(joined, flat, preferred_element_type=jnp.float32)  15.7 us
    all_to_all x1, waiting for transfers between devices, local(): spread = lax.all_to_all(final, 'section', 0, 0, tiled=True)  4.63 us
    pallas_call x1, Pallas kernels, touch(): pl.pallas_call(_touch_body, out_shape=jax.ShapeDtypeStruct((8, 128), jnp....  3.27 us
  transfers between devices with their start and end apart: 27, of which 3 were waited for; matrix products, arithmetic and copies ran while one was open for 10% of the time, Pallas kernels for 3%

profile of v9, /device:TPU:256, one launch (start us, length us, event | category | flops | bytes accessed | tf_op | source)
XLA Modules:
  0.0 109.9 jit_solution(12940331946420045981)
XLA Ops:
  0.0 3.5 %collective-permute-start.1 = (bf16[8,2,8,384]{3,2,1,0:T(8,128)(2,1)}, bf16[8,2,8,384]{3,2,1,0:T(8,128)(2,1)S(1)}, u32[]{:S(2)}, u32[]{:S(2)}) collective-permute-start(bf16[8,2,8,384]{3,2,1,0:T(8,128)(2,1)} %param.4), channel_id=1, source_target_pairs={{0,1},{1,2},{2,3},{3,4},{4,5},{5,6},{6,7},{7,8},{8,9},{9,10},{10,1... | collective-permute-start | bytes 294920 | tf_op jit(solution)/shard_map/ppermute | solution.py:24
  3.5 0.9 slice.318
  4.4 5.7 %collective-permute-start = (bf16[8,2,1,384]{3,0,2,1:T(8,128)(2,1)S(1)}, bf16[8,2,1,384]{3,0,2,1:T(8,128)(2,1)S(1)}, u32[]{:S(2)}, u32[]{:S(2)}) collective-permute-start(bf16[8,2,1,384]{3,0,2,1:T(8,128)(2,1)S(1)} %copy.22), channel_id=1, source_target_pairs={{1,0},{2,1},{3,2},{4,3},{5,4},{6,5},{7,6},{8,7},{9,8},{10,9},{11,1... | collective-permute-start | bytes 36872 | tf_op jit(solution)/shard_map/ppermute | solution.py:24
  10.1 1.3 %fusion.80 = (s32[1]{0:T(128)}, s32[1]{0:T(128)}) fusion(s32[64]{0:T(128)} %param.5, s32[]{:T(128)S(6)} %max.3, s32[]{:T(128)S(6)} %select_n.70), kind=kLoop, calls=%fused_computation.244 | loop fusion | bytes 24 | tf_op jit(solution)/shard_map/dynamic_slice | solution.py:81
  12.7 0.7 convert_reduce_fusion
  13.4 1.0 broadcast_select_fusion
  16.9 3.3 %shard_map.46 = f32[8,128]{1,0:T(8,128)S(1)} custom-call(bf16[10368,384]{1,0:T(8,128)(2,1)} %bitcast.48), custom_call_target="tpu_custom_call" | custom-call | tf_op jit(solution)/shard_map/pallas_call | solution.py:14
  21.4 5.0 %fusion = bf16[8,2,8,384]{3,2,1,0:T(8,128)(2,1)S(1)} fusion(bf16[8,2,8,10368]{3,2,1,0:T(8,128)(2,1)S(1)} %slice_dynamic-update-slice_fusion.63, bf16[10368,384,1,1]{1,0,3,2:T(8,128)(2,1)} %bitcast.49, pred[8]{0:T(512)(128)(4,1)S(1)} %iota_compare_fusion.1), kind=kOutput, calls=%fused_computation.5 | convolution fusion | flops 1019314176 | bytes 10715144 | tf_op jit(solution)/shard_map/dot_general | solution.py:46
  26.4 1.3 %collective-permute-start.4 = (bf16[8,2,8,384]{3,2,1,0:T(8,128)(2,1)S(1)}, bf16[8,2,8,384]{3,2,1,0:T(8,128)(2,1)S(1)}, u32[]{:S(2)}, u32[]{:S(2)}) collective-permute-start(bf16[8,2,8,384]{3,2,1,0:T(8,128)(2,1)S(1)} %fusion), channel_id=1, source_target_pairs={{0,64},{1,65},{2,66},{3,67},{4,68},{5,69},{6,70},{7,71},{8,72},{9,... | collective-permute-start | bytes 294920 | tf_op jit(solution)/shard_map/ppermute | solution.py:24
  27.8 1.3 %collective-permute-start.2 = (bf16[8,2,1,384]{3,2,1,0:T(2,128)(2,1)S(1)}, bf16[8,2,1,384]{3,2,1,0:T(2,128)(2,1)S(1)}, u32[]{:S(2)}, u32[]{:S(2)}) collective-permute-start(bf16[8,2,1,384]{3,2,1,0:T(2,128)(2,1)S(1)} %get-tuple-element.45), channel_id=1, source_target_pairs={{1,64},{2,65},{3,66},{4,67},{5,68},{6,69},{7,70},{8,71},{9,72},{10... | collective-permute-start | bytes 36872 | tf_op jit(solution)/shard_map/ppermute | solution.py:24
  29.1 1.3 %collective-permute-start.3 = (bf16[8,2,1,384]{3,2,1,0:T(2,128)(2,1)S(1)}, bf16[8,2,1,384]{3,2,1,0:T(2,128)(2,1)S(1)}, u32[]{:S(2)}, u32[]{:S(2)}) collective-permute-start(bf16[8,2,1,384]{3,2,1,0:T(2,128)(2,1)S(1)} %get-tuple-element.46), channel_id=1, source_target_pairs={{0,65},{1,66},{2,67},{3,68},{4,69},{5,70},{6,71},{7,72},{8,73},{9,... | collective-permute-start | bytes 36872 | tf_op jit(solution)/shard_map/ppermute | solution.py:24
  30.6 1.3 %collective-permute-done.3 = bf16[8,2,1,384]{3,2,1,0:T(2,128)(2,1)S(1)} collective-permute-done((bf16[8,2,1,384]{3,2,1,0:T(2,128)(2,1)S(1)}, bf16[8,2,1,384]{3,2,1,0:T(2,128)(2,1)S(1)}, u32[]{:S(2)}, u32[]{:S(2)}) %collective-permute-start.3) | collective-permute-done | bytes 12320 | tf_op jit(solution)/shard_map/ppermute | solution.py:24
  32.9 1.5 %fusion.5 = bf16[8,2,8,384]{3,2,1,0:T(8,128)(2,1)S(1)} fusion(bf16[8,2,8,10368]{3,2,1,0:T(8,128)(2,1)S(1)} %slice_dynamic-update-slice_fusion.54, bf16[10368,384,1,1]{1,0,3,2:T(8,128)(2,1)S(1)} %bitcast.52, bf16[8,2,8,384]{3,2,1,0:T(8,128)(2,1)S(1)} %broadcast_select_fusion, pred[8]{0:T(512)(128)(4,1)S(1)} %iota_compare_fusion.1), kind=kOutput, calls=%fused_computation.10 | convolution fusion | flops 1019412480 | bytes 10813448 | tf_op jit(solution)/shard_map/dot_general | solution.py:46
  34.5 0.7 collective-permute-start.8
  37.6 1.5 %fusion.2 = bf16[8,2,8,384]{3,2,1,0:T(8,128)(2,1)S(1)} fusion(bf16[8,2,8,10368]{3,2,1,0:T(8,128)(2,1)S(1)} %slice_dynamic-update-slice_fusion.45, bf16[10368,384,1,1]{1,0,3,2:T(8,128)(2,1)S(1)} %bitcast.53, pred[8]{0:T(512)(128)(4,1)S(1)} %iota_compare_fusion.1), kind=kOutput, calls=%fused_computation.7 | convolution fusion | flops 1019314176 | bytes 10715144 | tf_op jit(solution)/shard_map/dot_general | solution.py:46
  39.1 0.7 collective-permute-start.11
  41.2 0.7 collective-permute-start.5
  43.0 1.5 %fusion.70 = bf16[8,2,8,384]{3,2,1,0:T(8,128)(2,1)S(1)} fusion(bf16[8,2,8,384]{3,2,1,0:T(8,128)(2,1)S(1)} %collective-permute-done.5, pred[8]{0:T(512)(128)(4,1)S(1)} %iota_compare_fusion.1, bf16[8,2,8,10368]{3,2,1,0:T(8,128)(2,1)S(1)} %slice_dynamic-update-slice_fusion.36, bf16[10368,384,1,1]{1,0,3,2:T(8,128)(2,1)S(1)} %bitcast.54), kind=kOutput, calls=%fused_computation.206 | convolution fusion | flops 1019412480 | bytes 10813448 | tf_op jit(solution)/shard_map/dot_general | solution.py:46
  44.5 0.7 collective-permute-start.15
  45.9 0.8 collective-permute-start.14
  47.8 1.5 %fusion.3 = bf16[8,2,8,384]{3,2,1,0:T(8,128)(2,1)S(1)} fusion(bf16[8,2,8,10368]{3,2,1,0:T(8,128)(2,1)S(1)} %slice_dynamic-update-slice_fusion.27, bf16[10368,384,1,1]{1,0,3,2:T(8,128)(2,1)S(1)} %bitcast.55, pred[8]{0:T(512)(128)(4,1)S(1)} %iota_compare_fusion.1), kind=kOutput, calls=%fused_computation.8 | convolution fusion | flops 1019314176 | bytes 10715144 | tf_op jit(solution)/shard_map/dot_general | solution.py:46
  49.4 0.7 collective-permute-start.18
  51.5 0.7 collective-permute-start.12
  53.2 1.5 %fusion.81 = f32[8,2,8,384]{3,2,1,0:T(8,128)S(1)} fusion(bf16[8,2,8,10368]{3,2,1,0:T(8,128)(2,1)S(1)} %slice_dynamic-update-slice_fusion.18, bf16[10368,384,1,1]{1,0,3,2:T(8,128)(2,1)S(1)} %bitcast.56), kind=kOutput, calls=%fused_computation.245 | convolution fusion | flops 1019215872 | bytes 10813440 | tf_op jit(solution)/shard_map/dot_general | solution.py:46
  54.8 0.7 collective-permute-start.22
  58.0 1.5 %fusion.4 = bf16[8,2,8,384]{3,2,1,0:T(8,128)(2,1)S(1)} fusion(bf16[8,2,8,10368]{3,2,1,0:T(8,128)(2,1)S(1)} %slice_dynamic-update-slice_fusion.9, bf16[10368,384,1,1]{1,0,3,2:T(8,128)(2,1)S(1)} %bitcast.57, pred[8]{0:T(512)(128)(4,1)S(1)} %iota_compare_fusion.1), kind=kOutput, calls=%fused_computation.9 | convolution fusion | flops 1019314176 | bytes 10715144 | tf_op jit(solution)/shard_map/dot_general | solution.py:46
  59.5 0.7 collective-permute-start.25
  61.6 0.7 collective-permute-start.19
  63.4 1.5 %fusion.82 = f32[8,2,8,384]{3,2,1,0:T(8,128)S(1)} fusion(bf16[8,2,8,10368]{3,2,1,0:T(8,128)(2,1)S(1)} %slice_dynamic-update-slice_fusion, bf16[10368,384,1,1]{1,0,3,2:T(8,128)(2,1)S(1)} %bitcast.58), kind=kOutput, calls=%fused_computation.246 | convolution fusion | flops 1019215872 | bytes 10813440 | tf_op jit(solution)/shard_map/dot_general | solution.py:46
  64.9 0.7 fusion.72
  65.6 37.9 %all-to-all-start = ((bf16[8,2,8,384]{3,2,1,0:T(8,128)(2,1)}), bf16[8,2,8,384]{3,2,1,0:T(8,128)(2,1)S(1)}, u32[]{:S(2)}, u32[]{:S(2)}) async-start(bf16[8,2,8,384]{3,2,1,0:T(8,128)(2,1)} %fusion.72), calls=%async_computation | async-start | bytes 196608 | tf_op jit(solution)/shard_map/all_to_all | solution.py:107
  104.7 4.6 %all-to-all-done = bf16[8,2,8,384]{3,2,1,0:T(8,128)(2,1)S(1)} async-done(((bf16[8,2,8,384]{3,2,1,0:T(8,128)(2,1)}), bf16[8,2,8,384]{3,2,1,0:T(8,128)(2,1)S(1)}, u32[]{:S(2)}, u32[]{:S(2)}) %all-to-all-start) | async-done | bytes 98336 | tf_op jit(solution)/shard_map/all_to_all | solution.py:107
  (183 shorter events, 17.4 us)
Async XLA Ops:
  0.0 20.3 %collective-permute-start.1 = (bf16[8,2,8,384]{3,2,1,0:T(8,128)(2,1)}, bf16[8,2,8,384]{3,2,1,0:T(8,128)(2,1)S(1)}, u32[]{:S(2)}, u32[]{:S(2)}) collective-permute-start(bf16[8,2,8,384]{3,2,1,0:T(8,128)(2,1)} %param.4), channel_id=1, source_target_pairs={{0,1},{1,2},{2,3},{3,4},{4,5},{5,6},{6,7},{7,8},{8,9},{9,10},{10,1... | collective-permute-start | bytes 294920 | tf_op jit(solution)/shard_map/ppermute | solution.py:24
  4.4 15.9 %collective-permute-start = (bf16[8,2,1,384]{3,0,2,1:T(8,128)(2,1)S(1)}, bf16[8,2,1,384]{3,0,2,1:T(8,128)(2,1)S(1)}, u32[]{:S(2)}, u32[]{:S(2)}) collective-permute-start(bf16[8,2,1,384]{3,0,2,1:T(8,128)(2,1)S(1)} %copy.22), channel_id=1, source_target_pairs={{1,0},{2,1},{3,2},{4,3},{5,4},{6,5},{7,6},{8,7},{9,8},{10,9},{11,1... | collective-permute-start | bytes 36872 | tf_op jit(solution)/shard_map/ppermute | solution.py:24
  21.3 11.6 %slice-start = ((s8[7962624]{0:T(1024)(128)(4,1)}), s8[4194304]{0:T(1024)(128)(4,1)S(1)}, s32[]{:S(2)}) async-start(s8[7962624]{0:T(1024)(128)(4,1)} %bitcast.50), calls=%async_computation.1 | async-start | bytes 8388608
  21.4 11.5 %slice-start.1 = ((s8[7962624]{0:T(1024)(128)(4,1)}), s8[3768320]{0:T(1024)(128)(4,1)S(1)}, s32[]{:S(2)}) async-start(s8[7962624]{0:T(1024)(128)(4,1)} %bitcast.50), calls=%async_computation.2 | async-start | bytes 7536640
  26.4 5.5 %collective-permute-start.4 = (bf16[8,2,8,384]{3,2,1,0:T(8,128)(2,1)S(1)}, bf16[8,2,8,384]{3,2,1,0:T(8,128)(2,1)S(1)}, u32[]{:S(2)}, u32[]{:S(2)}) collective-permute-start(bf16[8,2,8,384]{3,2,1,0:T(8,128)(2,1)S(1)} %fusion), channel_id=1, source_target_pairs={{0,64},{1,65},{2,66},{3,67},{4,68},{5,69},{6,70},{7,71},{8,72},{9,... | collective-permute-start | bytes 294920 | tf_op jit(solution)/shard_map/ppermute | solution.py:24
  27.8 2.8 %collective-permute-start.2 = (bf16[8,2,1,384]{3,2,1,0:T(2,128)(2,1)S(1)}, bf16[8,2,1,384]{3,2,1,0:T(2,128)(2,1)S(1)}, u32[]{:S(2)}, u32[]{:S(2)}) collective-permute-start(bf16[8,2,1,384]{3,2,1,0:T(2,128)(2,1)S(1)} %get-tuple-element.45), channel_id=1, source_target_pairs={{1,64},{2,65},{3,66},{4,67},{5,68},{6,69},{7,70},{8,71},{9,72},{10... | collective-permute-start | bytes 36872 | tf_op jit(solution)/shard_map/ppermute | solution.py:24
  29.1 2.8 %collective-permute-start.3 = (bf16[8,2,1,384]{3,2,1,0:T(2,128)(2,1)S(1)}, bf16[8,2,1,384]{3,2,1,0:T(2,128)(2,1)S(1)}, u32[]{:S(2)}, u32[]{:S(2)}) collective-permute-start(bf16[8,2,1,384]{3,2,1,0:T(2,128)(2,1)S(1)} %get-tuple-element.46), channel_id=1, source_target_pairs={{0,65},{1,66},{2,67},{3,68},{4,69},{5,70},{6,71},{7,72},{8,73},{9,... | collective-permute-start | bytes 36872 | tf_op jit(solution)/shard_map/ppermute | solution.py:24
  34.5 2.1 %collective-permute-start.8 = (bf16[8,2,8,384]{3,2,1,0:T(8,128)(2,1)S(1)}, bf16[8,2,8,384]{3,2,1,0:T(8,128)(2,1)S(1)}, u32[]{:S(2)}, u32[]{:S(2)}) collective-permute-start(bf16[8,2,8,384]{3,2,1,0:T(8,128)(2,1)S(1)} %fusion.5), channel_id=1, source_target_pairs={{64,128},{65,129},{66,130},{67,131},{68,132},{69,133},{70,134},{71... | collective-permute-start | bytes 294920 | tf_op jit(solution)/shard_map/ppermute | solution.py:24
  35.2 1.3 %collective-permute-start.6 = (bf16[8,2,1,384]{3,2,1,0:T(2,128)(2,1)S(1)}, bf16[8,2,1,384]{3,2,1,0:T(2,128)(2,1)S(1)}, u32[]{:S(2)}, u32[]{:S(2)}) collective-permute-start(bf16[8,2,1,384]{3,2,1,0:T(2,128)(2,1)S(1)} %get-tuple-element.43), channel_id=1, source_target_pairs={{65,128},{66,129},{67,130},{68,131},{69,132},{70,133},{71,134},{72... | collective-permute-start | bytes 36872 | tf_op jit(solution)/shard_map/ppermute | solution.py:24
  35.9 0.7 collective-permute-start.7
  39.1 2.8 %collective-permute-start.11 = (bf16[8,2,8,384]{3,2,1,0:T(8,128)(2,1)S(1)}, bf16[8,2,8,384]{3,2,1,0:T(8,128)(2,1)S(1)}, u32[]{:S(2)}, u32[]{:S(2)}) collective-permute-start(bf16[8,2,8,384]{3,2,1,0:T(8,128)(2,1)S(1)} %fusion.2), channel_id=1, source_target_pairs={{128,192},{129,193},{130,194},{131,195},{132,196},{133,197},{134,1... | collective-permute-start | bytes 294920 | tf_op jit(solution)/shard_map/ppermute | solution.py:24
  39.9 2.0 %collective-permute-start.9 = (bf16[8,2,1,384]{3,2,1,0:T(2,128)(2,1)S(1)}, bf16[8,2,1,384]{3,2,1,0:T(2,128)(2,1)S(1)}, u32[]{:S(2)}, u32[]{:S(2)}) collective-permute-start(bf16[8,2,1,384]{3,2,1,0:T(2,128)(2,1)S(1)} %get-tuple-element.41), channel_id=1, source_target_pairs={{129,192},{130,193},{131,194},{132,195},{133,196},{134,197},{135,1... | collective-permute-start | bytes 36872 | tf_op jit(solution)/shard_map/ppermute | solution.py:24
  40.5 1.4 %collective-permute-start.10 = (bf16[8,2,1,384]{3,2,1,0:T(2,128)(2,1)S(1)}, bf16[8,2,1,384]{3,2,1,0:T(2,128)(2,1)S(1)}, u32[]{:S(2)}, u32[]{:S(2)}) collective-permute-start(bf16[8,2,1,384]{3,2,1,0:T(2,128)(2,1)S(1)} %get-tuple-element.42), channel_id=1, source_target_pairs={{128,193},{129,194},{130,195},{131,196},{132,197},{133,198},{134,1... | collective-permute-start | bytes 36872 | tf_op jit(solution)/shard_map/ppermute | solution.py:24
  41.2 1.8 %collective-permute-start.5 = (bf16[8,2,8,384]{3,2,1,0:T(8,128)(2,1)S(1)}, bf16[8,2,8,384]{3,2,1,0:T(8,128)(2,1)S(1)}, u32[]{:S(2)}, u32[]{:S(2)}) collective-permute-start(bf16[8,2,8,384]{3,2,1,0:T(8,128)(2,1)S(1)} %fusion.5), channel_id=1, source_target_pairs={{64,192},{65,193},{66,194},{67,195},{68,196},{69,197},{70,198},{71... | collective-permute-start | bytes 294920 | tf_op jit(solution)/shard_map/ppermute | solution.py:24
  44.5 2.3 %collective-permute-start.15 = (bf16[8,2,8,384]{3,2,1,0:T(8,128)(2,1)S(1)}, bf16[8,2,8,384]{3,2,1,0:T(8,128)(2,1)S(1)}, u32[]{:S(2)}, u32[]{:S(2)}) collective-permute-start(bf16[8,2,8,384]{3,2,1,0:T(8,128)(2,1)S(1)} %fusion.70), channel_id=1, source_target_pairs={{192,256},{193,257},{194,258},{195,259},{196,260},{197,261},{198,2... | collective-permute-start | bytes 294920 | tf_op jit(solution)/shard_map/ppermute | solution.py:24
  45.2 1.5 %collective-permute-start.13 = (bf16[8,2,1,384]{3,2,1,0:T(2,128)(2,1)S(1)}, bf16[8,2,1,384]{3,2,1,0:T(2,128)(2,1)S(1)}, u32[]{:S(2)}, u32[]{:S(2)}) collective-permute-start(bf16[8,2,1,384]{3,2,1,0:T(2,128)(2,1)S(1)} %get-tuple-element.39), channel_id=1, source_target_pairs={{193,256},{194,257},{195,258},{196,259},{197,260},{198,261},{199,2... | collective-permute-start | bytes 36872 | tf_op jit(solution)/shard_map/ppermute | solution.py:24
  45.9 0.9 collective-permute-start.14
  49.4 2.8 %collective-permute-start.18 = (bf16[8,2,8,384]{3,2,1,0:T(8,128)(2,1)S(1)}, bf16[8,2,8,384]{3,2,1,0:T(8,128)(2,1)S(1)}, u32[]{:S(2)}, u32[]{:S(2)}) collective-permute-start(bf16[8,2,8,384]{3,2,1,0:T(8,128)(2,1)S(1)} %fusion.3), channel_id=1, source_target_pairs={{256,320},{257,321},{258,322},{259,323},{260,324},{261,325},{262,3... | collective-permute-start | bytes 294920 | tf_op jit(solution)/shard_map/ppermute | solution.py:24
  50.1 2.0 %collective-permute-start.16 = (bf16[8,2,1,384]{3,2,1,0:T(2,128)(2,1)S(1)}, bf16[8,2,1,384]{3,2,1,0:T(2,128)(2,1)S(1)}, u32[]{:S(2)}, u32[]{:S(2)}) collective-permute-start(bf16[8,2,1,384]{3,2,1,0:T(2,128)(2,1)S(1)} %get-tuple-element.37), channel_id=1, source_target_pairs={{257,320},{258,321},{259,322},{260,323},{261,324},{262,325},{263,3... | collective-permute-start | bytes 36872 | tf_op jit(solution)/shard_map/ppermute | solution.py:24
  50.8 1.4 %collective-permute-start.17 = (bf16[8,2,1,384]{3,2,1,0:T(2,128)(2,1)S(1)}, bf16[8,2,1,384]{3,2,1,0:T(2,128)(2,1)S(1)}, u32[]{:S(2)}, u32[]{:S(2)}) collective-permute-start(bf16[8,2,1,384]{3,2,1,0:T(2,128)(2,1)S(1)} %get-tuple-element.38), channel_id=1, source_target_pairs={{256,321},{257,322},{258,323},{259,324},{260,325},{261,326},{262,3... | collective-permute-start | bytes 36872 | tf_op jit(solution)/shard_map/ppermute | solution.py:24
  51.5 3.3 %collective-permute-start.12 = (bf16[8,2,8,384]{3,2,1,0:T(8,128)(2,1)S(1)}, bf16[8,2,8,384]{3,2,1,0:T(8,128)(2,1)S(1)}, u32[]{:S(2)}, u32[]{:S(2)}) collective-permute-start(bf16[8,2,8,384]{3,2,1,0:T(8,128)(2,1)S(1)} %fusion.70), channel_id=1, source_target_pairs={{192,320},{193,321},{194,322},{195,323},{196,324},{197,325},{198,3... | collective-permute-start | bytes 294920 | tf_op jit(solution)/shard_map/ppermute | solution.py:24
  54.8 2.1 %collective-permute-start.22 = (bf16[8,2,8,384]{3,2,1,0:T(8,128)(2,1)S(1)}, bf16[8,2,8,384]{3,2,1,0:T(8,128)(2,1)S(1)}, u32[]{:S(2)}, u32[]{:S(2)}) collective-permute-start(bf16[8,2,8,384]{3,2,1,0:T(8,128)(2,1)S(1)} %fusion.71), channel_id=1, source_target_pairs={{320,384},{321,385},{322,386},{323,387},{324,388},{325,389},{326,3... | collective-permute-start | bytes 294920 | tf_op jit(solution)/shard_map/ppermute | solution.py:24
  55.6 1.3 %collective-permute-start.20 = (bf16[8,2,1,384]{3,2,1,0:T(2,128)(2,1)S(1)}, bf16[8,2,1,384]{3,2,1,0:T(2,128)(2,1)S(1)}, u32[]{:S(2)}, u32[]{:S(2)}) collective-permute-start(bf16[8,2,1,384]{3,2,1,0:T(2,128)(2,1)S(1)} %get-tuple-element.35), channel_id=1, source_target_pairs={{321,384},{322,385},{323,386},{324,387},{325,388},{326,389},{327,3... | collective-permute-start | bytes 36872 | tf_op jit(solution)/shard_map/ppermute | solution.py:24
  56.2 0.7 collective-permute-start.21
  59.5 2.8 %collective-permute-start.25 = (bf16[8,2,8,384]{3,2,1,0:T(8,128)(2,1)S(1)}, bf16[8,2,8,384]{3,2,1,0:T(8,128)(2,1)S(1)}, u32[]{:S(2)}, u32[]{:S(2)}) collective-permute-start(bf16[8,2,8,384]{3,2,1,0:T(8,128)(2,1)S(1)} %fusion.4), channel_id=1, source_target_pairs={{384,448},{385,449},{386,450},{387,451},{388,452},{389,453},{390,4... | collective-permute-start | bytes 294920 | tf_op jit(solution)/shard_map/ppermute | solution.py:24
  60.3 2.0 %collective-permute-start.23 = (bf16[8,2,1,384]{3,2,1,0:T(2,128)(2,1)S(1)}, bf16[8,2,1,384]{3,2,1,0:T(2,128)(2,1)S(1)}, u32[]{:S(2)}, u32[]{:S(2)}) collective-permute-start(bf16[8,2,1,384]{3,2,1,0:T(2,128)(2,1)S(1)} %get-tuple-element.33), channel_id=1, source_target_pairs={{385,448},{386,449},{387,450},{388,451},{389,452},{390,453},{391,4... | collective-permute-start | bytes 36872 | tf_op jit(solution)/shard_map/ppermute | solution.py:24
  60.9 1.4 %collective-permute-start.24 = (bf16[8,2,1,384]{3,2,1,0:T(2,128)(2,1)S(1)}, bf16[8,2,1,384]{3,2,1,0:T(2,128)(2,1)S(1)}, u32[]{:S(2)}, u32[]{:S(2)}) collective-permute-start(bf16[8,2,1,384]{3,2,1,0:T(2,128)(2,1)S(1)} %get-tuple-element.34), channel_id=1, source_target_pairs={{384,449},{385,450},{386,451},{387,452},{388,453},{389,454},{390,4... | collective-permute-start | bytes 36872 | tf_op jit(solution)/shard_map/ppermute | solution.py:24
  61.6 3.3 %collective-permute-start.19 = (bf16[8,2,8,384]{3,2,1,0:T(8,128)(2,1)S(1)}, bf16[8,2,8,384]{3,2,1,0:T(8,128)(2,1)S(1)}, u32[]{:S(2)}, u32[]{:S(2)}) collective-permute-start(bf16[8,2,8,384]{3,2,1,0:T(8,128)(2,1)S(1)} %fusion.71), channel_id=1, source_target_pairs={{320,448},{321,449},{322,450},{323,451},{324,452},{325,453},{326,4... | collective-permute-start | bytes 294920 | tf_op jit(solution)/shard_map/ppermute | solution.py:24
  65.6 43.7 %all-to-all-start = ((bf16[8,2,8,384]{3,2,1,0:T(8,128)(2,1)}), bf16[8,2,8,384]{3,2,1,0:T(8,128)(2,1)S(1)}, u32[]{:S(2)}, u32[]{:S(2)}) async-start(bf16[8,2,8,384]{3,2,1,0:T(8,128)(2,1)} %fusion.72), calls=%async_computation | async-start | bytes 196608 | tf_op jit(solution)/shard_map/all_to_all | solution.py:107

commit v10 on v4

--- a/solution.py
+++ b/solution.py
@@ -81,10 +81,12 @@
             break
         first, last = edges(produced)
         left, right = diagonal(first, last, stage)
-        nxt = hop(produced, [(stage, stage + 1)], "section")
-        if stage % 2 == 1 and stage + 2 < segments:
-            residual = hop(produced, [(stage, stage + 2)], "section")
-        current = nxt
+        if stage % 2 == 0:
+            arrived = hop(jnp.stack([produced, residual]), [(stage, stage + 1)], "section")
+            current, residual = arrived[0], arrived[1]
+        else:
+            current = hop(produced, [(stage, stage + 1)], "section")
+            residual = current
     final = produced
     spread = lax.all_to_all(final, "section", 0, 0, tiled=True)
     return spread[segments - 1 : segments]

time: 106 us -> 106 us (level)
  starting transfers between devices: 27.2 us -> 25.2 us
  blocking collectives: 43.5 us -> 45.4 us
    ppermute x26 -> x23, starting transfers between devices: 27.2 us -> 25.2 us  [hop(): return lax.ppermute(block, axes, pairs)]
    all_to_all x1, blocking collectives: 43.5 us -> 45.4 us  [local(): spread = lax.all_to_all(final, 'section', 0, 0, tiled=True)]
    another operation x0 -> x5, other arithmetic: none -> 1.09 us  [local(): jnp.stack([produced, residual])]
    unnamed x69 -> x67, local copies, waits for them, and re-layouts: 5.04 us -> 4.49 us
  transfers between devices with their start and end apart: 26 -> 23, of which waited for: 2 -> 2; matrix products, arithmetic and copies ran while one was open for 10% -> 6% of each run, Pallas kernels for 0% -> 0%
where the time goes in v10:
time: 106 us; the launch traced here: 105 us
  blocking collectives  45.4 us (43%)
  starting transfers between devices  25.2 us (24%)
  matrix products  12.2 us (12%)
  local copies, waits for them, and re-layouts  8.92 us (8%)
  other arithmetic  7.76 us (7%)
  between operations  4.38 us (4%)
  waiting for transfers between devices  1.5 us (1%)
    all_to_all x1, blocking collectives, local(): spread = lax.all_to_all(final, 'section', 0, 0, tiled=True)  45.4 us
    ppermute x23, starting transfers between devices, hop(): return lax.ppermute(block, axes, pairs)  25.2 us
    dot_general x8, matrix products, convolve(): out = jnp.dot(joined, flat, preferred_element_type=jnp.float32)  12.2 us
    unnamed x67, local copies, waits for them, and re-layouts  4.49 us
  transfers between devices with their start and end apart: 23, of which 2 were waited for; matrix products, arithmetic and copies ran while one was open for 6% of the time, Pallas kernels for 0%

profile of v10, /device:TPU:256, one launch (start us, length us, event | category | flops | bytes accessed | tf_op | source)
XLA Modules:
  0.0 105.4 jit_solution(2519728737985992891)
XLA Ops:
  0.0 3.5 %collective-permute-start.1 = (bf16[8,2,8,384]{3,2,1,0:T(8,128)(2,1)}, bf16[8,2,8,384]{3,2,1,0:T(8,128)(2,1)S(1)}, u32[]{:S(2)}, u32[]{:S(2)}) collective-permute-start(bf16[8,2,8,384]{3,2,1,0:T(8,128)(2,1)} %param.4), channel_id=1, source_target_pairs={{0,1},{1,2},{2,3},{3,4},{4,5},{5,6},{6,7},{7,8},{8,9},{9,10},{10,1... | collective-permute-start | bytes 294920 | tf_op jit(solution)/shard_map/ppermute | solution.py:8
  3.5 0.9 slice.339
  4.4 5.7 %collective-permute-start = (bf16[8,2,1,384]{3,0,2,1:T(8,128)(2,1)S(1)}, bf16[8,2,1,384]{3,0,2,1:T(8,128)(2,1)S(1)}, u32[]{:S(2)}, u32[]{:S(2)}) collective-permute-start(bf16[8,2,1,384]{3,0,2,1:T(8,128)(2,1)S(1)} %copy.22), channel_id=1, source_target_pairs={{1,0},{2,1},{3,2},{4,3},{5,4},{6,5},{7,6},{8,7},{9,8},{10,9},{11,1... | collective-permute-start | bytes 36872 | tf_op jit(solution)/shard_map/ppermute | solution.py:8
  10.1 1.3 %fusion.83 = (s32[1]{0:T(128)}, s32[1]{0:T(128)}) fusion(s32[64]{0:T(128)} %param.5, s32[]{:T(128)S(6)} %max.3, s32[]{:T(128)S(6)} %select_n.70), kind=kLoop, calls=%fused_computation.258 | loop fusion | bytes 24 | tf_op jit(solution)/shard_map/dynamic_slice | solution.py:65
  12.0 1.0 broadcast_select_fusion
  13.0 1.0 fusion.100
  14.5 0.7 convert_reduce_fusion
  18.8 2.5 %copy-done = bf16[1,3,3,1152,384]{4,3,2,1,0:T(8,128)(2,1)S(1)} copy-done((bf16[1,3,3,1152,384]{4,3,2,1,0:T(8,128)(2,1)S(1)}, bf16[1,3,3,1152,384]{4,3,2,1,0:T(8,128)(2,1)}, u32[]{:S(2)}) %copy-start) | copy-done | bytes 7962648
  21.3 1.5 %fusion = bf16[8,2,8,384]{3,2,1,0:T(8,128)(2,1)S(1)} fusion(bf16[8,2,8,10368]{3,2,1,0:T(8,128)(2,1)S(1)} %slice_dynamic-update-slice_fusion.63, bf16[10368,384,1,1]{1,0,3,2:T(8,128)(2,1)S(1)} %bitcast.84, pred[8]{0:T(512)(128)(4,1)S(1)} %iota_compare_fusion.1), kind=kOutput, calls=%fused_computation.4 | convolution fusion | flops 1019314176 | bytes 10715144 | tf_op jit(solution)/shard_map/dot_general | solution.py:30
  22.9 1.3 %collective-permute-start.2 = (bf16[2,8,2,8,384]{4,3,2,1,0:T(8,128)(2,1)S(1)}, bf16[2,8,2,8,384]{4,3,2,1,0:T(8,128)(2,1)S(1)}, u32[]{:S(2)}, u32[]{:S(2)}) collective-permute-start(bf16[2,8,2,8,384]{4,3,2,1,0:T(8,128)(2,1)S(1)} %pad_maximum_fusion.8), channel_id=1, source_target_pairs={{0,64},{1,65},{2,66},{3,67},{4,68},{5,69},{6,70},{7,71},{8,72},{9,... | collective-permute-start | bytes 589832 | tf_op jit(solution)/shard_map/ppermute | solution.py:8
  24.3 1.3 %collective-permute-start.3 = (bf16[8,2,1,384]{3,2,1,0:T(2,128)(2,1)S(1)}, bf16[8,2,1,384]{3,2,1,0:T(2,128)(2,1)S(1)}, u32[]{:S(2)}, u32[]{:S(2)}) collective-permute-start(bf16[8,2,1,384]{3,2,1,0:T(2,128)(2,1)S(1)} %get-tuple-element.41), channel_id=1, source_target_pairs={{1,64},{2,65},{3,66},{4,67},{5,68},{6,69},{7,70},{8,71},{9,72},{10... | collective-permute-start | bytes 36872 | tf_op jit(solution)/shard_map/ppermute | solution.py:8
  25.6 1.3 %collective-permute-start.4 = (bf16[8,2,1,384]{3,2,1,0:T(2,128)(2,1)S(1)}, bf16[8,2,1,384]{3,2,1,0:T(2,128)(2,1)S(1)}, u32[]{:S(2)}, u32[]{:S(2)}) collective-permute-start(bf16[8,2,1,384]{3,2,1,0:T(2,128)(2,1)S(1)} %get-tuple-element.42), channel_id=1, source_target_pairs={{0,65},{1,66},{2,67},{3,68},{4,69},{5,70},{6,71},{7,72},{8,73},{9,... | collective-permute-start | bytes 36872 | tf_op jit(solution)/shard_map/ppermute | solution.py:8
  27.1 1.2 %collective-permute-done.4 = bf16[8,2,1,384]{3,2,1,0:T(2,128)(2,1)S(1)} collective-permute-done((bf16[8,2,1,384]{3,2,1,0:T(2,128)(2,1)S(1)}, bf16[8,2,1,384]{3,2,1,0:T(2,128)(2,1)S(1)}, u32[]{:S(2)}, u32[]{:S(2)}) %collective-permute-start.4) | collective-permute-done | bytes 12320 | tf_op jit(solution)/shard_map/ppermute | solution.py:8
  29.4 1.5 %fusion.72 = bf16[8,2,8,384]{3,2,1,0:T(8,128)(2,1)S(1)} fusion(bf16[2,8,2,8,384]{4,3,2,1,0:T(8,128)(2,1)S(1)} %collective-permute-done.2, pred[8]{0:T(512)(128)(4,1)S(1)} %iota_compare_fusion.1, bf16[8,2,8,10368]{3,2,1,0:T(8,128)(2,1)S(1)} %slice_dynamic-update-slice_fusion.54, bf16[10368,384,1,1]{1,0,3,2:T(8,128)(2,1)S(1)} %bitcast.85), kind=kOutput, calls=%fused_computation.212 | convolution fusion | flops 1019412480 | bytes 10813448 | tf_op jit(solution)/shard_map/dot_general | solution.py:30
  30.9 0.7 collective-permute-start.7
  31.6 0.7 collective-permute-start.5
  32.3 0.7 collective-permute-start.6
  34.1 1.5 %fusion.1 = bf16[8,2,8,384]{3,2,1,0:T(8,128)(2,1)S(1)} fusion(bf16[8,2,8,10368]{3,2,1,0:T(8,128)(2,1)S(1)} %slice_dynamic-update-slice_fusion.45, bf16[10368,384,1,1]{1,0,3,2:T(8,128)(2,1)S(1)} %bitcast.86, pred[8]{0:T(512)(128)(4,1)S(1)} %iota_compare_fusion.1), kind=kOutput, calls=%fused_computation.5 | convolution fusion | flops 1019314176 | bytes 10715144 | tf_op jit(solution)/shard_map/dot_general | solution.py:30
  35.6 0.7 collective-permute-start.8
  36.4 0.7 collective-permute-start.9
  38.8 1.5 %fusion.73 = bf16[8,2,8,384]{3,2,1,0:T(8,128)(2,1)S(1)} fusion(bf16[2,8,2,8,384]{4,3,2,1,0:T(8,128)(2,1)S(1)} %collective-permute-done.8, pred[8]{0:T(512)(128)(4,1)S(1)} %iota_compare_fusion.1, bf16[8,2,8,10368]{3,2,1,0:T(8,128)(2,1)S(1)} %slice_dynamic-update-slice_fusion.36, bf16[10368,384,1,1]{1,0,3,2:T(8,128)(2,1)S(1)} %bitcast.87), kind=kOutput, calls=%fused_computation.213 | convolution fusion | flops 1019412480 | bytes 10813448 | tf_op jit(solution)/shard_map/dot_general | solution.py:30
  40.3 0.7 collective-permute-start.13
  41.7 0.8 collective-permute-start.12
  43.7 1.5 %fusion.2 = bf16[8,2,8,384]{3,2,1,0:T(8,128)(2,1)S(1)} fusion(bf16[8,2,8,10368]{3,2,1,0:T(8,128)(2,1)S(1)} %slice_dynamic-update-slice_fusion.27, bf16[10368,384,1,1]{1,0,3,2:T(8,128)(2,1)S(1)} %bitcast.88, pred[8]{0:T(512)(128)(4,1)S(1)} %iota_compare_fusion.1), kind=kOutput, calls=%fused_computation.6 | convolution fusion | flops 1019314176 | bytes 10715144 | tf_op jit(solution)/shard_map/dot_general | solution.py:30
  45.2 0.7 collective-permute-start.14
  46.7 0.7 collective-permute-start.16
  48.4 1.5 %fusion.74 = bf16[8,2,8,384]{3,2,1,0:T(8,128)(2,1)S(1)} fusion(bf16[2,8,2,8,384]{4,3,2,1,0:T(8,128)(2,1)S(1)} %collective-permute-done.14, pred[8]{0:T(512)(128)(4,1)S(1)} %iota_compare_fusion.1, bf16[8,2,8,10368]{3,2,1,0:T(8,128)(2,1)S(1)} %slice_dynamic-update-slice_fusion.18, bf16[10368,384,1,1]{1,0,3,2:T(8,128)(2,1)S(1)} %bitcast.89), kind=kOutput, calls=%fused_computation.214 | convolution fusion | flops 1019412480 | bytes 10813448 | tf_op jit(solution)/shard_map/dot_general | solution.py:30
  50.0 0.7 collective-permute-start.19
  53.1 1.5 %fusion.3 = bf16[8,2,8,384]{3,2,1,0:T(8,128)(2,1)S(1)} fusion(bf16[8,2,8,10368]{3,2,1,0:T(8,128)(2,1)S(1)} %slice_dynamic-update-slice_fusion.9, bf16[10368,384,1,1]{1,0,3,2:T(8,128)(2,1)S(1)} %bitcast.90, pred[8]{0:T(512)(128)(4,1)S(1)} %iota_compare_fusion.1), kind=kOutput, calls=%fused_computation.7 | convolution fusion | flops 1019314176 | bytes 10715144 | tf_op jit(solution)/shard_map/dot_general | solution.py:30
  54.7 0.7 collective-permute-start.20
  57.9 1.5 %fusion.75 = bf16[8,2,8,384]{3,2,1,0:T(8,128)(2,1)S(1)} fusion(bf16[2,8,2,8,384]{4,3,2,1,0:T(8,128)(2,1)S(1)} %collective-permute-done.20, pred[8]{0:T(512)(128)(4,1)S(1)} %iota_compare_fusion.1, bf16[8,2,8,10368]{3,2,1,0:T(8,128)(2,1)S(1)} %slice_dynamic-update-slice_fusion, bf16[10368,384,1,1]{1,0,3,2:T(8,128)(2,1)S(1)} %bitcast.91), kind=kOutput, calls=%fused_computation.215 | convolution fusion | flops 1019412480 | bytes 10813448 | tf_op jit(solution)/shard_map/dot_general | solution.py:30
  59.4 45.4 %all_to_all.5 = bf16[8,2,8,384]{3,2,1,0:T(8,128)(2,1)S(1)} all-to-all(bf16[8,2,8,384]{3,2,1,0:T(8,128)(2,1)S(1)} %fusion.75), channel_id=1, replica_groups=mesh['section'=8,'tile'=64] {'section'}, dimensions={0} | all-to-all | bytes 196608 | tf_op jit(solution)/shard_map/all_to_all | solution.py:91
  (178 shorter events, 14.2 us)
Async XLA Ops:
  0.0 17.8 %collective-permute-start.1 = (bf16[8,2,8,384]{3,2,1,0:T(8,128)(2,1)}, bf16[8,2,8,384]{3,2,1,0:T(8,128)(2,1)S(1)}, u32[]{:S(2)}, u32[]{:S(2)}) collective-permute-start(bf16[8,2,8,384]{3,2,1,0:T(8,128)(2,1)} %param.4), channel_id=1, source_target_pairs={{0,1},{1,2},{2,3},{3,4},{4,5},{5,6},{6,7},{7,8},{8,9},{9,10},{10,1... | collective-permute-start | bytes 294920 | tf_op jit(solution)/shard_map/ppermute | solution.py:8
  4.4 13.3 %collective-permute-start = (bf16[8,2,1,384]{3,0,2,1:T(8,128)(2,1)S(1)}, bf16[8,2,1,384]{3,0,2,1:T(8,128)(2,1)S(1)}, u32[]{:S(2)}, u32[]{:S(2)}) collective-permute-start(bf16[8,2,1,384]{3,0,2,1:T(8,128)(2,1)S(1)} %copy.22), channel_id=1, source_target_pairs={{1,0},{2,1},{3,2},{4,3},{5,4},{6,5},{7,6},{8,7},{9,8},{10,9},{11,1... | collective-permute-start | bytes 36872 | tf_op jit(solution)/shard_map/ppermute | solution.py:8
  18.1 3.3 %copy-start = (bf16[1,3,3,1152,384]{4,3,2,1,0:T(8,128)(2,1)S(1)}, bf16[1,3,3,1152,384]{4,3,2,1,0:T(8,128)(2,1)}, u32[]{:S(2)}) copy-start(bf16[1,3,3,1152,384]{4,3,2,1,0:T(8,128)(2,1)} %param.6) | copy-start | bytes 23887876
  22.9 4.2 %collective-permute-start.2 = (bf16[2,8,2,8,384]{4,3,2,1,0:T(8,128)(2,1)S(1)}, bf16[2,8,2,8,384]{4,3,2,1,0:T(8,128)(2,1)S(1)}, u32[]{:S(2)}, u32[]{:S(2)}) collective-permute-start(bf16[2,8,2,8,384]{4,3,2,1,0:T(8,128)(2,1)S(1)} %pad_maximum_fusion.8), channel_id=1, source_target_pairs={{0,64},{1,65},{2,66},{3,67},{4,68},{5,69},{6,70},{7,71},{8,72},{9,... | collective-permute-start | bytes 589832 | tf_op jit(solution)/shard_map/ppermute | solution.py:8
  24.3 2.8 %collective-permute-start.3 = (bf16[8,2,1,384]{3,2,1,0:T(2,128)(2,1)S(1)}, bf16[8,2,1,384]{3,2,1,0:T(2,128)(2,1)S(1)}, u32[]{:S(2)}, u32[]{:S(2)}) collective-permute-start(bf16[8,2,1,384]{3,2,1,0:T(2,128)(2,1)S(1)} %get-tuple-element.41), channel_id=1, source_target_pairs={{1,64},{2,65},{3,66},{4,67},{5,68},{6,69},{7,70},{8,71},{9,72},{10... | collective-permute-start | bytes 36872 | tf_op jit(solution)/shard_map/ppermute | solution.py:8
  25.6 2.8 %collective-permute-start.4 = (bf16[8,2,1,384]{3,2,1,0:T(2,128)(2,1)S(1)}, bf16[8,2,1,384]{3,2,1,0:T(2,128)(2,1)S(1)}, u32[]{:S(2)}, u32[]{:S(2)}) collective-permute-start(bf16[8,2,1,384]{3,2,1,0:T(2,128)(2,1)S(1)} %get-tuple-element.42), channel_id=1, source_target_pairs={{0,65},{1,66},{2,67},{3,68},{4,69},{5,70},{6,71},{7,72},{8,73},{9,... | collective-permute-start | bytes 36872 | tf_op jit(solution)/shard_map/ppermute | solution.py:8
  30.9 2.1 %collective-permute-start.7 = (bf16[8,2,8,384]{3,2,1,0:T(8,128)(2,1)S(1)}, bf16[8,2,8,384]{3,2,1,0:T(8,128)(2,1)S(1)}, u32[]{:S(2)}, u32[]{:S(2)}) collective-permute-start(bf16[8,2,8,384]{3,2,1,0:T(8,128)(2,1)S(1)} %fusion.72), channel_id=1, source_target_pairs={{64,128},{65,129},{66,130},{67,131},{68,132},{69,133},{70,134},{71... | collective-permute-start | bytes 294920 | tf_op jit(solution)/shard_map/ppermute | solution.py:8
  31.6 1.3 %collective-permute-start.5 = (bf16[8,2,1,384]{3,2,1,0:T(2,128)(2,1)S(1)}, bf16[8,2,1,384]{3,2,1,0:T(2,128)(2,1)S(1)}, u32[]{:S(2)}, u32[]{:S(2)}) collective-permute-start(bf16[8,2,1,384]{3,2,1,0:T(2,128)(2,1)S(1)} %get-tuple-element.39), channel_id=1, source_target_pairs={{65,128},{66,129},{67,130},{68,131},{69,132},{70,133},{71,134},{72... | collective-permute-start | bytes 36872 | tf_op jit(solution)/shard_map/ppermute | solution.py:8
  32.3 0.7 collective-permute-start.6
  35.6 2.1 %collective-permute-start.8 = (bf16[2,8,2,8,384]{4,3,2,1,0:T(8,128)(2,1)S(1)}, bf16[2,8,2,8,384]{4,3,2,1,0:T(8,128)(2,1)S(1)}, u32[]{:S(2)}, u32[]{:S(2)}) collective-permute-start(bf16[2,8,2,8,384]{4,3,2,1,0:T(8,128)(2,1)S(1)} %pad_maximum_fusion.9), channel_id=1, source_target_pairs={{128,192},{129,193},{130,194},{131,195},{132,196},{133,197},{134,1... | collective-permute-start | bytes 589832 | tf_op jit(solution)/shard_map/ppermute | solution.py:8
  36.4 1.3 %collective-permute-start.9 = (bf16[8,2,1,384]{3,2,1,0:T(2,128)(2,1)S(1)}, bf16[8,2,1,384]{3,2,1,0:T(2,128)(2,1)S(1)}, u32[]{:S(2)}, u32[]{:S(2)}) collective-permute-start(bf16[8,2,1,384]{3,2,1,0:T(2,128)(2,1)S(1)} %get-tuple-element.37), channel_id=1, source_target_pairs={{129,192},{130,193},{131,194},{132,195},{133,196},{134,197},{135,1... | collective-permute-start | bytes 36872 | tf_op jit(solution)/shard_map/ppermute | solution.py:8
  37.0 0.7 collective-permute-start.10
  40.3 2.3 %collective-permute-start.13 = (bf16[8,2,8,384]{3,2,1,0:T(8,128)(2,1)S(1)}, bf16[8,2,8,384]{3,2,1,0:T(8,128)(2,1)S(1)}, u32[]{:S(2)}, u32[]{:S(2)}) collective-permute-start(bf16[8,2,8,384]{3,2,1,0:T(8,128)(2,1)S(1)} %fusion.73), channel_id=1, source_target_pairs={{192,256},{193,257},{194,258},{195,259},{196,260},{197,261},{198,2... | collective-permute-start | bytes 294920 | tf_op jit(solution)/shard_map/ppermute | solution.py:8
  41.1 1.5 %collective-permute-start.11 = (bf16[8,2,1,384]{3,2,1,0:T(2,128)(2,1)S(1)}, bf16[8,2,1,384]{3,2,1,0:T(2,128)(2,1)S(1)}, u32[]{:S(2)}, u32[]{:S(2)}) collective-permute-start(bf16[8,2,1,384]{3,2,1,0:T(2,128)(2,1)S(1)} %get-tuple-element.35), channel_id=1, source_target_pairs={{193,256},{194,257},{195,258},{196,259},{197,260},{198,261},{199,2... | collective-permute-start | bytes 36872 | tf_op jit(solution)/shard_map/ppermute | solution.py:8
  41.7 0.9 collective-permute-start.12
  45.2 2.1 %collective-permute-start.14 = (bf16[2,8,2,8,384]{4,3,2,1,0:T(8,128)(2,1)S(1)}, bf16[2,8,2,8,384]{4,3,2,1,0:T(8,128)(2,1)S(1)}, u32[]{:S(2)}, u32[]{:S(2)}) collective-permute-start(bf16[2,8,2,8,384]{4,3,2,1,0:T(8,128)(2,1)S(1)} %pad_maximum_fusion.10), channel_id=1, source_target_pairs={{256,320},{257,321},{258,322},{259,323},{260,324},{261,325},{262,3... | collective-permute-start | bytes 589832 | tf_op jit(solution)/shard_map/ppermute | solution.py:8
  46.0 1.3 %collective-permute-start.15 = (bf16[8,2,1,384]{3,2,1,0:T(2,128)(2,1)S(1)}, bf16[8,2,1,384]{3,2,1,0:T(2,128)(2,1)S(1)}, u32[]{:S(2)}, u32[]{:S(2)}) collective-permute-start(bf16[8,2,1,384]{3,2,1,0:T(2,128)(2,1)S(1)} %get-tuple-element.33), channel_id=1, source_target_pairs={{257,320},{258,321},{259,322},{260,323},{261,324},{262,325},{263,3... | collective-permute-start | bytes 36872 | tf_op jit(solution)/shard_map/ppermute | solution.py:8
  46.7 0.7 collective-permute-start.16
  50.0 2.1 %collective-permute-start.19 = (bf16[8,2,8,384]{3,2,1,0:T(8,128)(2,1)S(1)}, bf16[8,2,8,384]{3,2,1,0:T(8,128)(2,1)S(1)}, u32[]{:S(2)}, u32[]{:S(2)}) collective-permute-start(bf16[8,2,8,384]{3,2,1,0:T(8,128)(2,1)S(1)} %fusion.74), channel_id=1, source_target_pairs={{320,384},{321,385},{322,386},{323,387},{324,388},{325,389},{326,3... | collective-permute-start | bytes 294920 | tf_op jit(solution)/shard_map/ppermute | solution.py:8
  50.7 1.3 %collective-permute-start.17 = (bf16[8,2,1,384]{3,2,1,0:T(2,128)(2,1)S(1)}, bf16[8,2,1,384]{3,2,1,0:T(2,128)(2,1)S(1)}, u32[]{:S(2)}, u32[]{:S(2)}) collective-permute-start(bf16[8,2,1,384]{3,2,1,0:T(2,128)(2,1)S(1)} %get-tuple-element.31), channel_id=1, source_target_pairs={{321,384},{322,385},{323,386},{324,387},{325,388},{326,389},{327,3... | collective-permute-start | bytes 36872 | tf_op jit(solution)/shard_map/ppermute | solution.py:8
  51.4 0.7 collective-permute-start.18
  54.7 2.1 %collective-permute-start.20 = (bf16[2,8,2,8,384]{4,3,2,1,0:T(8,128)(2,1)S(1)}, bf16[2,8,2,8,384]{4,3,2,1,0:T(8,128)(2,1)S(1)}, u32[]{:S(2)}, u32[]{:S(2)}) collective-permute-start(bf16[2,8,2,8,384]{4,3,2,1,0:T(8,128)(2,1)S(1)} %pad_maximum_fusion.11), channel_id=1, source_target_pairs={{384,448},{385,449},{386,450},{387,451},{388,452},{389,453},{390,4... | collective-permute-start | bytes 589832 | tf_op jit(solution)/shard_map/ppermute | solution.py:8
  55.4 1.3 %collective-permute-start.21 = (bf16[8,2,1,384]{3,2,1,0:T(2,128)(2,1)S(1)}, bf16[8,2,1,384]{3,2,1,0:T(2,128)(2,1)S(1)}, u32[]{:S(2)}, u32[]{:S(2)}) collective-permute-start(bf16[8,2,1,384]{3,2,1,0:T(2,128)(2,1)S(1)} %get-tuple-element.29), channel_id=1, source_target_pairs={{385,448},{386,449},{387,450},{388,451},{389,452},{390,453},{391,4... | collective-permute-start | bytes 36872 | tf_op jit(solution)/shard_map/ppermute | solution.py:8
  56.1 0.7 collective-permute-start.22

commit v11 on v4

--- a/solution.py
+++ b/solution.py
@@ -60,12 +60,16 @@
         right = hop(first, [(src + t + 1, dst + t) for t in range(tiles - 1)], both)
         return left, right
 
+    left_count = col_counts[jnp.maximum(tile_index - 1, 0)]
+    masked = jnp.where(col_live, latents, zero)
+    latents, masked, gain, live_cols, left_count, col_live = lax.optimization_barrier(
+        (latents, masked, gain, live_cols, left_count, col_live)
+    )
     from_left = hop(latents, [(t - 1, t) for t in range(1, tiles)], "tile")
     from_right = hop(latents[:, :, 0:1], [(t + 1, t) for t in range(tiles - 1)], "tile")
-    left_count = col_counts[jnp.maximum(tile_index - 1, 0)]
     left = lax.dynamic_slice_in_dim(from_left, left_count - 1, 1, 2)
     right = from_right
-    stream = jnp.where(col_live, latents, zero)
+    stream = masked
     current = stream
     residual = stream
     for stage in range(segments):

time: 106 us -> 106 us (level)
  starting transfers between devices: 27.2 us -> 29.5 us
  blocking collectives: 43.5 us -> 41.2 us
    ppermute x26, starting transfers between devices: 27.2 us -> 29.5 us  [hop(): return lax.ppermute(block, axes, pairs)]
    all_to_all x1, blocking collectives: 43.5 us -> 41.2 us  [local(): spread = lax.all_to_all(final, 'section', 0, 0, tiled=True)]
    unnamed x69 -> x66, local copies, waits for them, and re-layouts: 5.04 us -> 4.48 us
  transfers between devices with their start and end apart: 26 -> 26, of which waited for: 2 -> 2; matrix products, arithmetic and copies ran while one was open for 10% -> 7% of each run, Pallas kernels for 0% -> 0%
where the time goes in v11:
time: 106 us; the launch traced here: 105 us
  blocking collectives  41.2 us (39%)
  starting transfers between devices  29.5 us (28%)
  matrix products  12.2 us (12%)
  local copies, waits for them, and re-layouts  8.89 us (8%)
  other arithmetic  7.55 us (7%)
  between operations  4.58 us (4%)
  waiting for transfers between devices  1.54 us (1%)
    all_to_all x1, blocking collectives, local(): spread = lax.all_to_all(final, 'section', 0, 0, tiled=True)  41.2 us
    ppermute x26, starting transfers between devices, hop(): return lax.ppermute(block, axes, pairs)  29.5 us
    dot_general x8, matrix products, convolve(): out = jnp.dot(joined, flat, preferred_element_type=jnp.float32)  12.2 us
    unnamed x66, local copies, waits for them, and re-layouts  4.48 us
  transfers between devices with their start and end apart: 26, of which 2 were waited for; matrix products, arithmetic and copies ran while one was open for 7% of the time, Pallas kernels for 0%

profile of v11, /device:TPU:256, one launch (start us, length us, event | category | flops | bytes accessed | tf_op | source)
XLA Modules:
  0.0 105.4 jit_solution(11786431462345377583)
XLA Ops:
  0.0 1.3 %fusion.80 = (s32[1]{0:T(128)}, s32[1]{0:T(128)}) fusion(s32[64]{0:T(128)} %param.5, s32[]{:T(128)S(6)} %max.3, s32[]{:T(128)S(6)} %select_n.70), kind=kLoop, calls=%fused_computation.244 | loop fusion | bytes 24 | tf_op jit(solution)/shard_map/dynamic_slice | solution.py:63
  2.6 0.7 convert_reduce_fusion
  3.3 1.0 broadcast_select_fusion
  4.3 3.5 %collective-permute-start.1 = (bf16[8,2,8,384]{3,2,1,0:T(8,128)(2,1)}, bf16[8,2,8,384]{3,2,1,0:T(8,128)(2,1)S(1)}, u32[]{:S(2)}, u32[]{:S(2)}) collective-permute-start(bf16[8,2,8,384]{3,2,1,0:T(8,128)(2,1)} %param.4), channel_id=1, source_target_pairs={{0,1},{1,2},{2,3},{3,4},{4,5},{5,6},{6,7},{7,8},{8,9},{9,10},{10,1... | collective-permute-start | bytes 294920 | tf_op jit(solution)/shard_map/ppermute | solution.py:8
  7.8 0.9 copy.5
  8.7 5.7 %collective-permute-start = (bf16[8,2,1,384]{3,0,2,1:T(8,128)(2,1)S(1)}, bf16[8,2,1,384]{3,0,2,1:T(8,128)(2,1)S(1)}, u32[]{:S(2)}, u32[]{:S(2)}) collective-permute-start(bf16[8,2,1,384]{3,0,2,1:T(8,128)(2,1)S(1)} %slice.420), channel_id=1, source_target_pairs={{1,0},{2,1},{3,2},{4,3},{5,4},{6,5},{7,6},{8,7},{9,8},{10,9},{11,1... | collective-permute-start | bytes 36872 | tf_op jit(solution)/shard_map/ppermute | solution.py:8
  18.8 2.5 %copy-done = bf16[1,3,3,1152,384]{4,3,2,1,0:T(8,128)(2,1)S(1)} copy-done((bf16[1,3,3,1152,384]{4,3,2,1,0:T(8,128)(2,1)S(1)}, bf16[1,3,3,1152,384]{4,3,2,1,0:T(8,128)(2,1)}, u32[]{:S(2)}) %copy-start) | copy-done | bytes 7962648
  21.3 1.5 %fusion = bf16[8,2,8,384]{3,2,1,0:T(8,128)(2,1)S(1)} fusion(bf16[8,2,8,10368]{3,2,1,0:T(8,128)(2,1)S(1)} %slice_dynamic-update-slice_fusion.63, bf16[10368,384,1,1]{1,0,3,2:T(8,128)(2,1)S(1)} %bitcast.47, pred[8]{0:T(512)(128)(4,1)S(1)} %bitcast.62), kind=kOutput, calls=%fused_computation.5 | convolution fusion | flops 1019314176 | bytes 10715144 | tf_op jit(solution)/shard_map/dot_general | solution.py:30
  22.8 1.3 %collective-permute-start.4 = (bf16[8,2,8,384]{3,2,1,0:T(8,128)(2,1)S(1)}, bf16[8,2,8,384]{3,2,1,0:T(8,128)(2,1)S(1)}, u32[]{:S(2)}, u32[]{:S(2)}) collective-permute-start(bf16[8,2,8,384]{3,2,1,0:T(8,128)(2,1)S(1)} %fusion), channel_id=1, source_target_pairs={{0,64},{1,65},{2,66},{3,67},{4,68},{5,69},{6,70},{7,71},{8,72},{9,... | collective-permute-start | bytes 294920 | tf_op jit(solution)/shard_map/ppermute | solution.py:8
  24.2 3.6 %collective-permute-start.2 = (bf16[8,2,1,384]{3,2,1,0:T(2,128)(2,1)S(1)}, bf16[8,2,1,384]{3,2,1,0:T(2,128)(2,1)S(1)}, u32[]{:S(2)}, u32[]{:S(2)}) collective-permute-start(bf16[8,2,1,384]{3,2,1,0:T(2,128)(2,1)S(1)} %get-tuple-element.53), channel_id=1, source_target_pairs={{1,64},{2,65},{3,66},{4,67},{5,68},{6,69},{7,70},{8,71},{9,72},{10... | collective-permute-start | bytes 36872 | tf_op jit(solution)/shard_map/ppermute | solution.py:8
  27.8 1.3 %collective-permute-start.3 = (bf16[8,2,1,384]{3,2,1,0:T(2,128)(2,1)S(1)}, bf16[8,2,1,384]{3,2,1,0:T(2,128)(2,1)S(1)}, u32[]{:S(2)}, u32[]{:S(2)}) collective-permute-start(bf16[8,2,1,384]{3,2,1,0:T(2,128)(2,1)S(1)} %get-tuple-element.54), channel_id=1, source_target_pairs={{0,65},{1,66},{2,67},{3,68},{4,69},{5,70},{6,71},{7,72},{8,73},{9,... | collective-permute-start | bytes 36872 | tf_op jit(solution)/shard_map/ppermute | solution.py:8
  29.3 1.3 %collective-permute-done.3 = bf16[8,2,1,384]{3,2,1,0:T(2,128)(2,1)S(1)} collective-permute-done((bf16[8,2,1,384]{3,2,1,0:T(2,128)(2,1)S(1)}, bf16[8,2,1,384]{3,2,1,0:T(2,128)(2,1)S(1)}, u32[]{:S(2)}, u32[]{:S(2)}) %collective-permute-start.3) | collective-permute-done | bytes 12320 | tf_op jit(solution)/shard_map/ppermute | solution.py:8
  31.6 1.5 %fusion.5 = bf16[8,2,8,384]{3,2,1,0:T(8,128)(2,1)S(1)} fusion(bf16[8,2,8,10368]{3,2,1,0:T(8,128)(2,1)S(1)} %slice_dynamic-update-slice_fusion.54, bf16[10368,384,1,1]{1,0,3,2:T(8,128)(2,1)S(1)} %bitcast.48, bf16[8,2,8,384]{3,2,1,0:T(8,128)(2,1)S(1)} %broadcast_select_fusion, pred[8]{0:T(512)(128)(4,1)S(1)} %bitcast.63), kind=kOutput, calls=%fused_computation.10 | convolution fusion | flops 1019412480 | bytes 10813448 | tf_op jit(solution)/shard_map/dot_general | solution.py:30
  33.2 0.7 collective-permute-start.8
  34.6 0.7 collective-permute-start.7
  36.3 1.5 %fusion.2 = bf16[8,2,8,384]{3,2,1,0:T(8,128)(2,1)S(1)} fusion(bf16[8,2,8,10368]{3,2,1,0:T(8,128)(2,1)S(1)} %slice_dynamic-update-slice_fusion.45, bf16[10368,384,1,1]{1,0,3,2:T(8,128)(2,1)S(1)} %bitcast.49, pred[8]{0:T(512)(128)(4,1)S(1)} %bitcast.64), kind=kOutput, calls=%fused_computation.7 | convolution fusion | flops 1019314176 | bytes 10715144 | tf_op jit(solution)/shard_map/dot_general | solution.py:30
  37.9 0.7 collective-permute-start.11
  38.6 0.7 collective-permute-start.9
  39.9 0.7 collective-permute-start.5
  41.7 1.5 %fusion.70 = bf16[8,2,8,384]{3,2,1,0:T(8,128)(2,1)S(1)} fusion(bf16[8,2,8,384]{3,2,1,0:T(8,128)(2,1)S(1)} %collective-permute-done.5, pred[8]{0:T(512)(128)(4,1)S(1)} %bitcast.65, bf16[8,2,8,10368]{3,2,1,0:T(8,128)(2,1)S(1)} %slice_dynamic-update-slice_fusion.36, bf16[10368,384,1,1]{1,0,3,2:T(8,128)(2,1)S(1)} %bitcast.50), kind=kOutput, calls=%fused_computation.206 | convolution fusion | flops 1019412480 | bytes 10813448 | tf_op jit(solution)/shard_map/dot_general | solution.py:30
  43.2 0.7 collective-permute-start.15
  44.6 0.8 collective-permute-start.14
  46.6 1.5 %fusion.3 = bf16[8,2,8,384]{3,2,1,0:T(8,128)(2,1)S(1)} fusion(bf16[8,2,8,10368]{3,2,1,0:T(8,128)(2,1)S(1)} %slice_dynamic-update-slice_fusion.27, bf16[10368,384,1,1]{1,0,3,2:T(8,128)(2,1)S(1)} %bitcast.51, pred[8]{0:T(512)(128)(4,1)S(1)} %bitcast.66), kind=kOutput, calls=%fused_computation.8 | convolution fusion | flops 1019314176 | bytes 10715144 | tf_op jit(solution)/shard_map/dot_general | solution.py:30
  48.1 0.7 collective-permute-start.18
  50.2 0.7 collective-permute-start.12
  51.9 1.5 %fusion.81 = f32[8,2,8,384]{3,2,1,0:T(8,128)S(1)} fusion(bf16[8,2,8,10368]{3,2,1,0:T(8,128)(2,1)S(1)} %slice_dynamic-update-slice_fusion.18, bf16[10368,384,1,1]{1,0,3,2:T(8,128)(2,1)S(1)} %bitcast.52), kind=kOutput, calls=%fused_computation.245 | convolution fusion | flops 1019215872 | bytes 10813440 | tf_op jit(solution)/shard_map/dot_general | solution.py:30
  53.5 0.7 collective-permute-start.22
  56.7 1.5 %fusion.4 = bf16[8,2,8,384]{3,2,1,0:T(8,128)(2,1)S(1)} fusion(bf16[8,2,8,10368]{3,2,1,0:T(8,128)(2,1)S(1)} %slice_dynamic-update-slice_fusion.9, bf16[10368,384,1,1]{1,0,3,2:T(8,128)(2,1)S(1)} %bitcast.53, pred[8]{0:T(512)(128)(4,1)S(1)} %bitcast.68), kind=kOutput, calls=%fused_computation.9 | convolution fusion | flops 1019314176 | bytes 10715144 | tf_op jit(solution)/shard_map/dot_general | solution.py:30
  58.2 0.7 collective-permute-start.25
  60.3 0.7 collective-permute-start.19
  62.1 1.5 %fusion.82 = f32[8,2,8,384]{3,2,1,0:T(8,128)S(1)} fusion(bf16[8,2,8,10368]{3,2,1,0:T(8,128)(2,1)S(1)} %slice_dynamic-update-slice_fusion, bf16[10368,384,1,1]{1,0,3,2:T(8,128)(2,1)S(1)} %bitcast.54), kind=kOutput, calls=%fused_computation.246 | convolution fusion | flops 1019215872 | bytes 10813440 | tf_op jit(solution)/shard_map/dot_general | solution.py:30
  63.7 41.2 %all_to_all.5 = bf16[8,2,8,384]{3,2,1,0:T(8,128)(2,1)S(1)} all-to-all(bf16[8,2,8,384]{3,2,1,0:T(8,128)(2,1)S(1)} %fusion.72), channel_id=1, replica_groups=mesh['section'=8,'tile'=64] {'section'}, dimensions={0} | all-to-all | bytes 196608 | tf_op jit(solution)/shard_map/all_to_all | solution.py:93
  (178 shorter events, 16.2 us)
Async XLA Ops:
  4.3 13.4 %collective-permute-start.1 = (bf16[8,2,8,384]{3,2,1,0:T(8,128)(2,1)}, bf16[8,2,8,384]{3,2,1,0:T(8,128)(2,1)S(1)}, u32[]{:S(2)}, u32[]{:S(2)}) collective-permute-start(bf16[8,2,8,384]{3,2,1,0:T(8,128)(2,1)} %param.4), channel_id=1, source_target_pairs={{0,1},{1,2},{2,3},{3,4},{4,5},{5,6},{6,7},{7,8},{8,9},{9,10},{10,1... | collective-permute-start | bytes 294920 | tf_op jit(solution)/shard_map/ppermute | solution.py:8
  8.7 9.0 %collective-permute-start = (bf16[8,2,1,384]{3,0,2,1:T(8,128)(2,1)S(1)}, bf16[8,2,1,384]{3,0,2,1:T(8,128)(2,1)S(1)}, u32[]{:S(2)}, u32[]{:S(2)}) collective-permute-start(bf16[8,2,1,384]{3,0,2,1:T(8,128)(2,1)S(1)} %slice.420), channel_id=1, source_target_pairs={{1,0},{2,1},{3,2},{4,3},{5,4},{6,5},{7,6},{8,7},{9,8},{10,9},{11,1... | collective-permute-start | bytes 36872 | tf_op jit(solution)/shard_map/ppermute | solution.py:8
  18.0 3.3 %copy-start = (bf16[1,3,3,1152,384]{4,3,2,1,0:T(8,128)(2,1)S(1)}, bf16[1,3,3,1152,384]{4,3,2,1,0:T(8,128)(2,1)}, u32[]{:S(2)}) copy-start(bf16[1,3,3,1152,384]{4,3,2,1,0:T(8,128)(2,1)} %param.6) | copy-start | bytes 23887876
  22.8 7.8 %collective-permute-start.4 = (bf16[8,2,8,384]{3,2,1,0:T(8,128)(2,1)S(1)}, bf16[8,2,8,384]{3,2,1,0:T(8,128)(2,1)S(1)}, u32[]{:S(2)}, u32[]{:S(2)}) collective-permute-start(bf16[8,2,8,384]{3,2,1,0:T(8,128)(2,1)S(1)} %fusion), channel_id=1, source_target_pairs={{0,64},{1,65},{2,66},{3,67},{4,68},{5,69},{6,70},{7,71},{8,72},{9,... | collective-permute-start | bytes 294920 | tf_op jit(solution)/shard_map/ppermute | solution.py:8
  24.2 5.1 %collective-permute-start.2 = (bf16[8,2,1,384]{3,2,1,0:T(2,128)(2,1)S(1)}, bf16[8,2,1,384]{3,2,1,0:T(2,128)(2,1)S(1)}, u32[]{:S(2)}, u32[]{:S(2)}) collective-permute-start(bf16[8,2,1,384]{3,2,1,0:T(2,128)(2,1)S(1)} %get-tuple-element.53), channel_id=1, source_target_pairs={{1,64},{2,65},{3,66},{4,67},{5,68},{6,69},{7,70},{8,71},{9,72},{10... | collective-permute-start | bytes 36872 | tf_op jit(solution)/shard_map/ppermute | solution.py:8
  27.8 2.8 %collective-permute-start.3 = (bf16[8,2,1,384]{3,2,1,0:T(2,128)(2,1)S(1)}, bf16[8,2,1,384]{3,2,1,0:T(2,128)(2,1)S(1)}, u32[]{:S(2)}, u32[]{:S(2)}) collective-permute-start(bf16[8,2,1,384]{3,2,1,0:T(2,128)(2,1)S(1)} %get-tuple-element.54), channel_id=1, source_target_pairs={{0,65},{1,66},{2,67},{3,68},{4,69},{5,70},{6,71},{7,72},{8,73},{9,... | collective-permute-start | bytes 36872 | tf_op jit(solution)/shard_map/ppermute | solution.py:8
  33.2 2.1 %collective-permute-start.8 = (bf16[8,2,8,384]{3,2,1,0:T(8,128)(2,1)S(1)}, bf16[8,2,8,384]{3,2,1,0:T(8,128)(2,1)S(1)}, u32[]{:S(2)}, u32[]{:S(2)}) collective-permute-start(bf16[8,2,8,384]{3,2,1,0:T(8,128)(2,1)S(1)} %fusion.5), channel_id=1, source_target_pairs={{64,128},{65,129},{66,130},{67,131},{68,132},{69,133},{70,134},{71... | collective-permute-start | bytes 294920 | tf_op jit(solution)/shard_map/ppermute | solution.py:8
  33.9 1.3 %collective-permute-start.6 = (bf16[8,2,1,384]{3,2,1,0:T(2,128)(2,1)S(1)}, bf16[8,2,1,384]{3,2,1,0:T(2,128)(2,1)S(1)}, u32[]{:S(2)}, u32[]{:S(2)}) collective-permute-start(bf16[8,2,1,384]{3,2,1,0:T(2,128)(2,1)S(1)} %get-tuple-element.51), channel_id=1, source_target_pairs={{65,128},{66,129},{67,130},{68,131},{69,132},{70,133},{71,134},{72... | collective-permute-start | bytes 36872 | tf_op jit(solution)/shard_map/ppermute | solution.py:8
  34.6 0.7 collective-permute-start.7
  37.9 2.8 %collective-permute-start.11 = (bf16[8,2,8,384]{3,2,1,0:T(8,128)(2,1)S(1)}, bf16[8,2,8,384]{3,2,1,0:T(8,128)(2,1)S(1)}, u32[]{:S(2)}, u32[]{:S(2)}) collective-permute-start(bf16[8,2,8,384]{3,2,1,0:T(8,128)(2,1)S(1)} %fusion.2), channel_id=1, source_target_pairs={{128,192},{129,193},{130,194},{131,195},{132,196},{133,197},{134,1... | collective-permute-start | bytes 294920 | tf_op jit(solution)/shard_map/ppermute | solution.py:8
  38.6 2.0 %collective-permute-start.9 = (bf16[8,2,1,384]{3,2,1,0:T(2,128)(2,1)S(1)}, bf16[8,2,1,384]{3,2,1,0:T(2,128)(2,1)S(1)}, u32[]{:S(2)}, u32[]{:S(2)}) collective-permute-start(bf16[8,2,1,384]{3,2,1,0:T(2,128)(2,1)S(1)} %get-tuple-element.49), channel_id=1, source_target_pairs={{129,192},{130,193},{131,194},{132,195},{133,196},{134,197},{135,1... | collective-permute-start | bytes 36872 | tf_op jit(solution)/shard_map/ppermute | solution.py:8
  39.3 1.4 %collective-permute-start.10 = (bf16[8,2,1,384]{3,2,1,0:T(2,128)(2,1)S(1)}, bf16[8,2,1,384]{3,2,1,0:T(2,128)(2,1)S(1)}, u32[]{:S(2)}, u32[]{:S(2)}) collective-permute-start(bf16[8,2,1,384]{3,2,1,0:T(2,128)(2,1)S(1)} %get-tuple-element.50), channel_id=1, source_target_pairs={{128,193},{129,194},{130,195},{131,196},{132,197},{133,198},{134,1... | collective-permute-start | bytes 36872 | tf_op jit(solution)/shard_map/ppermute | solution.py:8
  39.9 1.8 %collective-permute-start.5 = (bf16[8,2,8,384]{3,2,1,0:T(8,128)(2,1)S(1)}, bf16[8,2,8,384]{3,2,1,0:T(8,128)(2,1)S(1)}, u32[]{:S(2)}, u32[]{:S(2)}) collective-permute-start(bf16[8,2,8,384]{3,2,1,0:T(8,128)(2,1)S(1)} %fusion.5), channel_id=1, source_target_pairs={{64,192},{65,193},{66,194},{67,195},{68,196},{69,197},{70,198},{71... | collective-permute-start | bytes 294920 | tf_op jit(solution)/shard_map/ppermute | solution.py:8
  43.2 2.3 %collective-permute-start.15 = (bf16[8,2,8,384]{3,2,1,0:T(8,128)(2,1)S(1)}, bf16[8,2,8,384]{3,2,1,0:T(8,128)(2,1)S(1)}, u32[]{:S(2)}, u32[]{:S(2)}) collective-permute-start(bf16[8,2,8,384]{3,2,1,0:T(8,128)(2,1)S(1)} %fusion.70), channel_id=1, source_target_pairs={{192,256},{193,257},{194,258},{195,259},{196,260},{197,261},{198,2... | collective-permute-start | bytes 294920 | tf_op jit(solution)/shard_map/ppermute | solution.py:8
  44.0 1.5 %collective-permute-start.13 = (bf16[8,2,1,384]{3,2,1,0:T(2,128)(2,1)S(1)}, bf16[8,2,1,384]{3,2,1,0:T(2,128)(2,1)S(1)}, u32[]{:S(2)}, u32[]{:S(2)}) collective-permute-start(bf16[8,2,1,384]{3,2,1,0:T(2,128)(2,1)S(1)} %get-tuple-element.47), channel_id=1, source_target_pairs={{193,256},{194,257},{195,258},{196,259},{197,260},{198,261},{199,2... | collective-permute-start | bytes 36872 | tf_op jit(solution)/shard_map/ppermute | solution.py:8
  44.6 0.9 collective-permute-start.14
  48.1 2.8 %collective-permute-start.18 = (bf16[8,2,8,384]{3,2,1,0:T(8,128)(2,1)S(1)}, bf16[8,2,8,384]{3,2,1,0:T(8,128)(2,1)S(1)}, u32[]{:S(2)}, u32[]{:S(2)}) collective-permute-start(bf16[8,2,8,384]{3,2,1,0:T(8,128)(2,1)S(1)} %fusion.3), channel_id=1, source_target_pairs={{256,320},{257,321},{258,322},{259,323},{260,324},{261,325},{262,3... | collective-permute-start | bytes 294920 | tf_op jit(solution)/shard_map/ppermute | solution.py:8
  48.8 2.0 %collective-permute-start.16 = (bf16[8,2,1,384]{3,2,1,0:T(2,128)(2,1)S(1)}, bf16[8,2,1,384]{3,2,1,0:T(2,128)(2,1)S(1)}, u32[]{:S(2)}, u32[]{:S(2)}) collective-permute-start(bf16[8,2,1,384]{3,2,1,0:T(2,128)(2,1)S(1)} %get-tuple-element.45), channel_id=1, source_target_pairs={{257,320},{258,321},{259,322},{260,323},{261,324},{262,325},{263,3... | collective-permute-start | bytes 36872 | tf_op jit(solution)/shard_map/ppermute | solution.py:8
  49.5 1.4 %collective-permute-start.17 = (bf16[8,2,1,384]{3,2,1,0:T(2,128)(2,1)S(1)}, bf16[8,2,1,384]{3,2,1,0:T(2,128)(2,1)S(1)}, u32[]{:S(2)}, u32[]{:S(2)}) collective-permute-start(bf16[8,2,1,384]{3,2,1,0:T(2,128)(2,1)S(1)} %get-tuple-element.46), channel_id=1, source_target_pairs={{256,321},{257,322},{258,323},{259,324},{260,325},{261,326},{262,3... | collective-permute-start | bytes 36872 | tf_op jit(solution)/shard_map/ppermute | solution.py:8
  50.2 3.3 %collective-permute-start.12 = (bf16[8,2,8,384]{3,2,1,0:T(8,128)(2,1)S(1)}, bf16[8,2,8,384]{3,2,1,0:T(8,128)(2,1)S(1)}, u32[]{:S(2)}, u32[]{:S(2)}) collective-permute-start(bf16[8,2,8,384]{3,2,1,0:T(8,128)(2,1)S(1)} %fusion.70), channel_id=1, source_target_pairs={{192,320},{193,321},{194,322},{195,323},{196,324},{197,325},{198,3... | collective-permute-start | bytes 294920 | tf_op jit(solution)/shard_map/ppermute | solution.py:8
  53.5 2.1 %collective-permute-start.22 = (bf16[8,2,8,384]{3,2,1,0:T(8,128)(2,1)S(1)}, bf16[8,2,8,384]{3,2,1,0:T(8,128)(2,1)S(1)}, u32[]{:S(2)}, u32[]{:S(2)}) collective-permute-start(bf16[8,2,8,384]{3,2,1,0:T(8,128)(2,1)S(1)} %fusion.71), channel_id=1, source_target_pairs={{320,384},{321,385},{322,386},{323,387},{324,388},{325,389},{326,3... | collective-permute-start | bytes 294920 | tf_op jit(solution)/shard_map/ppermute | solution.py:8
  54.3 1.3 %collective-permute-start.20 = (bf16[8,2,1,384]{3,2,1,0:T(2,128)(2,1)S(1)}, bf16[8,2,1,384]{3,2,1,0:T(2,128)(2,1)S(1)}, u32[]{:S(2)}, u32[]{:S(2)}) collective-permute-start(bf16[8,2,1,384]{3,2,1,0:T(2,128)(2,1)S(1)} %get-tuple-element.43), channel_id=1, source_target_pairs={{321,384},{322,385},{323,386},{324,387},{325,388},{326,389},{327,3... | collective-permute-start | bytes 36872 | tf_op jit(solution)/shard_map/ppermute | solution.py:8
  54.9 0.7 collective-permute-start.21
  58.2 2.8 %collective-permute-start.25 = (bf16[8,2,8,384]{3,2,1,0:T(8,128)(2,1)S(1)}, bf16[8,2,8,384]{3,2,1,0:T(8,128)(2,1)S(1)}, u32[]{:S(2)}, u32[]{:S(2)}) collective-permute-start(bf16[8,2,8,384]{3,2,1,0:T(8,128)(2,1)S(1)} %fusion.4), channel_id=1, source_target_pairs={{384,448},{385,449},{386,450},{387,451},{388,452},{389,453},{390,4... | collective-permute-start | bytes 294920 | tf_op jit(solution)/shard_map/ppermute | solution.py:8
  59.0 2.0 %collective-permute-start.23 = (bf16[8,2,1,384]{3,2,1,0:T(2,128)(2,1)S(1)}, bf16[8,2,1,384]{3,2,1,0:T(2,128)(2,1)S(1)}, u32[]{:S(2)}, u32[]{:S(2)}) collective-permute-start(bf16[8,2,1,384]{3,2,1,0:T(2,128)(2,1)S(1)} %get-tuple-element.41), channel_id=1, source_target_pairs={{385,448},{386,449},{387,450},{388,451},{389,452},{390,453},{391,4... | collective-permute-start | bytes 36872 | tf_op jit(solution)/shard_map/ppermute | solution.py:8
  59.6 1.4 %collective-permute-start.24 = (bf16[8,2,1,384]{3,2,1,0:T(2,128)(2,1)S(1)}, bf16[8,2,1,384]{3,2,1,0:T(2,128)(2,1)S(1)}, u32[]{:S(2)}, u32[]{:S(2)}) collective-permute-start(bf16[8,2,1,384]{3,2,1,0:T(2,128)(2,1)S(1)} %get-tuple-element.42), channel_id=1, source_target_pairs={{384,449},{385,450},{386,451},{387,452},{388,453},{389,454},{390,4... | collective-permute-start | bytes 36872 | tf_op jit(solution)/shard_map/ppermute | solution.py:8
  60.3 3.3 %collective-permute-start.19 = (bf16[8,2,8,384]{3,2,1,0:T(8,128)(2,1)S(1)}, bf16[8,2,8,384]{3,2,1,0:T(8,128)(2,1)S(1)}, u32[]{:S(2)}, u32[]{:S(2)}) collective-permute-start(bf16[8,2,8,384]{3,2,1,0:T(8,128)(2,1)S(1)} %fusion.71), channel_id=1, source_target_pairs={{320,448},{321,449},{322,450},{323,451},{324,452},{325,453},{326,4... | collective-permute-start | bytes 294920 | tf_op jit(solution)/shard_map/ppermute | solution.py:8
